TPU v7x, 512 devices: a whole 4x8x8 slice. The times are simulated.
512 devices in a mesh: segment: 16 (over y, z_lo), ctx: 32 (over x, z_hi, core).
Axes of the slice: x: 4, y: 8, z: 8 (z_hi: 4, z_lo: 2; z = z_hi * 2 + z_lo), core: 2. Of those that a mesh axis runs over, the one named last changes fastest.
Arguments:
- perturbed_frame_activation: bfloat16 [2, 256, 1536], P(None, 'ctx'), may hold values from -8 to 8
- inbound_activation: bfloat16 [16, 256, 1536], P('segment', 'ctx'), may hold values from -6 to 6
- section_block_indices: int32 [16], P('segment'), may hold values from 1 to 2, as said below
- tile_arrival_permutation: int32 [2], replicated, may hold values from 0 to 1, each once
- adaptive_shifting: float32 [16, 2, 1536], P('segment'), may hold values from -6 to 6
- adaptive_scaling: float32 [16, 2, 1536], P('segment'), may hold values from -4 to 4
- tier_query_factor: float32 [16, 2, 1536], P('segment'), may hold values from 0.3 to 3
- tier_skip_coefficient: float32 [16, 2, 1536], P('segment'), may hold values from -12 to 12
- earlier_step_lookup_matrix: bfloat16 [16, 2, 2, 256, 1536], P('segment', None, None, 'ctx'), may hold values from -10.5 to 10.5
- earlier_step_content_matrix: bfloat16 [16, 2, 2, 256, 1536], P('segment', None, None, 'ctx'), may hold values from -3 to 3
Outputs:
- section_out: bfloat16 [16, 2, 256, 1536], P('segment', None, 'ctx')
Inputs may be any that keep to these rules, and one draw needn't show every extreme that they name: `section_block_indices`: some segment uses exactly 2 slots and some exactly 1. `tile_arrival_permutation`: each patch once.
All inputs are finite; a program needn't handle non-finite values.
Results may differ from a plain program's by a relative error of at most 0.013.
Values may be sent and summed in bfloat16 or wider, within the bound.
No kernel may reach another device: no remote copies, remote signals or barrier semaphores. Data moves between devices by JAX's collectives and lax.ppermute only.
A program may use at most 64 MiB of HBM per device.

v0:
```python
import math

import jax
import jax.numpy as jnp
from jax import lax
from jax.sharding import PartitionSpec as P

HD = 128


EPSILON = 1e-06


def from_behind(value, axis, steps):
    count = lax.axis_size(axis)
    initial, last = (max(0, -steps), min(count, count - steps))
    return lax.ppermute(value, axis, [(source, source + steps) for source in range(initial, last)])


def head_norm(values):
    return values * lax.rsqrt(jnp.mean(values * values, axis=-1, keepdims=True) + EPSILON)


def attend_block(query_heads, key_rows, value_rows, head_count):
    key_count = key_rows.shape[0]
    key_heads = key_rows.reshape(key_count, head_count, HD)
    value_heads = value_rows.reshape(key_count, head_count, HD)
    scores = jnp.einsum(
        "phd,nhd->phn", query_heads, key_heads, preferred_element_type=jnp.float32
    ) * (1.0 / math.sqrt(HD))
    weights = jnp.exp(scores)
    softmax_total = jnp.sum(weights, axis=-1)
    numerator = jnp.einsum(
        "phn,nhd->phd",
        weights.astype(jnp.bfloat16),
        value_heads,
        preferred_element_type=jnp.float32,
    )
    return (numerator, softmax_total)


def per_device(
    perturbed_frame_activation,
    inbound_activation,
    section_block_indices,
    tile_arrival_permutation,
    adaptive_shifting,
    adaptive_scaling,
    tier_query_factor,
    tier_skip_coefficient,
    earlier_step_lookup_matrix,
    earlier_step_content_matrix,
):
    partition_number = lax.axis_index("segment")
    patch_count = tile_arrival_permutation.shape[0]
    piece_element_count = inbound_activation.shape[1]
    embedding_width = inbound_activation.shape[2]
    head_count = embedding_width // HD
    slot_count = earlier_step_lookup_matrix.shape[1]
    cached_probe_vectors = earlier_step_lookup_matrix[0]
    cached_payload_vectors = earlier_step_content_matrix[0]
    layers_here = section_block_indices[0]
    inbound_activation_grid = inbound_activation[0]
    zero_index = jnp.zeros((), jnp.int32)
    gathered_outcomes = []
    for round_counter in range(patch_count):
        tile_number = tile_arrival_permutation[
            jnp.mod(round_counter - partition_number, patch_count)
        ]
        passing_vessel = jnp.where(
            partition_number == 0,
            perturbed_frame_activation[tile_arrival_permutation[round_counter]],
            inbound_activation_grid,
        )
        for tier_number in range(slot_count):
            live_flag = layers_here > tier_number
            activation_single_precision = passing_vessel.astype(jnp.float32)
            hidden = (
                activation_single_precision
                * lax.rsqrt(
                    jnp.mean(
                        activation_single_precision * activation_single_precision,
                        axis=-1,
                        keepdims=True,
                    )
                    + EPSILON
                )
                * (1.0 + adaptive_scaling[0, tier_number])
                + adaptive_shifting[0, tier_number]
            )
            query_heads = head_norm(hidden.reshape(piece_element_count, head_count, HD)).astype(
                jnp.bfloat16
            )
            fresh_key = (
                head_norm(
                    (hidden * tier_query_factor[0, tier_number]).reshape(
                        piece_element_count, head_count, HD
                    )
                )
                .reshape(piece_element_count, embedding_width)
                .astype(jnp.bfloat16)
            )
            fresh_value = hidden.astype(jnp.bfloat16)
            position = (tile_number, zero_index, zero_index)
            layer_keys = jnp.where(
                live_flag,
                lax.dynamic_update_slice(
                    cached_probe_vectors[tier_number], fresh_key[None], position
                ),
                cached_probe_vectors[tier_number],
            )
            layer_values = jnp.where(
                live_flag,
                lax.dynamic_update_slice(
                    cached_payload_vectors[tier_number], fresh_value[None], position
                ),
                cached_payload_vectors[tier_number],
            )
            cached_probe_vectors = cached_probe_vectors.at[tier_number].set(layer_keys)
            cached_payload_vectors = cached_payload_vectors.at[tier_number].set(layer_values)
            flat_keys = layer_keys.reshape(patch_count * piece_element_count, embedding_width)
            flat_values = layer_values.reshape(patch_count * piece_element_count, embedding_width)
            numerator, softmax_total = attend_block(
                query_heads,
                lax.all_gather(flat_keys, "ctx", axis=0, tiled=True),
                lax.all_gather(flat_values, "ctx", axis=0, tiled=True),
                head_count,
            )
            numerator, softmax_total = (numerator, softmax_total)
            attended = (numerator / softmax_total[..., None]).reshape(
                piece_element_count, embedding_width
            )
            passing_vessel = jnp.where(
                live_flag,
                (
                    activation_single_precision + tier_skip_coefficient[0, tier_number] * attended
                ).astype(jnp.bfloat16),
                passing_vessel,
            )
        gathered_outcomes.append(passing_vessel)
        if round_counter + 1 < patch_count:
            inbound_activation_grid = from_behind(passing_vessel, "segment", 1)
    return jnp.stack(gathered_outcomes)[None]


def solution(mesh):
    return jax.shard_map(
        per_device,
        mesh=mesh,
        in_specs=(
            P(None, "ctx", None),
            P("segment", "ctx", None),
            P("segment"),
            P(),
            P("segment", None, None),
            P("segment", None, None),
            P("segment", None, None),
            P("segment", None, None),
            P("segment", None, None, "ctx", None),
            P("segment", None, None, "ctx", None),
        ),
        out_specs=P("segment", None, "ctx", None),
        check_vma=False,
    )
```

profile of v0, /device:TPU:1, one launch (start us, length us, event | category | flops | bytes accessed | tf_op | source)
XLA Modules:
  0.0 519.2 jit_solution(11718202191412952001)
XLA Ops:
  6.5 1.5 fusion.124
  11.4 0.9 fusion.34
  12.3 0.8 add_reduce_fusion
  13.9 0.8 slice_reduce_fusion
  15.6 0.8 fusion.122
  16.4 0.8 fusion.123
  19.5 0.8 slice_reduce_fusion.2
  20.3 63.6 %all-gather.11.cloned.1.call-done = bf16[512,1536]{1,0:T(8,128)(2,1)} async-done(((bf16[16,1536]{1,0:T(8,128)(2,1)}), bf16[512,1536]{1,0:T(8,128)(2,1)}) %all-gather.11.cloned.1.call-update) | async-done | bytes 1572880 | tf_op jit(solution)/shard_map/all_gather | solution.py:125
  84.0 1.7 copy.28
  86.1 57.4 %all-gather.9.cloned.1.call-done = bf16[512,1536]{1,0:T(8,128)(2,1)} async-done(((bf16[16,1536]{1,0:T(8,128)(2,1)}), bf16[512,1536]{1,0:T(8,128)(2,1)}) %all-gather.9.cloned.1.call-update) | async-done | bytes 1572880 | tf_op jit(solution)/shard_map/all_gather | solution.py:126
  143.5 1.7 copy.27
  149.4 54.0 %all-gather.15.cloned.1.call-done = bf16[512,1536]{1,0:T(8,128)(2,1)} async-done(((bf16[16,1536]{1,0:T(8,128)(2,1)}), bf16[512,1536]{1,0:T(8,128)(2,1)}) %all-gather.15.cloned.1.call-update) | async-done | bytes 1572880 | tf_op jit(solution)/shard_map/all_gather | solution.py:125
  203.4 1.7 copy.32
  205.6 57.3 %all-gather.13.cloned.1.call-done = bf16[512,1536]{1,0:T(8,128)(2,1)} async-done(((bf16[16,1536]{1,0:T(8,128)(2,1)}), bf16[512,1536]{1,0:T(8,128)(2,1)}) %all-gather.13.cloned.1.call-update) | async-done | bytes 1572880 | tf_op jit(solution)/shard_map/all_gather | solution.py:126
  262.9 1.7 copy.31
  265.2 1.8 collective-permute-start
  270.5 60.1 %all-gather.19.cloned.1.call-done = bf16[512,1536]{1,0:T(8,128)(2,1)} async-done(((bf16[16,1536]{1,0:T(8,128)(2,1)}), bf16[512,1536]{1,0:T(8,128)(2,1)}) %all-gather.19.cloned.1.call-update) | async-done | bytes 1572880 | tf_op jit(solution)/shard_map/all_gather | solution.py:125
  330.6 1.7 copy.36
  332.8 57.3 %all-gather.17.cloned.1.call-done = bf16[512,1536]{1,0:T(8,128)(2,1)} async-done(((bf16[16,1536]{1,0:T(8,128)(2,1)}), bf16[512,1536]{1,0:T(8,128)(2,1)}) %all-gather.17.cloned.1.call-update) | async-done | bytes 1572880 | tf_op jit(solution)/shard_map/all_gather | solution.py:126
  390.1 1.7 copy.35
  394.2 55.8 %all-gather.23.cloned.1.call-done = bf16[512,1536]{1,0:T(8,128)(2,1)} async-done(((bf16[16,1536]{1,0:T(8,128)(2,1)}), bf16[512,1536]{1,0:T(8,128)(2,1)}) %all-gather.23.cloned.1.call-update) | async-done | bytes 1572880 | tf_op jit(solution)/shard_map/all_gather | solution.py:125
  449.9 1.7 copy.40
  452.1 57.4 %all-gather.21.cloned.1.call-done = bf16[512,1536]{1,0:T(8,128)(2,1)} async-done(((bf16[16,1536]{1,0:T(8,128)(2,1)}), bf16[512,1536]{1,0:T(8,128)(2,1)}) %all-gather.21.cloned.1.call-update) | async-done | bytes 1572880 | tf_op jit(solution)/shard_map/all_gather | solution.py:126
  509.5 1.7 copy.39
  (77 shorter events, 12.1 us)
Async XLA Ops:
  6.5 77.4 %all-gather.11.cloned.1.call-start = ((), (), s32[]{:S(2)}) async-start(), calls=%async_computation.1 | async-start | bytes 1622016 | tf_op jit(solution)/shard_map/all_gather | solution.py:125
  18.0 0.6 copy-start.6
  18.0 0.7 copy-start.9
  18.7 124.9 %all-gather.9.cloned.1.call-start = ((), (), s32[]{:S(2)}) async-start(), calls=%async_computation | async-start | bytes 1622016 | tf_op jit(solution)/shard_map/all_gather | solution.py:126
  19.4 184.0 %all-gather.15.cloned.1.call-start = ((), (), s32[]{:S(2)}) async-start(), calls=%async_computation.3 | async-start | bytes 1622016 | tf_op jit(solution)/shard_map/all_gather | solution.py:125
  146.2 0.6 copy-start
  146.2 0.7 copy-start.3
  146.9 116.0 %all-gather.13.cloned.1.call-start = ((), (), s32[]{:S(2)}) async-start(), calls=%async_computation.2 | async-start | bytes 1622016 | tf_op jit(solution)/shard_map/all_gather | solution.py:126
  147.4 183.2 %all-gather.19.cloned.1.call-start = ((), (), s32[]{:S(2)}) async-start(), calls=%async_computation.5 | async-start | bytes 1622016 | tf_op jit(solution)/shard_map/all_gather | solution.py:125
  264.6 2.4 copy-start.7
  264.6 2.4 copy-start.10
  264.6 4.1 copy-start.12
  264.6 5.8 %copy-start.1 = (bf16[2,8,1536]{2,1,0:T(8,128)(2,1)S(1)}, bf16[2,8,1536]{2,1,0:T(8,128)(2,1)}, u32[]{:S(2)}) copy-start(bf16[2,8,1536]{2,1,0:T(8,128)(2,1)} %copy-done) | copy-start | bytes 147460
  264.6 5.8 %copy-start.4 = (bf16[2,8,1536]{2,1,0:T(8,128)(2,1)S(1)}, bf16[2,8,1536]{2,1,0:T(8,128)(2,1)}, u32[]{:S(2)}) copy-start(bf16[2,8,1536]{2,1,0:T(8,128)(2,1)} %copy-done.3) | copy-start | bytes 147460
  265.2 3.6 collective-permute-start
  269.2 0.6 copy-start.8
  269.2 0.7 copy-start.11
  269.8 120.3 %all-gather.17.cloned.1.call-start = ((), (), s32[]{:S(2)}) async-start(), calls=%async_computation.4 | async-start | bytes 1622016 | tf_op jit(solution)/shard_map/all_gather | solution.py:126
  270.4 179.6 %all-gather.23.cloned.1.call-start = ((), (), s32[]{:S(2)}) async-start(), calls=%async_computation.7 | async-start | bytes 1622016 | tf_op jit(solution)/shard_map/all_gather | solution.py:125
  392.7 0.6 copy-start.2
  392.8 0.7 copy-start.5
  393.4 116.1 %all-gather.21.cloned.1.call-start = ((), (), s32[]{:S(2)}) async-start(), calls=%async_computation.6 | async-start | bytes 1622016 | tf_op jit(solution)/shard_map/all_gather | solution.py:126
Sparse Core Ops, SparseCore 0:
  18.8 65.1 all-gather.10
  87.1 56.4 all-gather.8
  147.0 56.3 all-gather.14
  206.4 56.4 all-gather.12
  269.9 60.6 all-gather.18
  333.6 56.4 all-gather.16
  393.5 56.3 all-gather.22
  453.1 56.4 all-gather.20
where the time goes:
time: 520 us; the launch traced here: 519 us
  waiting for transfers between devices  465 us (89%)
  between operations  22.2 us (4%)
  local copies, waits for them, and re-layouts  21.8 us (4%)
    all_gather x4, waiting for transfers between devices, per_device(): lax.all_gather(flat_keys, 'ctx', axis=0, tiled=True)  234 us
    all_gather x4, waiting for transfers between devices, per_device(): lax.all_gather(flat_values, 'ctx', axis=0, tiled=True)  229 us
  transfers between devices with their start and end apart: 9, of which 8 were waited for; matrix products, arithmetic and copies ran while one was open for 2% of the time, Pallas kernels for 0%

commit v1 on v0

v1 whole, which is shorter than its diff:
```python
import math

import jax
import jax.numpy as jnp
from jax import lax
from jax.sharding import Mesh
from jax.sharding import PartitionSpec as P

HD = 128
EPSILON = 1e-06

HEAD_AXIS = "cx"
TOKEN_AXES = ("cz", "cc")
CTX_AXES = ("cx", "cz", "cc")


def head_norm(values):
    return values * lax.rsqrt(jnp.mean(values * values, axis=-1, keepdims=True) + EPSILON)


def to_head_groups(rows, groups):
    *lead, n, width = rows.shape
    split = rows.reshape(*lead, n, groups, width // groups)
    return jnp.moveaxis(split, -2, 0)


def per_device(
    perturbed_frame_activation,
    inbound_activation,
    section_block_indices,
    tile_arrival_permutation,
    adaptive_shifting,
    adaptive_scaling,
    tier_query_factor,
    tier_skip_coefficient,
    earlier_step_lookup_matrix,
    earlier_step_content_matrix,
):
    segment = lax.axis_index("segment")
    patch_count = tile_arrival_permutation.shape[0]
    rows = inbound_activation.shape[1]
    width = inbound_activation.shape[2]
    heads = width // HD
    groups = lax.axis_size(HEAD_AXIS)
    group_width = width // groups
    group_heads = heads // groups
    slot_count = earlier_step_lookup_matrix.shape[1]
    layers_here = section_block_indices[0]
    scale = 1.0 / math.sqrt(HD)

    def gather_head_group(kv_rows):
        parts = to_head_groups(kv_rows, groups)
        mine = lax.all_to_all(parts, HEAD_AXIS, 0, 0)
        mine = jnp.moveaxis(mine, 0, -3)
        mine = mine.reshape(*mine.shape[:-3], groups * rows, group_width)
        return lax.all_gather(mine, TOKEN_AXES, axis=mine.ndim - 2, tiled=True)

    other_patch = tile_arrival_permutation[jnp.mod(1 - segment, patch_count)]
    other_k = lax.dynamic_index_in_dim(earlier_step_lookup_matrix[0], other_patch, 1, keepdims=False)
    other_v = lax.dynamic_index_in_dim(earlier_step_content_matrix[0], other_patch, 1, keepdims=False)
    other_kv = gather_head_group(jnp.stack([other_k, other_v], axis=1))

    def layer(state, tier, far_kv):
        live = layers_here > tier
        x = state.astype(jnp.float32)
        hidden = (
            x * lax.rsqrt(jnp.mean(x * x, axis=-1, keepdims=True) + EPSILON)
            * (1.0 + adaptive_scaling[0, tier])
            + adaptive_shifting[0, tier]
        )
        query = head_norm(hidden.reshape(rows, heads, HD)).reshape(rows, width).astype(jnp.bfloat16)
        fresh_key = (
            head_norm((hidden * tier_query_factor[0, tier]).reshape(rows, heads, HD))
            .reshape(rows, width)
            .astype(jnp.bfloat16)
        )
        fresh_value = hidden.astype(jnp.bfloat16)
        packed = to_head_groups(jnp.stack([query, fresh_key, fresh_value]), groups)
        mine = lax.all_to_all(packed, HEAD_AXIS, 0, 0)
        local_q = mine[:, 0].reshape(groups * rows, group_heads, HD)
        near_kv = jnp.moveaxis(mine[:, 1:], 0, 1).reshape(2, groups * rows, group_width)
        near_kv = lax.all_gather(near_kv, TOKEN_AXES, axis=1, tiled=True)
        keys = jnp.concatenate([near_kv[0], far_kv[0]], axis=0)
        values = jnp.concatenate([near_kv[1], far_kv[1]], axis=0)
        key_count = keys.shape[0]
        scores = jnp.einsum(
            "phd,nhd->phn",
            local_q,
            keys.reshape(key_count, group_heads, HD),
            preferred_element_type=jnp.float32,
        ) * scale
        weights = jnp.exp(scores)
        total = jnp.sum(weights, axis=-1)
        numerator = jnp.einsum(
            "phn,nhd->phd",
            weights.astype(jnp.bfloat16),
            values.reshape(key_count, group_heads, HD),
            preferred_element_type=jnp.float32,
        )
        attended = (numerator / total[..., None]).reshape(groups, rows, group_width)
        back = lax.all_to_all(attended, HEAD_AXIS, 0, 0)
        back = jnp.moveaxis(back, 0, 1).reshape(rows, width)
        new_state = (x + tier_skip_coefficient[0, tier] * back).astype(jnp.bfloat16)
        return jnp.where(live, new_state, state), near_kv

    outcomes = []
    state = jnp.where(
        segment == 0,
        lax.dynamic_index_in_dim(perturbed_frame_activation, tile_arrival_permutation[0], 0, keepdims=False),
        inbound_activation[0],
    )
    first_turn_kv = []
    for tier in range(slot_count):
        state, near_kv = layer(state, tier, other_kv[tier])
        first_turn_kv.append(near_kv)
    outcomes.append(state)
    for turn in range(1, patch_count):
        count = lax.axis_size("segment")
        arrived = lax.ppermute(state, "segment", [(i, i + 1) for i in range(count - 1)])
        state = jnp.where(
            segment == 0,
            lax.dynamic_index_in_dim(
                perturbed_frame_activation, tile_arrival_permutation[turn], 0, keepdims=False
            ),
            arrived,
        )
        for tier in range(slot_count):
            state, _ = layer(state, tier, first_turn_kv[tier])
        outcomes.append(state)
    return jnp.stack(outcomes)[None]


def solution(mesh):
    segments, ctx = mesh.devices.shape
    heads_mesh = Mesh(mesh.devices.reshape(segments, 4, ctx // 8, 2), ("segment",) + CTX_AXES)
    return jax.shard_map(
        per_device,
        mesh=heads_mesh,
        in_specs=(
            P(None, CTX_AXES, None),
            P("segment", CTX_AXES, None),
            P("segment"),
            P(),
            P("segment", None, None),
            P("segment", None, None),
            P("segment", None, None),
            P("segment", None, None),
            P("segment", None, None, CTX_AXES, None),
            P("segment", None, None, CTX_AXES, None),
        ),
        out_specs=P("segment", None, CTX_AXES, None),
        check_vma=False,
    )
```

time: 520 us -> 180 us (0.35)
  the two profiles are of different devices: /device:TPU:1 before, /device:TPU:33 now
where the time goes in v1:
time: 180 us; the launch traced here: 178 us
  blocking collectives  112 us (62%)
  starting transfers between devices  26.4 us (15%)
  waiting for transfers between devices  18.1 us (10%)
  local copies, waits for them, and re-layouts  8.84 us (5%)
  between operations  7.15 us (4%)
  other arithmetic  3.88 us (2%)
  matrix products  2.12 us (1%)
    all_gather x4, blocking collectives, layer(): near_kv = lax.all_gather(near_kv, TOKEN_AXES, axis=1, tiled=True)  75.5 us
    all_gather x1, blocking collectives, gather_head_group(): return lax.all_gather(mine, TOKEN_AXES, axis=mine.ndim - 2, tiled=True)  15.5 us
    all_to_all x2, blocking collectives, layer(): mine = lax.all_to_all(packed, HEAD_AXIS, 0, 0)  13.8 us
    all_to_all x3, waiting for transfers between devices, layer(): back = lax.all_to_all(attended, HEAD_AXIS, 0, 0)  12.4 us
    all_to_all x3, starting transfers between devices, layer(): back = lax.all_to_all(attended, HEAD_AXIS, 0, 0)  11.1 us
    all_to_all x2, starting transfers between devices, layer(): mine = lax.all_to_all(packed, HEAD_AXIS, 0, 0)  7.43 us
    all_to_all x1, blocking collectives, layer(): back = lax.all_to_all(attended, HEAD_AXIS, 0, 0)  6.75 us
    all_to_all x2, waiting for transfers between devices, layer(): mine = lax.all_to_all(packed, HEAD_AXIS, 0, 0)  5.49 us
  transfers between devices with their start and end apart: 7, of which 6 were waited for; matrix products, arithmetic and copies ran while one was open for 1% of the time, Pallas kernels for 0%

profile of v1, /device:TPU:33, one launch (start us, length us, event | category | flops | bytes accessed | tf_op | source)
XLA Modules:
  0.0 178.0 jit_solution(13781949084585847155)
XLA Ops:
  0.7 0.7 fusion.130
  5.1 4.1 %all-to-all-start = ((bf16[4,3,8,384]{3,2,1,0:T(8,128)(2,1)}), bf16[4,3,8,384]{3,2,1,0:T(8,128)(2,1)S(1)}, u32[]{:S(2)}, u32[]{:S(2)}) async-start(bf16[4,3,8,384]{3,2,1,0:T(8,128)(2,1)} %maximum_bitcast_fusion.1), calls=%async_computation | async-start | bytes 147456 | tf_op jit(solution)/shard_map/all_to_all | solution.py:79
  12.1 1.6 all-to-all-done
  13.8 3.3 %all-to-all-start.1 = ((bf16[4,2,2,8,384]{4,3,1,2,0:T(8,128)(2,1)}), bf16[4,2,2,8,384]{4,3,1,2,0:T(8,128)(2,1)S(1)}, u32[]{:S(2)}, u32[]{:S(2)}) async-start(bf16[4,2,2,8,384]{4,3,1,2,0:T(8,128)(2,1)} %copy.78), calls=%async_computation.1 | async-start | bytes 196608 | tf_op jit(solution)/shard_map/all_to_all | solution.py:53
  17.1 22.3 %all_gather.15 = bf16[2,256,384]{2,1,0:T(8,128)(2,1)S(1)} all-gather(bf16[2,32,384]{2,1,0:T(8,128)(2,1)S(1)} %copy_bitcast_fusion.4), channel_id=1, replica_groups=mesh['segment'=16,'cx'=4,'cz'=4,'cc'=2] {'cz','cc'}, dimensions={1}, use_global_device_ids=true | all-gather | bytes 442368 | tf_op jit(solution)/shard_map/all_gather | solution.py:82
  40.1 15.5 %all_gather.16 = bf16[2,2,256,384]{3,2,1,0:T(8,128)(2,1)S(1)} all-gather(bf16[2,2,32,384]{3,2,1,0:T(8,128)(2,1)S(1)} %bitcast.189), channel_id=1, replica_groups=mesh['segment'=16,'cx'=4,'cz'=4,'cc'=2] {'cz','cc'}, dimensions={2}, use_global_device_ids=true | all-gather | bytes 884736 | tf_op jit(solution)/shard_map/all_gather | solution.py:56
  56.9 0.6 reshape.603
  57.5 4.6 %all-to-all-start.2 = ((f32[4,8,384]{2,1,0:T(8,128)}), f32[4,8,384]{2,1,0:T(8,128)S(1)}, u32[]{:S(2)}, u32[]{:S(2)}) async-start(f32[4,8,384]{2,1,0:T(8,128)} %reshape.603), calls=%async_computation.2 | async-start | bytes 98304 | tf_op jit(solution)/shard_map/all_to_all | solution.py:101
  62.8 3.7 %all-to-all-done.2 = f32[4,8,384]{2,1,0:T(8,128)S(1)} async-done(((f32[4,8,384]{2,1,0:T(8,128)}), f32[4,8,384]{2,1,0:T(8,128)S(1)}, u32[]{:S(2)}, u32[]{:S(2)}) %all-to-all-start.2) | async-done | bytes 49184 | tf_op jit(solution)/shard_map/all_to_all | solution.py:101
  67.7 3.3 %all-to-all-start.3 = ((bf16[4,3,8,384]{3,2,1,0:T(8,128)(2,1)}), bf16[4,3,8,384]{3,2,1,0:T(8,128)(2,1)S(1)}, u32[]{:S(2)}, u32[]{:S(2)}) async-start(bf16[4,3,8,384]{3,2,1,0:T(8,128)(2,1)} %maximum_bitcast_fusion.2), calls=%async_computation.3 | async-start | bytes 147456 | tf_op jit(solution)/shard_map/all_to_all | solution.py:79
  71.6 3.8 %all-to-all-done.3 = bf16[4,3,8,384]{3,2,1,0:T(8,128)(2,1)S(1)} async-done(((bf16[4,3,8,384]{3,2,1,0:T(8,128)(2,1)}), bf16[4,3,8,384]{3,2,1,0:T(8,128)(2,1)S(1)}, u32[]{:S(2)}, u32[]{:S(2)}) %all-to-all-start.3) | async-done | bytes 73760 | tf_op jit(solution)/shard_map/all_to_all | solution.py:79
  75.5 17.4 %all_gather.17 = bf16[2,256,384]{2,1,0:T(8,128)(2,1)S(1)} all-gather(bf16[2,32,384]{2,1,0:T(8,128)(2,1)S(1)} %copy_bitcast_fusion.3), channel_id=1, replica_groups=mesh['segment'=16,'cx'=4,'cz'=4,'cc'=2] {'cz','cc'}, dimensions={1}, use_global_device_ids=true | all-gather | bytes 442368 | tf_op jit(solution)/shard_map/all_gather | solution.py:82
  94.2 0.6 reshape.608
  94.9 3.3 %all-to-all-start.4 = ((f32[4,8,384]{2,1,0:T(8,128)}), f32[4,8,384]{2,1,0:T(8,128)S(1)}, u32[]{:S(2)}, u32[]{:S(2)}) async-start(f32[4,8,384]{2,1,0:T(8,128)} %reshape.608), calls=%async_computation.4 | async-start | bytes 98304 | tf_op jit(solution)/shard_map/all_to_all | solution.py:101
  98.1 4.3 %all-to-all-done.4 = f32[4,8,384]{2,1,0:T(8,128)S(1)} async-done(((f32[4,8,384]{2,1,0:T(8,128)}), f32[4,8,384]{2,1,0:T(8,128)S(1)}, u32[]{:S(2)}, u32[]{:S(2)}) %all-to-all-start.4) | async-done | bytes 49184 | tf_op jit(solution)/shard_map/all_to_all | solution.py:101
  102.5 4.5 %collective-permute-start = (bf16[8,1536]{1,0:T(8,128)(2,1)S(1)}, bf16[8,1536]{1,0:T(8,128)(2,1)S(1)}, u32[]{:S(2)}, u32[]{:S(2)}) collective-permute-start(bf16[8,1536]{1,0:T(8,128)(2,1)S(1)} %fusion.104), channel_id=1, source_target_pairs={{0,32},{32,64},{64,96},{96,128},{128,160},{160,192},{192,224},{224... | collective-permute-start | bytes 73736 | tf_op jit(solution)/shard_map/ppermute | solution.py:119
  109.7 6.9 %all_to_all.45 = bf16[4,3,8,384]{3,2,1,0:T(8,128)(2,1)S(1)} all-to-all(bf16[4,3,8,384]{3,2,1,0:T(8,128)(2,1)S(1)} %maximum_bitcast_fusion.3), channel_id=1, replica_groups=mesh['segment'=16,'cx'=4,'cz'=4,'cc'=2] {'cx'}, dimensions={0} | all-to-all | bytes 147456 | tf_op jit(solution)/shard_map/all_to_all | solution.py:79
  116.6 18.3 %all_gather.18 = bf16[2,256,384]{2,1,0:T(8,128)(2,1)S(1)} all-gather(bf16[2,32,384]{2,1,0:T(8,128)(2,1)S(1)} %copy_bitcast_fusion.2), channel_id=1, replica_groups=mesh['segment'=16,'cx'=4,'cz'=4,'cc'=2] {'cz','cc'}, dimensions={1}, use_global_device_ids=true | all-gather | bytes 442368 | tf_op jit(solution)/shard_map/all_gather | solution.py:82
  136.2 6.7 %all_to_all.46 = f32[4,8,384]{2,1,0:T(8,128)S(1)} all-to-all(f32[4,8,384]{2,1,0:T(8,128)S(1)} %reshape.612), channel_id=1, replica_groups=mesh['segment'=16,'cx'=4,'cz'=4,'cc'=2] {'cx'}, dimensions={0} | all-to-all | bytes 98304 | tf_op jit(solution)/shard_map/all_to_all | solution.py:101
  143.4 6.9 %all_to_all.47 = bf16[4,3,8,384]{3,2,1,0:T(8,128)(2,1)S(1)} all-to-all(bf16[4,3,8,384]{3,2,1,0:T(8,128)(2,1)S(1)} %maximum_bitcast_fusion.4), channel_id=1, replica_groups=mesh['segment'=16,'cx'=4,'cz'=4,'cc'=2] {'cx'}, dimensions={0} | all-to-all | bytes 147456 | tf_op jit(solution)/shard_map/all_to_all | solution.py:79
  150.3 17.5 %all_gather.19 = bf16[2,256,384]{2,1,0:T(8,128)(2,1)S(1)} all-gather(bf16[2,32,384]{2,1,0:T(8,128)(2,1)S(1)} %copy_bitcast_fusion.1), channel_id=1, replica_groups=mesh['segment'=16,'cx'=4,'cz'=4,'cc'=2] {'cz','cc'}, dimensions={1}, use_global_device_ids=true | all-gather | bytes 442368 | tf_op jit(solution)/shard_map/all_gather | solution.py:82
  169.1 0.6 reshape.615
  169.8 3.3 %all-to-all-start.8 = ((f32[4,8,384]{2,1,0:T(8,128)}), f32[4,8,384]{2,1,0:T(8,128)S(1)}, u32[]{:S(2)}, u32[]{:S(2)}) async-start(f32[4,8,384]{2,1,0:T(8,128)} %reshape.615), calls=%async_computation.8 | async-start | bytes 98304 | tf_op jit(solution)/shard_map/all_to_all | solution.py:101
  173.1 4.3 %all-to-all-done.8 = f32[4,8,384]{2,1,0:T(8,128)S(1)} async-done(((f32[4,8,384]{2,1,0:T(8,128)}), f32[4,8,384]{2,1,0:T(8,128)S(1)}, u32[]{:S(2)}, u32[]{:S(2)}) %all-to-all-start.8) | async-done | bytes 49184 | tf_op jit(solution)/shard_map/all_to_all | solution.py:101
  (116 shorter events, 12.5 us)
Async XLA Ops:
  0.0 0.7 copy-start.8
  0.0 2.6 %copy-start.4 = (f32[1,2,1536]{2,1,0:T(2,128)S(1)}, f32[1,2,1536]{2,1,0:T(2,128)}, u32[]{:S(2)}) copy-start(f32[1,2,1536]{2,1,0:T(2,128)} %param.14) | copy-start | bytes 36868
  0.0 2.7 %copy-start.5 = (f32[1,2,1536]{2,1,0:T(2,128)S(1)}, f32[1,2,1536]{2,1,0:T(2,128)}, u32[]{:S(2)}) copy-start(f32[1,2,1536]{2,1,0:T(2,128)} %param.15) | copy-start | bytes 36868
  0.0 3.4 %copy-start = (bf16[2,8,1536]{2,1,0:T(8,128)(2,1)S(1)}, bf16[2,8,1536]{2,1,0:T(8,128)(2,1)}, u32[]{:S(2)}) copy-start(bf16[2,8,1536]{2,1,0:T(8,128)(2,1)} %param.10) | copy-start | bytes 147460
  2.6 0.8 copy-start.3
  3.4 0.7 copy-start.6
  4.5 6.9 %copy-start.2 = (bf16[1,2,2,8,1536]{4,3,2,1,0:T(8,128)(2,1)S(1)}, bf16[1,2,2,8,1536]{4,3,2,1,0:T(8,128)(2,1)}, u32[]{:S(2)}) copy-start(bf16[1,2,2,8,1536]{4,3,2,1,0:T(8,128)(2,1)} %param.18) | copy-start | bytes 294916
  5.1 6.2 %copy-start.1 = (bf16[1,2,2,8,1536]{4,3,2,1,0:T(8,128)(2,1)S(1)}, bf16[1,2,2,8,1536]{4,3,2,1,0:T(8,128)(2,1)}, u32[]{:S(2)}) copy-start(bf16[1,2,2,8,1536]{4,3,2,1,0:T(8,128)(2,1)} %param.19) | copy-start | bytes 294916
  5.1 8.7 %all-to-all-start = ((bf16[4,3,8,384]{3,2,1,0:T(8,128)(2,1)}), bf16[4,3,8,384]{3,2,1,0:T(8,128)(2,1)S(1)}, u32[]{:S(2)}, u32[]{:S(2)}) async-start(bf16[4,3,8,384]{3,2,1,0:T(8,128)(2,1)} %maximum_bitcast_fusion.1), calls=%async_computation | async-start | bytes 147456 | tf_op jit(solution)/shard_map/all_to_all | solution.py:79
  13.8 26.3 %all-to-all-start.1 = ((bf16[4,2,2,8,384]{4,3,1,2,0:T(8,128)(2,1)}), bf16[4,2,2,8,384]{4,3,1,2,0:T(8,128)(2,1)S(1)}, u32[]{:S(2)}, u32[]{:S(2)}) async-start(bf16[4,2,2,8,384]{4,3,1,2,0:T(8,128)(2,1)} %copy.78), calls=%async_computation.1 | async-start | bytes 196608 | tf_op jit(solution)/shard_map/all_to_all | solution.py:53
  57.5 4.6 %copy-start.7 = (f32[1,2,1536]{2,1,0:T(2,128)S(1)}, f32[1,2,1536]{2,1,0:T(2,128)}, u32[]{:S(2)}) copy-start(f32[1,2,1536]{2,1,0:T(2,128)} %param.17) | copy-start | bytes 36868
  57.5 9.0 %all-to-all-start.2 = ((f32[4,8,384]{2,1,0:T(8,128)}), f32[4,8,384]{2,1,0:T(8,128)S(1)}, u32[]{:S(2)}, u32[]{:S(2)}) async-start(f32[4,8,384]{2,1,0:T(8,128)} %reshape.603), calls=%async_computation.2 | async-start | bytes 98304 | tf_op jit(solution)/shard_map/all_to_all | solution.py:101
  67.7 7.8 %all-to-all-start.3 = ((bf16[4,3,8,384]{3,2,1,0:T(8,128)(2,1)}), bf16[4,3,8,384]{3,2,1,0:T(8,128)(2,1)S(1)}, u32[]{:S(2)}, u32[]{:S(2)}) async-start(bf16[4,3,8,384]{3,2,1,0:T(8,128)(2,1)} %maximum_bitcast_fusion.2), calls=%async_computation.3 | async-start | bytes 147456 | tf_op jit(solution)/shard_map/all_to_all | solution.py:79
  94.9 7.6 %all-to-all-start.4 = ((f32[4,8,384]{2,1,0:T(8,128)}), f32[4,8,384]{2,1,0:T(8,128)S(1)}, u32[]{:S(2)}, u32[]{:S(2)}) async-start(f32[4,8,384]{2,1,0:T(8,128)} %reshape.608), calls=%async_computation.4 | async-start | bytes 98304 | tf_op jit(solution)/shard_map/all_to_all | solution.py:101
  102.5 6.7 %collective-permute-start = (bf16[8,1536]{1,0:T(8,128)(2,1)S(1)}, bf16[8,1536]{1,0:T(8,128)(2,1)S(1)}, u32[]{:S(2)}, u32[]{:S(2)}) collective-permute-start(bf16[8,1536]{1,0:T(8,128)(2,1)S(1)} %fusion.104), channel_id=1, source_target_pairs={{0,32},{32,64},{64,96},{96,128},{128,160},{160,192},{192,224},{224... | collective-permute-start | bytes 73736 | tf_op jit(solution)/shard_map/ppermute | solution.py:119
  169.8 7.6 %all-to-all-start.8 = ((f32[4,8,384]{2,1,0:T(8,128)}), f32[4,8,384]{2,1,0:T(8,128)S(1)}, u32[]{:S(2)}, u32[]{:S(2)}) async-start(f32[4,8,384]{2,1,0:T(8,128)} %reshape.615), calls=%async_computation.8 | async-start | bytes 98304 | tf_op jit(solution)/shard_map/all_to_all | solution.py:101

commit v2 on v1

v2 whole, which is shorter than its diff:
```python
import math

import jax
import jax.numpy as jnp
from jax import lax
from jax.sharding import PartitionSpec as P

HD = 128
EPSILON = 1e-06


def head_norm(values):
    return values * lax.rsqrt(jnp.mean(values * values, axis=-1, keepdims=True) + EPSILON)


def per_device(
    perturbed_frame_activation,
    inbound_activation,
    section_block_indices,
    tile_arrival_permutation,
    adaptive_shifting,
    adaptive_scaling,
    tier_query_factor,
    tier_skip_coefficient,
    earlier_step_lookup_matrix,
    earlier_step_content_matrix,
):
    segment = lax.axis_index("segment")
    place = lax.axis_index("ctx")
    patch_count = tile_arrival_permutation.shape[0]
    rows = inbound_activation.shape[1]
    width = inbound_activation.shape[2]
    heads = width // HD
    slot_count = earlier_step_lookup_matrix.shape[1]
    layers_here = section_block_indices[0]
    scale = 1.0 / math.sqrt(HD)

    def pick_patch(stack, patch, axis):
        return lax.dynamic_index_in_dim(stack, patch, axis, keepdims=False)

    first_rows = jnp.where(
        segment == 0,
        pick_patch(perturbed_frame_activation, tile_arrival_permutation[0], 0),
        inbound_activation[0],
    )
    entry_rows = [first_rows[None]]
    for turn in range(1, patch_count):
        entry_rows.append(pick_patch(perturbed_frame_activation, tile_arrival_permutation[turn], 0)[None])
    other_patch = tile_arrival_permutation[jnp.mod(1 - segment, patch_count)]
    far_k = pick_patch(earlier_step_lookup_matrix[0], other_patch, 1)
    far_v = pick_patch(earlier_step_content_matrix[0], other_patch, 1)
    packed = jnp.concatenate(entry_rows + [far_k, far_v], axis=0)
    whole = lax.all_gather(packed, "ctx", axis=1, tiled=True)
    entry = whole[:patch_count]
    far_k = whole[patch_count : patch_count + slot_count]
    far_v = whole[patch_count + slot_count :]
    tokens = whole.shape[1]

    def layer(state, tier, keys_far, values_far):
        live = layers_here > tier
        x = state.astype(jnp.float32)
        hidden = (
            x * lax.rsqrt(jnp.mean(x * x, axis=-1, keepdims=True) + EPSILON)
            * (1.0 + adaptive_scaling[0, tier])
            + adaptive_shifting[0, tier]
        )
        query = head_norm(hidden.reshape(tokens, heads, HD)).astype(jnp.bfloat16)
        fresh_key = head_norm((hidden * tier_query_factor[0, tier]).reshape(tokens, heads, HD)).astype(
            jnp.bfloat16
        )
        fresh_value = hidden.astype(jnp.bfloat16).reshape(tokens, heads, HD)
        keys = jnp.concatenate([fresh_key, keys_far.reshape(tokens, heads, HD)], axis=0)
        values = jnp.concatenate([fresh_value, values_far.reshape(tokens, heads, HD)], axis=0)
        scores = jnp.einsum("phd,nhd->phn", query, keys, preferred_element_type=jnp.float32) * scale
        weights = jnp.exp(scores)
        total = jnp.sum(weights, axis=-1)
        numerator = jnp.einsum(
            "phn,nhd->phd", weights.astype(jnp.bfloat16), values, preferred_element_type=jnp.float32
        )
        attended = (numerator / total[..., None]).reshape(tokens, width)
        new_state = (x + tier_skip_coefficient[0, tier] * attended).astype(jnp.bfloat16)
        return jnp.where(live, new_state, state), fresh_key.reshape(tokens, width), fresh_value.reshape(
            tokens, width
        )

    def own_rows(state):
        return lax.dynamic_slice_in_dim(state, place * rows, rows, 0)

    outcomes = []
    state = entry[0]
    turn_zero_kv = []
    for tier in range(slot_count):
        state, fresh_key, fresh_value = layer(state, tier, far_k[tier], far_v[tier])
        turn_zero_kv.append((fresh_key, fresh_value))
    outcomes.append(own_rows(state))
    count = lax.axis_size("segment")
    for turn in range(1, patch_count):
        arrived = lax.ppermute(state, "segment", [(i, i + 1) for i in range(count - 1)])
        state = jnp.where(segment == 0, entry[turn], arrived)
        for tier in range(slot_count):
            state, _, _ = layer(state, tier, *turn_zero_kv[tier])
        outcomes.append(own_rows(state))
    return jnp.stack(outcomes)[None]


def solution(mesh):
    return jax.shard_map(
        per_device,
        mesh=mesh,
        in_specs=(
            P(None, "ctx", None),
            P("segment", "ctx", None),
            P("segment"),
            P(),
            P("segment", None, None),
            P("segment", None, None),
            P("segment", None, None),
            P("segment", None, None),
            P("segment", None, None, "ctx", None),
            P("segment", None, None, "ctx", None),
        ),
        out_specs=P("segment", None, "ctx", None),
        check_vma=False,
    )
```

time: 180 us -> 189 us (1.050)
  blocking collectives: 112 us -> 0 us
  waiting for transfers between devices: 18.1 us -> 90.8 us
  local copies, waits for them, and re-layouts: 8.84 us -> 40.8 us
  starting transfers between devices: 26.4 us -> 2.49 us
  other arithmetic: 3.88 us -> 19.9 us
  between operations: 7.15 us -> 20.3 us
  matrix products: 2.12 us -> 13.6 us
    all_gather x5 -> x0, blocking collectives: 91 us -> none  [the longest x4 75.5 us: layer(): near_kv = lax.all_gather(near_kv, TOKEN_AXES, axis=1, tiled=True)]
    all_gather x0 -> x1, waiting for transfers between devices: none -> 70.4 us  [per_device(): whole = lax.all_gather(packed, 'ctx', axis=1, tiled=True)]
    all_to_all x6 -> x0, starting transfers between devices: 21.9 us -> none  [the longest x3 11.1 us: layer(): back = lax.all_to_all(attended, HEAD_AXIS, 0, 0)]
    all_to_all x3 -> x0, blocking collectives: 20.5 us -> none  [the longest x2 13.8 us: layer(): mine = lax.all_to_all(packed, HEAD_AXIS, 0, 0)]
    ppermute x1, waiting for transfers between devices: 0.24 us -> 20.4 us  [per_device(): lax.ppermute(state, 'segment', [(i, i + 1) for i in range(count - 1)])]
    all_to_all x6 -> x0, waiting for transfers between devices: 17.9 us -> none  [the longest x3 12.4 us: layer(): back = lax.all_to_all(attended, HEAD_AXIS, 0, 0)]
    dot_general x8, matrix products: 2.12 us -> 13.6 us  [the longest x4 7.99 us: layer(): jnp.einsum('phn,nhd->phd', weights.astype(jnp.bfloat16), values, preferre...]
    reshape x8 -> x7, local copies, waits for them, and re-layouts: 1.99 us -> 11.5 us  [the longest x3 6.77 us: layer(): attended = (numerator / total[..., None]).reshape(tokens, width)]
  transfers between devices with their start and end apart: 7 -> 2, of which waited for: 6 -> 2; matrix products, arithmetic and copies ran while one was open for 1% -> 1% of each run, Pallas kernels for 0% -> 0%
where the time goes in v2:
time: 189 us; the launch traced here: 188 us
  waiting for transfers between devices  90.8 us (48%)
  local copies, waits for them, and re-layouts  40.8 us (22%)
  between operations  20.3 us (11%)
  other arithmetic  19.9 us (11%)
  matrix products  13.6 us (7%)
  starting transfers between devices  2.49 us (1%)
    all_gather x1, waiting for transfers between devices, per_device(): whole = lax.all_gather(packed, 'ctx', axis=1, tiled=True)  70.4 us
    ppermute x1, waiting for transfers between devices, per_device(): lax.ppermute(state, 'segment', [(i, i + 1) for i in range(count - 1)])  20.4 us
    dot_general x4, matrix products, layer(): jnp.einsum('phn,nhd->phd', weights.astype(jnp.bfloat16), values, preferre...  7.99 us
    slice x5, local copies, waits for them, and re-layouts, per_device(): state, fresh_key, fresh_value = layer(state, tier, far_k[tier], far_v[tier])  6.85 us
    reshape x3, local copies, waits for them, and re-layouts, layer(): attended = (numerator / total[..., None]).reshape(tokens, width)  6.77 us
    dot_general x4, matrix products, layer(): jnp.einsum('phd,nhd->phn', query, keys, preferred_element_type=jnp.float32)  5.63 us
    reduce_sum x4, other arithmetic, layer(): jnp.mean(x * x, axis=-1, keepdims=True) + EPSILON  5.12 us
    convert_element_type x3, other arithmetic, layer(): fresh_value = hidden.astype(jnp.bfloat16).reshape(tokens, heads, HD)  4.79 us
  transfers between devices with their start and end apart: 2, of which 2 were waited for; matrix products, arithmetic and copies ran while one was open for 1% of the time, Pallas kernels for 0%

profile of v2, /device:TPU:33, one launch (start us, length us, event | category | flops | bytes accessed | tf_op | source)
XLA Modules:
  0.0 187.9 jit_solution(44315173992806719)
XLA Ops:
  19.1 70.4 %all-gather.2.cloned.1.call-done = bf16[6,256,1536]{2,1,0:T(8,128)(2,1)} async-done(((bf16[6,8,1536]{2,1,0:T(8,128)(2,1)}), bf16[6,256,1536]{2,1,0:T(8,128)(2,1)}) %all-gather.2.cloned.1.call-update) | async-done | bytes 4718608 | tf_op jit(solution)/shard_map/all_gather | solution.py:53
  90.9 3.5 %fusion.105 = (bf16[1,256,1536]{2,1,0:T(8,128)(2,1)}, bf16[1,256,1536]{2,1,0:T(8,128)(2,1)}, bf16[1,256,1536]{2,1,0:T(8,128)(2,1)S(1)}, bf16[1,256,1536]{2,1,0:T(8,128)(2,1)S(1)}, bf16[1,256,1536]{2,1,0:T(8,128)(2,1)S(1)}) fusion(bf16[6,256,1536]{2,1,0:T(8,128)(2,1)} %all-gather.2.cloned.1.call-done), kind=kLoop, calls=%fused_computation.164 | loop fusion | bytes 7864320 | tf_op jit(solution)/shard_map/slice | solution.py:93
  104.0 1.5 bitcast_reduce_fusion.3
  105.5 2.0 %bitcast_divide_fusion.3 = f32[256,12,128]{2,0,1:T(8,128)S(1)} fusion(f32[12,512,256]{2,1,0:T(8,128)S(1)} %get-tuple-element.43, bf16[256,12,128]{2,0,1:T(8,128)(2,1)S(1)} %copy.29, bf16[256,12,128]{2,0,1:T(8,128)(2,1)S(1)} %get-tuple-element.36, f32[256,12]{0,1:T(8,128)S(1)} %get-tuple-element.42), kind=kOutput, calls=%fused_computation.81 | convolution fusion | flops 409337856 | bytes 9449472 | tf_op jit(solution)/shard_map/phn,nhd->phd/dot_general | solution.py:77
  107.5 1.6 copy.35
  109.1 3.0 %copy.36 = f32[256,1536]{1,0:T(8,128)} copy(f32[256,1536]{0,1:T(8,128)} %bitcast.90) | data formatting | bytes 3145728 | tf_op jit(solution)/shard_map/reshape | solution.py:80
  112.2 2.0 %fusion.23 = (f32[256]{0:T(256)S(1)}, bf16[256,1536]{1,0:T(8,128)(2,1)S(1)}) fusion(f32[256,1536]{1,0:T(8,128)} %copy.36, f32[1536]{0:T(1024)S(1)} %get-tuple-element.10, bf16[6,256,1536]{2,1,0:T(8,128)(2,1)} %all-gather.2.cloned.1.call-done, pred[]{:T(512)} %bitcast.1), kind=kLoop, calls=%fused_computation.44 | loop fusion | flops 3145472 | bytes 3152897 | tf_op jit(solution)/shard_map/reduce_sum | solution.py:63
  117.8 2.3 %bitcast_divide_fusion.2 = f32[256,12,128]{0,2,1:T(8,128)} fusion(f32[12,512,256]{2,1,0:T(8,128)S(1)} %get-tuple-element.45, bf16[256,12,128]{2,0,1:T(8,128)(2,1)S(1)} %copy-done.6, bf16[256,12,128]{2,0,1:T(8,128)(2,1)S(1)} %get-tuple-element.21, f32[256,12]{0,1:T(8,128)S(1)} %get-tuple-element.44), kind=kOutput, calls=%fused_computation.80 | convolution fusion | flops 409337856 | bytes 9449472 | tf_op jit(solution)/shard_map/phn,nhd->phd/dot_general | solution.py:77
  120.1 1.9 copy.44
  122.2 2.5 %collective-permute-start = (bf16[256,1536]{1,0:T(8,128)(2,1)S(1)}, bf16[256,1536]{1,0:T(8,128)(2,1)S(1)}, u32[]{:S(2)}, u32[]{:S(2)}) collective-permute-start(bf16[256,1536]{1,0:T(8,128)(2,1)S(1)} %fusion.68), channel_id=1, source_target_pairs={{0,32},{32,64},{64,96},{96,128},{128,160},{160,192},{192,224},{224... | collective-permute-start | bytes 2359304 | tf_op jit(solution)/shard_map/ppermute | solution.py:98
  124.8 20.4 %collective-permute-done = bf16[256,1536]{1,0:T(8,128)(2,1)S(1)} collective-permute-done((bf16[256,1536]{1,0:T(8,128)(2,1)S(1)}, bf16[256,1536]{1,0:T(8,128)(2,1)S(1)}, u32[]{:S(2)}, u32[]{:S(2)}) %collective-permute-start) | collective-permute-done | bytes 786464 | tf_op jit(solution)/shard_map/ppermute | solution.py:98
  145.1 1.5 fusion.25
  146.6 2.2 %fusion.99 = (bf16[256,1536]{1,0:T(8,128)(2,1)}, f32[256,1536]{1,0:T(8,128)}, f32[256,1536]{1,0:T(8,128)}) fusion(f32[1536]{0:T(1024)S(1)} %get-tuple-element.52, f32[1536]{0:T(1024)S(1)} %get-tuple-element.12, f32[256]{0:T(256)S(1)} %add_rsqrt_fusion.9, bf16[256,1536]{1,0:T(8,128)(2,1)S(1)} %get-tuple-element.20, f32[1536]{0:T(1024)S(1)} %get-tuple-element.16), kind=kLoop, calls=%fused_computation.162 | loop fusion | flops 2359296 | bytes 4738048 | tf_op jit(solution)/shard_map/convert_element_type | solution.py:71
  148.9 1.9 copy.47
  150.9 1.6 copy.48
  155.1 1.9 copy.49
  158.9 1.5 bitcast_reduce_fusion.1
  160.4 2.3 %bitcast_divide_fusion.1 = f32[256,12,128]{0,2,1:T(8,128)} fusion(f32[12,512,256]{2,1,0:T(8,128)S(1)} %get-tuple-element.47, bf16[256,12,128]{2,0,1:T(8,128)(2,1)S(1)} %copy-done.13, bf16[256,12,128]{2,0,1:T(8,128)(2,1)S(1)} %copy-done.9, f32[256,12]{0,1:T(8,128)S(1)} %get-tuple-element.46), kind=kOutput, calls=%fused_computation.79 | convolution fusion | flops 409337856 | bytes 9449472 | tf_op jit(solution)/shard_map/phn,nhd->phd/dot_general | solution.py:77
  162.7 1.9 copy.53
  164.6 1.4 fusion.100
  166.3 2.0 %fusion.98 = (bf16[256,1536]{1,0:T(8,128)(2,1)S(1)}, f32[256,1536]{1,0:T(8,128)}, f32[256,1536]{1,0:T(8,128)}) fusion(f32[1536]{0:T(1024)S(1)} %get-tuple-element.53, f32[1536]{0:T(1024)S(1)} %get-tuple-element.11, f32[256]{0:T(256)S(1)} %add_rsqrt_fusion.8, bf16[256,1536]{1,0:T(8,128)(2,1)S(1)} %get-tuple-element.18, f32[1536]{0:T(1024)S(1)} %get-tuple-element.15), kind=kLoop, calls=%fused_computation.161 | loop fusion | flops 2359296 | bytes 4738048 | tf_op jit(solution)/shard_map/convert_element_type | solution.py:71
  168.3 1.9 copy.56
  170.3 1.6 copy.57
  172.6 1.9 copy.58
  (85 shorter events, 32.9 us)
Async XLA Ops:
  6.5 83.0 %all-gather.2.cloned.1.call-start = ((), (), s32[]{:S(2)}) async-start(), calls=%async_computation | async-start | bytes 4866048 | tf_op jit(solution)/shard_map/all_gather | solution.py:53
  102.4 1.6 copy-start.8
  103.4 2.1 %copy-start.12 = (bf16[256,12,128]{2,0,1:T(8,128)(2,1)}, bf16[256,12,128]{2,0,1:T(8,128)(2,1)S(1)}, u32[]{:S(2)}) copy-start(bf16[256,12,128]{2,0,1:T(8,128)(2,1)S(1)} %get-tuple-element.36) | copy-start | bytes 2359300
  104.0 1.5 copy-start.4
  114.7 3.0 %copy-start.10 = (bf16[256,12,128]{2,0,1:T(8,128)(2,1)}, bf16[256,12,128]{2,0,1:T(8,128)(2,1)S(1)}, u32[]{:S(2)}) copy-start(bf16[256,12,128]{2,0,1:T(8,128)(2,1)S(1)} %get-tuple-element.21) | copy-start | bytes 2359300
  114.7 1.6 copy-start.7
  116.3 1.4 copy-start.2
  116.3 1.4 copy-start.6
  122.2 22.9 %collective-permute-start = (bf16[256,1536]{1,0:T(8,128)(2,1)S(1)}, bf16[256,1536]{1,0:T(8,128)(2,1)S(1)}, u32[]{:S(2)}, u32[]{:S(2)}) collective-permute-start(bf16[256,1536]{1,0:T(8,128)(2,1)S(1)} %fusion.68), channel_id=1, source_target_pairs={{0,32},{32,64},{64,96},{96,128},{128,160},{160,192},{192,224},{224... | collective-permute-start | bytes 2359304 | tf_op jit(solution)/shard_map/ppermute | solution.py:98
  157.0 1.4 copy-start
  157.1 1.7 copy-start.5
  158.9 1.5 copy-start.9
  158.9 1.5 copy-start.13
  174.5 1.4 copy-start.1
  174.6 1.7 copy-start.3
  176.4 1.3 copy-start.11
Sparse Core Ops, SparseCore 0:
  16.1 73.4 all-gather.1

commit v3 on v2

--- a/solution.py
+++ b/solution.py
@@ -3,6 +3,7 @@
 import jax
 import jax.numpy as jnp
 from jax import lax
+from jax.experimental import pallas as pl
 from jax.sharding import PartitionSpec as P
 
 HD = 128
@@ -11,6 +12,42 @@
 
 def head_norm(values):
     return values * lax.rsqrt(jnp.mean(values * values, axis=-1, keepdims=True) + EPSILON)
+
+
+def attention_kernel(q_ref, kn_ref, kf_ref, vn_ref, vf_ref, x_ref, skip_ref, o_ref):
+    scale = 1.0 / math.sqrt(HD)
+    dims = (((1,), (1,)), ((), ()))
+    for j in range(q_ref.shape[1] // HD):
+        cols = slice(j * HD, (j + 1) * HD)
+        query = q_ref[:, cols]
+        near = lax.dot_general(query, kn_ref[:, cols], dims, preferred_element_type=jnp.float32) * scale
+        far = lax.dot_general(query, kf_ref[:, cols], dims, preferred_element_type=jnp.float32) * scale
+        near = jnp.exp(near)
+        far = jnp.exp(far)
+        total = jnp.sum(near, axis=-1, keepdims=True) + jnp.sum(far, axis=-1, keepdims=True)
+        numerator = jnp.dot(
+            near.astype(jnp.bfloat16), vn_ref[:, cols], preferred_element_type=jnp.float32
+        ) + jnp.dot(far.astype(jnp.bfloat16), vf_ref[:, cols], preferred_element_type=jnp.float32)
+        attended = numerator / total
+        x = x_ref[:, cols].astype(jnp.float32)
+        o_ref[:, cols] = (x + skip_ref[:, cols] * attended).astype(o_ref.dtype)
+
+
+def attend_and_add(query, near_k, far_k, near_v, far_v, state, skip, block=384):
+    tokens, width = state.shape
+    tile = pl.BlockSpec((tokens, block), lambda i: (0, i))
+    return pl.pallas_call(
+        attention_kernel,
+        out_shape=jax.ShapeDtypeStruct((tokens, width), jnp.bfloat16),
+        grid=(width // block,),
+        in_specs=[tile] * 6 + [pl.BlockSpec((1, block), lambda i: (0, i))],
+        out_specs=tile,
+        cost_estimate=pl.CostEstimate(
+            flops=8 * tokens * 2 * tokens * width,
+            transcendentals=tokens * 2 * tokens * (width // HD),
+            bytes_accessed=7 * tokens * width * 2,
+        ),
+    )(query, near_k, far_k, near_v, far_v, state, skip.reshape(1, width))
 
 
 def per_device(
@@ -33,7 +70,6 @@
     heads = width // HD
     slot_count = earlier_step_lookup_matrix.shape[1]
     layers_here = section_block_indices[0]
-    scale = 1.0 / math.sqrt(HD)
 
     def pick_patch(stack, patch, axis):
         return lax.dynamic_index_in_dim(stack, patch, axis, keepdims=False)
@@ -64,24 +100,17 @@
             * (1.0 + adaptive_scaling[0, tier])
             + adaptive_shifting[0, tier]
         )
-        query = head_norm(hidden.reshape(tokens, heads, HD)).astype(jnp.bfloat16)
-        fresh_key = head_norm((hidden * tier_query_factor[0, tier]).reshape(tokens, heads, HD)).astype(
-            jnp.bfloat16
+        query = head_norm(hidden.reshape(tokens, heads, HD)).reshape(tokens, width).astype(jnp.bfloat16)
+        fresh_key = (
+            head_norm((hidden * tier_query_factor[0, tier]).reshape(tokens, heads, HD))
+            .reshape(tokens, width)
+            .astype(jnp.bfloat16)
         )
-        fresh_value = hidden.astype(jnp.bfloat16).reshape(tokens, heads, HD)
-        keys = jnp.concatenate([fresh_key, keys_far.reshape(tokens, heads, HD)], axis=0)
-        values = jnp.concatenate([fresh_value, values_far.reshape(tokens, heads, HD)], axis=0)
-        scores = jnp.einsum("phd,nhd->phn", query, keys, preferred_element_type=jnp.float32) * scale
-        weights = jnp.exp(scores)
-        total = jnp.sum(weights, axis=-1)
-        numerator = jnp.einsum(
-            "phn,nhd->phd", weights.astype(jnp.bfloat16), values, preferred_element_type=jnp.float32
+        fresh_value = hidden.astype(jnp.bfloat16)
+        new_state = attend_and_add(
+            query, fresh_key, keys_far, fresh_value, values_far, state, tier_skip_coefficient[0, tier]
         )
-        attended = (numerator / total[..., None]).reshape(tokens, width)
-        new_state = (x + tier_skip_coefficient[0, tier] * attended).astype(jnp.bfloat16)
-        return jnp.where(live, new_state, state), fresh_key.reshape(tokens, width), fresh_value.reshape(
-            tokens, width
-        )
+        return jnp.where(live, new_state, state), fresh_key, fresh_value
 
     def own_rows(state):
         return lax.dynamic_slice_in_dim(state, place * rows, rows, 0)

time: 189 us -> 211 us (1.12)
  Pallas kernels: 0 us -> 24.2 us
  other arithmetic: 19.9 us -> 38.9 us
  matrix products: 13.6 us -> 0 us
  local copies, waits for them, and re-layouts: 40.8 us -> 33.3 us
    mul x2 -> x22, local copies, waits for them, and re-layouts: 3.74 us -> 28.3 us  [the longest x16 17.1 us: head_norm(): values * lax.rsqrt(jnp.mean(values * values, axis=-1, keepdims=True) + EP...]
    pallas_call x0 -> x4, Pallas kernels: none -> 24.2 us  [attend_and_add(): pl.pallas_call(attention_kernel, out_shape=jax.ShapeDtypeStruct((tokens,...]
    dot_general x8 -> x0, matrix products: 13.6 us -> none  [the longest x4 7.99 us: layer(): jnp.einsum('phn,nhd->phd', weights.astype(jnp.bfloat16), values, preferre...]
    reshape x7 -> x0, local copies, waits for them, and re-layouts: 11.5 us -> none  [the longest x3 6.77 us: layer(): attended = (numerator / total[..., None]).reshape(tokens, width)]
    convert_element_type x8 -> x7, other arithmetic: 8.21 us -> 17.8 us  [the longest x4 13.8 us: layer(): fresh_value = hidden.astype(jnp.bfloat16)]
    slice x7 -> x0, local copies, waits for them, and re-layouts: 7.94 us -> none  [the longest x5 6.85 us: per_device(): state, fresh_key, fresh_value = layer(state, tier, far_k[tier], far_v[tier])]
    mul x0 -> x3, other arithmetic: none -> 4.47 us  [head_norm(): values * values]
    squeeze x0 -> x1, other arithmetic: none -> 4.08 us  [per_device(): state, fresh_key, fresh_value = layer(state, tier, far_k[tier], far_v[tier])]
where the time goes in v3:
time: 211 us; the launch traced here: 209 us
  waiting for transfers between devices  90.6 us (43%)
  other arithmetic  38.9 us (18%)
  local copies, waits for them, and re-layouts  33.3 us (16%)
  Pallas kernels  24.2 us (11%)
  between operations  20.1 us (10%)
    all_gather x1, waiting for transfers between devices, per_device(): whole = lax.all_gather(packed, 'ctx', axis=1, tiled=True)  69.8 us
    pallas_call x4, Pallas kernels, attend_and_add(): pl.pallas_call(attention_kernel, out_shape=jax.ShapeDtypeStruct((tokens,...  24.2 us
    ppermute x1, waiting for transfers between devices, per_device(): lax.ppermute(state, 'segment', [(i, i + 1) for i in range(count - 1)])  20.8 us
    mul x16, local copies, waits for them, and re-layouts, head_norm(): values * lax.rsqrt(jnp.mean(values * values, axis=-1, keepdims=True) + EP...  17.1 us
    convert_element_type x4, other arithmetic, layer(): fresh_value = hidden.astype(jnp.bfloat16)  13.8 us
    mul x6, local copies, waits for them, and re-layouts, head_norm(): values * values  11.2 us
    reduce_sum x4, other arithmetic, layer(): jnp.mean(x * x, axis=-1, keepdims=True) + EPSILON  6.08 us
    mul x3, other arithmetic, head_norm(): values * values  4.47 us
  transfers between devices with their start and end apart: 2, of which 2 were waited for; matrix products, arithmetic and copies ran while one was open for 1% of the time, Pallas kernels for 0%

profile of v3, /device:TPU:33, one launch (start us, length us, event | category | flops | bytes accessed | tf_op | source)
XLA Modules:
  0.0 209.3 jit_solution(9871258647385442857)
XLA Ops:
  19.7 69.8 %all-gather.2.cloned.1.call-done = bf16[6,256,1536]{2,1,0:T(8,128)(2,1)} async-done(((bf16[6,8,1536]{2,1,0:T(8,128)(2,1)}), bf16[6,256,1536]{2,1,0:T(8,128)(2,1)}) %all-gather.2.cloned.1.call-update) | async-done | bytes 4718608 | tf_op jit(solution)/shard_map/all_gather | solution.py:89
  89.6 4.1 %slice_bitcast_fusion.1 = (bf16[256,1536]{1,0:T(8,128)(2,1)}, f32[1,256,1536]{2,1,0:T(8,128)S(1)}, bf16[256,1536]{1,0:T(8,128)(2,1)}, bf16[256,1536]{1,0:T(8,128...) fusion(bf16[6,256,1536]{2,1,0:T(8,128)(2,1)} %all-gather.2.cloned.1.call-done), kind=kLoop, calls=%fused_computation.55 | loop fusion | flops 393216 | bytes 9437184 | tf_op jit(solution)/shard_map/squeeze | solution.py:122
  97.1 1.6 copy.13
  98.7 3.5 %fusion.3 = (bf16[256,1536]{1,0:T(8,128)(2,1)}, bf16[256,1536]{1,0:T(8,128)(2,1)}, bf16[256,1536]{1,0:T(8,128)(2,1)}) fusion(f32[1536]{0:T(1024)S(1)} %get-tuple-element.46, f32[1536]{0:T(1024)S(1)} %get-tuple-element.10, f32[256]{0:T(256)S(1)} %add_rsqrt_fusion.11, bf16[6,256,1536]{2,1,0:T(8,128)(2,1)} %all-gather.2.cloned.1.call-done, ...), kind=kLoop, calls=%fused_computation.11 | loop fusion | flops 3932160 | bytes 6310912 | tf_op jit(solution)/shard_map/convert_element_type | solution.py:109
  102.2 6.0 %shard_map.100 = bf16[256,1536]{1,0:T(8,128)(2,1)} custom-call(bf16[256,1536]{1,0:T(8,128)(2,1)} %get-tuple-element.21.q_ref, bf16[256,1536]{1,0:T(8,128)(2,1)} %get-tuple-element.20.kn_ref.kf_ref, bf16[256,1536]{1,0:T(8,128)(2,1)} %get-tuple-element.26.kf_ref, bf16[256,1536]{1,0:T(8,128)(2,1)} %get-tuple-element.19.vn_ref.vf_ref, ...), custom_call_target="tpu_custom_call" | custom-call | flops 1610612736 | bytes 5505024 | tf_op jit(solution)/shard_map/pallas_call | solution.py:39
  108.2 1.7 fusion.9
  111.5 1.9 copy.14
  113.6 1.6 copy.15
  115.3 3.4 %fusion.12 = (bf16[256,1536]{1,0:T(8,128)(2,1)}, bf16[256,1536]{1,0:T(8,128)(2,1)}, f32[256,1536]{1,0:T(8,128)}) fusion(bf16[256,1536]{1,0:T(8,128)(2,1)S(1)} %get-tuple-element.18.x_ref, f32[1536]{0:T(1024)S(1)} %get-tuple-element.47, f32[1536]{0:T(1024)S(1)} %get-tuple-element.9, f32[256]{0:T(256)S(1)} %add_rsqrt_fusion.10, f32[256,1536]{1,0:T(8,128)} %copy.15, ...), kind=kLoop, calls=%fused_computation.20 | loop fusion | flops 3538944 | bytes 5524480 | tf_op jit(solution)/shard_map/convert_element_type | solution.py:109
  118.7 1.9 copy.16
  122.0 1.9 copy.17
  125.2 6.1 %shard_map.101 = bf16[256,1536]{1,0:T(8,128)(2,1)} custom-call(bf16[256,1536]{1,0:T(8,128)(2,1)} %get-tuple-element.35.q_ref, bf16[256,1536]{1,0:T(8,128)(2,1)} %fusion.18.kn_ref.kf_ref, bf16[256,1536]{1,0:T(8,128)(2,1)} %get-tuple-element.24.kf_ref, bf16[256,1536]{1,0:T(8,128)(2,1)} %get-tuple-element.34.vn_ref.vf_ref, ...), custom_call_target="tpu_custom_call" | custom-call | flops 1610612736 | bytes 5505024 | tf_op jit(solution)/shard_map/pallas_call | solution.py:39
  132.5 2.1 %collective-permute-start = (bf16[256,1536]{1,0:T(8,128)(2,1)S(1)}, bf16[256,1536]{1,0:T(8,128)(2,1)S(1)}, u32[]{:S(2)}, u32[]{:S(2)}) collective-permute-start(bf16[256,1536]{1,0:T(8,128)(2,1)S(1)} %broadcast_select_fusion.2), channel_id=1, source_target_pairs={{0,32},{32,64},{64,96},{96,128},{128,160},{160,192},{192,224},{224... | collective-permute-start | bytes 2359304 | tf_op jit(solution)/shard_map/ppermute | solution.py:127
  134.7 20.8 %collective-permute-done = bf16[256,1536]{1,0:T(8,128)(2,1)S(1)} collective-permute-done((bf16[256,1536]{1,0:T(8,128)(2,1)S(1)}, bf16[256,1536]{1,0:T(8,128)(2,1)S(1)}, u32[]{:S(2)}, u32[]{:S(2)}) %collective-permute-start) | collective-permute-done | bytes 786464 | tf_op jit(solution)/shard_map/ppermute | solution.py:127
  158.4 1.9 copy.18
  162.2 3.5 %fusion.23 = (bf16[256,1536]{1,0:T(8,128)(2,1)}, bf16[256,1536]{1,0:T(8,128)(2,1)}, f32[256,1536]{1,0:T(8,128)}) fusion(bf16[256,1536]{1,0:T(8,128)(2,1)S(1)} %get-tuple-element.16.x_ref, f32[256]{0:T(256)S(1)} %add_rsqrt_fusion.9, f32[1536]{0:T(1024)S(1)} %get-tuple-element.46, f32[1536]{0:T(1024)S(1)} %get-tuple-element.10, f32[256,1536]{1,0:T(8,128)} %copy.19, ...), kind=kLoop, calls=%fused_computation.31 | loop fusion | flops 3538944 | bytes 5524480 | tf_op jit(solution)/shard_map/convert_element_type | solution.py:109
  165.7 1.9 copy.20
  169.0 1.9 copy.21
  172.2 6.1 %shard_map.102 = bf16[256,1536]{1,0:T(8,128)(2,1)} custom-call(bf16[256,1536]{1,0:T(8,128)(2,1)} %get-tuple-element.32.q_ref, bf16[256,1536]{1,0:T(8,128)(2,1)} %fusion.29.kn_ref, bf16[256,1536]{1,0:T(8,128)(2,1)} %get-tuple-element.20.kn_ref.kf_ref, bf16[256,1536]{1,0:T(8,128)(2,1)} %get-tuple-element.31.vn_ref, ...), custom_call_target="tpu_custom_call" | custom-call | flops 1610612736 | bytes 5505024 | tf_op jit(solution)/shard_map/pallas_call | solution.py:39
  181.3 1.9 copy.22
  185.0 3.5 %fusion.34 = (bf16[256,1536]{1,0:T(8,128)(2,1)}, bf16[256,1536]{1,0:T(8,128)(2,1)}, f32[256,1536]{1,0:T(8,128)}) fusion(bf16[256,1536]{1,0:T(8,128)(2,1)S(1)} %get-tuple-element.14.x_ref, f32[256]{0:T(256)S(1)} %add_rsqrt_fusion.8, f32[1536]{0:T(1024)S(1)} %get-tuple-element.47, f32[1536]{0:T(1024)S(1)} %get-tuple-element.9, f32[256,1536]{1,0:T(8,128)} %copy.23, ...), kind=kLoop, calls=%fused_computation.42 | loop fusion | flops 3538944 | bytes 5524480 | tf_op jit(solution)/shard_map/convert_element_type | solution.py:109
  188.5 1.9 copy.24
  191.8 1.9 copy.25
  195.0 6.0 %shard_map.103 = bf16[256,1536]{1,0:T(8,128)(2,1)} custom-call(bf16[256,1536]{1,0:T(8,128)(2,1)} %get-tuple-element.29.q_ref, bf16[256,1536]{1,0:T(8,128)(2,1)} %fusion.40.kn_ref, bf16[256,1536]{1,0:T(8,128)(2,1)} %fusion.18.kn_ref.kf_ref, bf16[256,1536]{1,0:T(8,128)(2,1)} %get-tuple-element.28.vn_ref, bf16[256,1536]{1,0:T(8,128)(2,1)} %get-tuple-element.34.vn_ref.vf_ref, ...), custom_call_target="tpu_custom_call" | custom-call | flops 1610612736 | bytes 5505024 | tf_op jit(solution)/shard_map/pallas_call | solution.py:39
  (63 shorter events, 32.4 us)
Async XLA Ops:
  6.5 83.0 %all-gather.2.cloned.1.call-start = ((), (), s32[]{:S(2)}) async-start(), calls=%async_computation | async-start | bytes 4866048 | tf_op jit(solution)/shard_map/all_gather | solution.py:89
  110.0 14.0 %copy-start = (bf16[256,1536]{1,0:T(8,128)(2,1)}, bf16[256,1536]{1,0:T(8,128)(2,1)S(1)}, u32[]{:S(2)}) copy-start(bf16[256,1536]{1,0:T(8,128)(2,1)S(1)} %get-tuple-element.18.x_ref) | copy-start | bytes 2359300
  125.2 6.1 %copy-start.1 = (bf16[256,1536]{1,0:T(8,128)(2,1)S(1)}, bf16[256,1536]{1,0:T(8,128)(2,1)}, u32[]{:S(2)}) copy-start(bf16[256,1536]{1,0:T(8,128)(2,1)} %copy-done) | copy-start | bytes 2359300
  132.5 22.9 %collective-permute-start = (bf16[256,1536]{1,0:T(8,128)(2,1)S(1)}, bf16[256,1536]{1,0:T(8,128)(2,1)S(1)}, u32[]{:S(2)}, u32[]{:S(2)}) collective-permute-start(bf16[256,1536]{1,0:T(8,128)(2,1)S(1)} %broadcast_select_fusion.2), channel_id=1, source_target_pairs={{0,32},{32,64},{64,96},{96,128},{128,160},{160,192},{192,224},{224... | collective-permute-start | bytes 2359304 | tf_op jit(solution)/shard_map/ppermute | solution.py:127
  156.9 13.9 %copy-start.2 = (bf16[256,1536]{1,0:T(8,128)(2,1)}, bf16[256,1536]{1,0:T(8,128)(2,1)S(1)}, u32[]{:S(2)}) copy-start(bf16[256,1536]{1,0:T(8,128)(2,1)S(1)} %get-tuple-element.16.x_ref) | copy-start | bytes 2359300
  172.2 6.1 %copy-start.3 = (bf16[256,1536]{1,0:T(8,128)(2,1)S(1)}, bf16[256,1536]{1,0:T(8,128)(2,1)}, u32[]{:S(2)}) copy-start(bf16[256,1536]{1,0:T(8,128)(2,1)} %copy-done.2) | copy-start | bytes 2359300
  179.8 13.9 %copy-start.4 = (bf16[256,1536]{1,0:T(8,128)(2,1)}, bf16[256,1536]{1,0:T(8,128)(2,1)S(1)}, u32[]{:S(2)}) copy-start(bf16[256,1536]{1,0:T(8,128)(2,1)S(1)} %get-tuple-element.14.x_ref) | copy-start | bytes 2359300
Sparse Core Ops, SparseCore 0:
  16.1 73.4 all-gather.1

commit v4 on v3

--- a/solution.py
+++ b/solution.py
@@ -14,40 +14,60 @@
     return values * lax.rsqrt(jnp.mean(values * values, axis=-1, keepdims=True) + EPSILON)
 
 
-def attention_kernel(q_ref, kn_ref, kf_ref, vn_ref, vf_ref, x_ref, skip_ref, o_ref):
+def layer_kernel(
+    full_ref, x_ref, shift_ref, stretch_ref, factor_ref, skip_ref, kf_ref, vf_ref, o_ref, k_ref, v_ref
+):
     scale = 1.0 / math.sqrt(HD)
     dims = (((1,), (1,)), ((), ()))
-    for j in range(q_ref.shape[1] // HD):
+    whole = full_ref[...].astype(jnp.float32)
+    row_scale = lax.rsqrt(jnp.mean(whole * whole, axis=-1, keepdims=True) + EPSILON)
+    for j in range(x_ref.shape[1] // HD):
         cols = slice(j * HD, (j + 1) * HD)
-        query = q_ref[:, cols]
-        near = lax.dot_general(query, kn_ref[:, cols], dims, preferred_element_type=jnp.float32) * scale
+        x = x_ref[:, cols].astype(jnp.float32)
+        hidden = x * row_scale * (1.0 + stretch_ref[:, cols]) + shift_ref[:, cols]
+        query = head_norm(hidden).astype(jnp.bfloat16)
+        fresh_key = head_norm(hidden * factor_ref[:, cols]).astype(jnp.bfloat16)
+        fresh_value = hidden.astype(jnp.bfloat16)
+        k_ref[:, cols] = fresh_key
+        v_ref[:, cols] = fresh_value
+        near = lax.dot_general(query, fresh_key, dims, preferred_element_type=jnp.float32) * scale
         far = lax.dot_general(query, kf_ref[:, cols], dims, preferred_element_type=jnp.float32) * scale
         near = jnp.exp(near)
         far = jnp.exp(far)
         total = jnp.sum(near, axis=-1, keepdims=True) + jnp.sum(far, axis=-1, keepdims=True)
         numerator = jnp.dot(
-            near.astype(jnp.bfloat16), vn_ref[:, cols], preferred_element_type=jnp.float32
+            near.astype(jnp.bfloat16), fresh_value, preferred_element_type=jnp.float32
         ) + jnp.dot(far.astype(jnp.bfloat16), vf_ref[:, cols], preferred_element_type=jnp.float32)
         attended = numerator / total
-        x = x_ref[:, cols].astype(jnp.float32)
         o_ref[:, cols] = (x + skip_ref[:, cols] * attended).astype(o_ref.dtype)
 
 
-def attend_and_add(query, near_k, far_k, near_v, far_v, state, skip, block=384):
+def fused_layer(state, shift, stretch, factor, skip, far_k, far_v, block=384):
     tokens, width = state.shape
     tile = pl.BlockSpec((tokens, block), lambda i: (0, i))
+    line = pl.BlockSpec((1, block), lambda i: (0, i))
+    out = jax.ShapeDtypeStruct((tokens, width), jnp.bfloat16)
     return pl.pallas_call(
-        attention_kernel,
-        out_shape=jax.ShapeDtypeStruct((tokens, width), jnp.bfloat16),
+        layer_kernel,
+        out_shape=(out, out, out),
         grid=(width // block,),
-        in_specs=[tile] * 6 + [pl.BlockSpec((1, block), lambda i: (0, i))],
-        out_specs=tile,
+        in_specs=[pl.BlockSpec((tokens, width), lambda i: (0, 0)), tile, line, line, line, line, tile, tile],
+        out_specs=(tile, tile, tile),
         cost_estimate=pl.CostEstimate(
             flops=8 * tokens * 2 * tokens * width,
             transcendentals=tokens * 2 * tokens * (width // HD),
             bytes_accessed=7 * tokens * width * 2,
         ),
-    )(query, near_k, far_k, near_v, far_v, state, skip.reshape(1, width))
+    )(
+        state,
+        state,
+        shift.reshape(1, width),
+        stretch.reshape(1, width),
+        factor.reshape(1, width),
+        skip.reshape(1, width),
+        far_k,
+        far_v,
+    )
 
 
 def per_device(
@@ -67,7 +87,6 @@
     patch_count = tile_arrival_permutation.shape[0]
     rows = inbound_activation.shape[1]
     width = inbound_activation.shape[2]
-    heads = width // HD
     slot_count = earlier_step_lookup_matrix.shape[1]
     layers_here = section_block_indices[0]
 
@@ -94,21 +113,14 @@
 
     def layer(state, tier, keys_far, values_far):
         live = layers_here > tier
-        x = state.astype(jnp.float32)
-        hidden = (
-            x * lax.rsqrt(jnp.mean(x * x, axis=-1, keepdims=True) + EPSILON)
-            * (1.0 + adaptive_scaling[0, tier])
-            + adaptive_shifting[0, tier]
-        )
-        query = head_norm(hidden.reshape(tokens, heads, HD)).reshape(tokens, width).astype(jnp.bfloat16)
-        fresh_key = (
-            head_norm((hidden * tier_query_factor[0, tier]).reshape(tokens, heads, HD))
-            .reshape(tokens, width)
-            .astype(jnp.bfloat16)
-        )
-        fresh_value = hidden.astype(jnp.bfloat16)
-        new_state = attend_and_add(
-            query, fresh_key, keys_far, fresh_value, values_far, state, tier_skip_coefficient[0, tier]
+        new_state, fresh_key, fresh_value = fused_layer(
+            state,
+            adaptive_shifting[0, tier],
+            adaptive_scaling[0, tier],
+            tier_query_factor[0, tier],
+            tier_skip_coefficient[0, tier],
+            keys_far,
+            values_far,
         )
         return jnp.where(live, new_state, state), fresh_key, fresh_value
 

time: 211 us -> 162 us (0.77)
  other arithmetic: 38.9 us -> 10.7 us
  local copies, waits for them, and re-layouts: 33.3 us -> 9.21 us
  Pallas kernels: 24.2 us -> 28.2 us
    mul x22 -> x0, local copies, waits for them, and re-layouts: 28.3 us -> none  [the longest x16 17.1 us: head_norm(): values * lax.rsqrt(jnp.mean(values * values, axis=-1, keepdims=True) + EP...]
    convert_element_type x7 -> x0, other arithmetic: 17.8 us -> none  [the longest x4 13.8 us: layer(): fresh_value = hidden.astype(jnp.bfloat16)]
    reduce_sum x11 -> x0, other arithmetic: 7.6 us -> none  [the longest x4 6.08 us: layer(): jnp.mean(x * x, axis=-1, keepdims=True) + EPSILON]
    select_n x1 -> x3, other arithmetic: 1.22 us -> 5.72 us  [layer(): return (jnp.where(live, new_state, state), fresh_key, fresh_value)]
    mul x3 -> x0, other arithmetic: 4.47 us -> none  [head_norm(): values * values]
    squeeze x0 -> x1, local copies, waits for them, and re-layouts: none -> 4.13 us  [per_device(): state, fresh_key, fresh_value = layer(state, tier, far_k[tier], far_v[tier])]
    squeeze x1 -> x0, other arithmetic: 4.08 us -> none  [per_device(): state, fresh_key, fresh_value = layer(state, tier, far_k[tier], far_v[tier])]
    pallas_call x4, Pallas kernels: 24.2 us -> 28.2 us  [fused_layer(): pl.pallas_call(layer_kernel, out_shape=(out, out, out), grid=(width // bl...]
  transfers between devices with their start and end apart: 2 -> 2, of which waited for: 2 -> 2; matrix products, arithmetic and copies ran while one was open for 1% -> 2% of each run, Pallas kernels for 0% -> 0%
where the time goes in v4:
time: 162 us; the launch traced here: 161 us
  waiting for transfers between devices  90.5 us (56%)
  Pallas kernels  28.2 us (17%)
  between operations  19.8 us (12%)
  other arithmetic  10.7 us (7%)
  local copies, waits for them, and re-layouts  9.21 us (6%)
  starting transfers between devices  2.48 us (2%)
    all_gather x1, waiting for transfers between devices, per_device(): whole = lax.all_gather(packed, 'ctx', axis=1, tiled=True)  70.1 us
    pallas_call x4, Pallas kernels, fused_layer(): pl.pallas_call(layer_kernel, out_shape=(out, out, out), grid=(width // bl...  28.2 us
    ppermute x1, waiting for transfers between devices, per_device(): lax.ppermute(state, 'segment', [(i, i + 1) for i in range(count - 1)])  20.4 us
    select_n x3, other arithmetic, layer(): return (jnp.where(live, new_state, state), fresh_key, fresh_value)  5.72 us
    squeeze x1, local copies, waits for them, and re-layouts, per_device(): state, fresh_key, fresh_value = layer(state, tier, far_k[tier], far_v[tier])  4.13 us
  transfers between devices with their start and end apart: 2, of which 2 were waited for; matrix products, arithmetic and copies ran while one was open for 2% of the time, Pallas kernels for 0%

profile of v4, /device:TPU:33, one launch (start us, length us, event | category | flops | bytes accessed | tf_op | source)
XLA Modules:
  0.0 161.0 jit_solution(1255856830049815363)
XLA Ops:
  6.5 0.0 all-gather.2.cloned.1.call-start
  6.5 1.4 fusion.2
  13.7 0.8 dynamic-slice_bitcast_fusion
  14.5 0.8 dynamic-slice_select_fusion.1
  15.3 0.7 pad_maximum_fusion
  15.9 0.0 all-gather.2.cloned.1.call-update
  16.6 1.4 slice_bitcast_fusion.8
  18.0 1.4 slice_bitcast_fusion.6
  19.4 70.1 %all-gather.2.cloned.1.call-done = bf16[6,256,1536]{2,1,0:T(8,128)(2,1)} async-done(((bf16[6,8,1536]{2,1,0:T(8,128)(2,1)}), bf16[6,256,1536]{2,1,0:T(8,128)(2,1)}) %all-gather.2.cloned.1.call-update) | async-done | bytes 4718608 | tf_op jit(solution)/shard_map/all_gather | solution.py:108
  89.5 4.1 %slice_bitcast_fusion.1 = (bf16[256,1536]{1,0:T(8,128)(2,1)}, bf16[256,1536]{1,0:T(8,128)(2,1)}, bf16[256,1536]{1,0:T(8,128)(2,1)}, bf16[256,1536]{1,0:T(8,128)(2,1)}, bf16[256,1536]{1,0:T(8,128)(2,1)}) fusion(bf16[6,256,1536]{2,1,0:T(8,128)(2,1)} %all-gather.2.cloned.1.call-done), kind=kLoop, calls=%fused_computation.2 | loop fusion | bytes 7864320 | tf_op jit(solution)/shard_map/squeeze | solution.py:134
  93.7 7.0 %shard_map.100 = (bf16[256,1536]{1,0:T(8,128)(2,1)}, bf16[256,1536]{1,0:T(8,128)(2,1)}, bf16[256,1536]{1,0:T(8,128)(2,1)}) custom-call(bf16[256,1536]{1,0:T(8,128)(2,1)} %get-tuple-element.25.full_ref.x_ref, bf16[256,1536]{1,0:T(8,128)(2,1)} %get-tuple-element.25.full_ref.x_ref, f32[1,1536]{1,0:T(1,128)} %get-tuple-element.43.shift_ref, ...), custom_call_target="tpu_custom_call" | custom-call | flops 1610612736 | bytes 5505024 | tf_op jit(solution)/shard_map/pallas_call | solution.py:50
  100.7 2.4 %broadcast_select_fusion.1.full_ref.x_ref = bf16[256,1536]{1,0:T(8,128)(2,1)} fusion(bf16[256,1536]{1,0:T(8,128)(2,1)} %get-tuple-element.13, pred[]{:T(512)} %bitcast.1, bf16[6,256,1536]{2,1,0:T(8,128)(2,1)} %all-gather.2.cloned.1.call-done), kind=kLoop, calls=%fused_computation.8 | loop fusion | flops 393216 | bytes 2359297 | tf_op jit(solution)/shard_map/jit(_where)/select_n | solution.py:125
  103.1 7.1 %shard_map.101 = (bf16[256,1536]{1,0:T(8,128)(2,1)}, bf16[256,1536]{1,0:T(8,128)(2,1)}, bf16[256,1536]{1,0:T(8,128)(2,1)}) custom-call(bf16[256,1536]{1,0:T(8,128)(2,1)} %broadcast_select_fusion.1.full_ref.x_ref, bf16[256,1536]{1,0:T(8,128)(2,1)} %broadcast_select_fusion.1.full_ref.x_ref, f32[1,1536]{1,0:T(1,128)} %get-tuple-element.44.shift_ref, ...), custom_call_target="tpu_custom_call" | custom-call | flops 1610612736 | bytes 5505024 | tf_op jit(solution)/shard_map/pallas_call | solution.py:50
  110.1 0.0 copy-done.1
  110.1 1.2 broadcast_select_fusion.2
  111.4 2.5 %collective-permute-start = (bf16[256,1536]{1,0:T(8,128)(2,1)S(1)}, bf16[256,1536]{1,0:T(8,128)(2,1)S(1)}, u32[]{:S(2)}, u32[]{:S(2)}) collective-permute-start(bf16[256,1536]{1,0:T(8,128)(2,1)S(1)} %broadcast_select_fusion.2), channel_id=1, source_target_pairs={{0,32},{32,64},{64,96},{96,128},{128,160},{160,192},{192,224},{224... | collective-permute-start | bytes 2359304 | tf_op jit(solution)/shard_map/ppermute | solution.py:139
  113.9 20.4 %collective-permute-done = bf16[256,1536]{1,0:T(8,128)(2,1)S(1)} collective-permute-done((bf16[256,1536]{1,0:T(8,128)(2,1)S(1)}, bf16[256,1536]{1,0:T(8,128)(2,1)S(1)}, u32[]{:S(2)}, u32[]{:S(2)}) %collective-permute-start) | collective-permute-done | bytes 786464 | tf_op jit(solution)/shard_map/ppermute | solution.py:139
  134.3 2.2 %fusion.full_ref.x_ref = bf16[256,1536]{1,0:T(8,128)(2,1)} fusion(bf16[256,1536]{1,0:T(8,128)(2,1)S(1)} %collective-permute-done, bf16[6,256,1536]{2,1,0:T(8,128)(2,1)} %all-gather.2.cloned.1.call-done, pred[]{:T(512)S(6)} %eq.6), kind=kLoop, calls=%fused_computation.1 | loop fusion | flops 393216 | bytes 2359297 | tf_op jit(solution)/shard_map/jit(_where)/select_n | solution.py:140
  136.4 7.1 %shard_map.102 = (bf16[256,1536]{1,0:T(8,128)(2,1)}, bf16[256,1536]{1,0:T(8,128)(2,1)}, bf16[256,1536]{1,0:T(8,128)(2,1)}) custom-call(bf16[256,1536]{1,0:T(8,128)(2,1)} %fusion.full_ref.x_ref, bf16[256,1536]{1,0:T(8,128)(2,1)} %fusion.full_ref.x_ref, f32[1,1536]{1,0:T(1,128)} %get-tuple-element.43.shift_ref, f32[1,1536]{1,0:T(1,128)} %get-tuple-element.33.stretch_ref, ...), custom_call_target="tpu_custom_call" | custom-call | flops 1610612736 | bytes 5505024 | tf_op jit(solution)/shard_map/pallas_call | solution.py:50
  143.6 0.0 copy-done
  143.6 2.1 %broadcast_select_fusion.full_ref.x_ref = bf16[256,1536]{1,0:T(8,128)(2,1)} fusion(bf16[256,1536]{1,0:T(8,128)(2,1)} %get-tuple-element.17, bf16[256,1536]{1,0:T(8,128)(2,1)S(1)} %copy-done, pred[]{:T(512)} %bitcast.1), kind=kLoop, calls=%fused_computation.7 | loop fusion | flops 393216 | bytes 2359297 | tf_op jit(solution)/shard_map/jit(_where)/select_n | solution.py:125
  145.7 7.1 %shard_map.103 = (bf16[256,1536]{1,0:T(8,128)(2,1)}, bf16[256,1536]{1,0:T(8,128)(2,1)}, bf16[256,1536]{1,0:T(8,128)(2,1)}) custom-call(bf16[256,1536]{1,0:T(8,128)(2,1)} %broadcast_select_fusion.full_ref.x_ref, bf16[256,1536]{1,0:T(8,128)(2,1)} %broadcast_select_fusion.full_ref.x_ref, f32[1,1536]{1,0:T(1,128)} %get-tuple-element.44.shift_ref, ...), custom_call_target="tpu_custom_call" | custom-call | flops 1610612736 | bytes 5505024 | tf_op jit(solution)/shard_map/pallas_call | solution.py:50
  152.8 0.8 fusion.1
  153.5 0.6 maximum_bitcast_fusion
  (3 shorter events, 0.0 us)
Async XLA Ops:
  6.5 83.0 %all-gather.2.cloned.1.call-start = ((), (), s32[]{:S(2)}) async-start(), calls=%async_computation | async-start | bytes 4866048 | tf_op jit(solution)/shard_map/all_gather | solution.py:108
  103.0 7.1 %copy-start.1 = (bf16[256,1536]{1,0:T(8,128)(2,1)S(1)}, bf16[256,1536]{1,0:T(8,128)(2,1)}, u32[]{:S(2)}) copy-start(bf16[256,1536]{1,0:T(8,128)(2,1)} %broadcast_select_fusion.1.full_ref.x_ref) | copy-start | bytes 2359300
  111.4 22.9 %collective-permute-start = (bf16[256,1536]{1,0:T(8,128)(2,1)S(1)}, bf16[256,1536]{1,0:T(8,128)(2,1)S(1)}, u32[]{:S(2)}, u32[]{:S(2)}) collective-permute-start(bf16[256,1536]{1,0:T(8,128)(2,1)S(1)} %broadcast_select_fusion.2), channel_id=1, source_target_pairs={{0,32},{32,64},{64,96},{96,128},{128,160},{160,192},{192,224},{224... | collective-permute-start | bytes 2359304 | tf_op jit(solution)/shard_map/ppermute | solution.py:139
  136.4 7.1 %copy-start = (bf16[256,1536]{1,0:T(8,128)(2,1)S(1)}, bf16[256,1536]{1,0:T(8,128)(2,1)}, u32[]{:S(2)}) copy-start(bf16[256,1536]{1,0:T(8,128)(2,1)} %fusion.full_ref.x_ref) | copy-start | bytes 2359300
Sparse Core Ops, SparseCore 0:
  16.1 73.4 all-gather.1

commit v5 on v4

v5 whole, which is shorter than its diff:
```python
import functools
import math

import jax
import jax.numpy as jnp
from jax import lax
from jax.experimental import pallas as pl
from jax.experimental.pallas import tpu as pltpu
from jax.sharding import PartitionSpec as P

HD = 128
EPSILON = 1e-06


def head_norm(values):
    return values * lax.rsqrt(jnp.mean(values * values, axis=-1, keepdims=True) + EPSILON)


def layer_kernel(flags_ref, *refs, two_sources, keep_kv):
    if two_sources:
        full_ref, x_ref, entry_full_ref, entry_x_ref, *refs = refs
    else:
        full_ref, x_ref, *refs = refs
    shift_ref, stretch_ref, factor_ref, skip_ref, kf_ref, vf_ref, o_ref, *kv_refs = refs
    live = flags_ref[0] > 0
    scale = 1.0 / math.sqrt(HD)
    dims = (((1,), (1,)), ((), ()))
    whole = full_ref[...]
    state = x_ref[...]
    if two_sources:
        use_entry = flags_ref[1] > 0
        whole = jnp.where(use_entry, entry_full_ref[...], whole)
        state = jnp.where(use_entry, entry_x_ref[...], state)
    whole = whole.astype(jnp.float32)
    row_scale = lax.rsqrt(jnp.mean(whole * whole, axis=-1, keepdims=True) + EPSILON)
    for j in range(state.shape[1] // HD):
        cols = slice(j * HD, (j + 1) * HD)
        x_rounded = state[:, cols]
        x = x_rounded.astype(jnp.float32)
        hidden = x * row_scale * (1.0 + stretch_ref[:, cols]) + shift_ref[:, cols]
        query = head_norm(hidden).astype(jnp.bfloat16)
        fresh_key = head_norm(hidden * factor_ref[:, cols]).astype(jnp.bfloat16)
        fresh_value = hidden.astype(jnp.bfloat16)
        if keep_kv:
            kv_refs[0][:, cols] = fresh_key
            kv_refs[1][:, cols] = fresh_value
        near = lax.dot_general(query, fresh_key, dims, preferred_element_type=jnp.float32) * scale
        far = lax.dot_general(query, kf_ref[:, cols], dims, preferred_element_type=jnp.float32) * scale
        near = jnp.exp(near)
        far = jnp.exp(far)
        total = jnp.sum(near, axis=-1, keepdims=True) + jnp.sum(far, axis=-1, keepdims=True)
        numerator = jnp.dot(
            near.astype(jnp.bfloat16), fresh_value, preferred_element_type=jnp.float32
        ) + jnp.dot(far.astype(jnp.bfloat16), vf_ref[:, cols], preferred_element_type=jnp.float32)
        attended = numerator / total
        new_state = (x + skip_ref[:, cols] * attended).astype(o_ref.dtype)
        o_ref[:, cols] = jnp.where(live, new_state, x_rounded)


def fused_layer(flags, source, params, tier, far_k, far_v, entry=None, keep_kv=True, block=384):
    array, slab = source
    _, tokens, width = array.shape

    def slab_specs(slab_index):
        return [
            pl.BlockSpec((None, tokens, width), lambda i, f: (slab_index, 0, 0)),
            pl.BlockSpec((None, tokens, block), lambda i, f: (slab_index, 0, i)),
        ]

    def tile_of(slab_index):
        return pl.BlockSpec((None, tokens, block), lambda i, f: (slab_index, 0, i))

    line = pl.BlockSpec((None, 1, block), lambda i, f: (tier, 0, i))
    in_specs = slab_specs(slab)
    operands = [array, array]
    if entry is not None:
        in_specs += slab_specs(entry[1])
        operands += [entry[0], entry[0]]
    in_specs += [line] * 4 + [tile_of(far_k[1]), tile_of(far_v[1])]
    operands += [p.reshape(p.shape[0], 1, width) for p in params] + [far_k[0], far_v[0]]
    out_tile = pl.BlockSpec((tokens, block), lambda i, f: (0, i))
    out = jax.ShapeDtypeStruct((tokens, width), jnp.bfloat16)
    count = 3 if keep_kv else 1
    results = pl.pallas_call(
        functools.partial(layer_kernel, two_sources=entry is not None, keep_kv=keep_kv),
        out_shape=(out,) * count,
        grid_spec=pltpu.PrefetchScalarGridSpec(
            num_scalar_prefetch=1,
            grid=(width // block,),
            in_specs=in_specs,
            out_specs=(out_tile,) * count,
        ),
        cost_estimate=pl.CostEstimate(
            flops=8 * tokens * 2 * tokens * width,
            transcendentals=tokens * 2 * tokens * (width // HD),
            bytes_accessed=(4 + 2 * count) * tokens * width,
        ),
    )(flags, *operands)
    return results if keep_kv else (results[0], None, None)


def per_device(
    perturbed_frame_activation,
    inbound_activation,
    section_block_indices,
    tile_arrival_permutation,
    adaptive_shifting,
    adaptive_scaling,
    tier_query_factor,
    tier_skip_coefficient,
    earlier_step_lookup_matrix,
    earlier_step_content_matrix,
):
    segment = lax.axis_index("segment")
    place = lax.axis_index("ctx")
    patch_count = tile_arrival_permutation.shape[0]
    rows = inbound_activation.shape[1]
    width = inbound_activation.shape[2]
    slot_count = earlier_step_lookup_matrix.shape[1]
    layers_here = section_block_indices[0]

    def pick_patch(stack, patch, axis):
        return lax.dynamic_index_in_dim(stack, patch, axis, keepdims=False)

    first_rows = jnp.where(
        segment == 0,
        pick_patch(perturbed_frame_activation, tile_arrival_permutation[0], 0),
        inbound_activation[0],
    )
    entry_rows = [first_rows[None]]
    for turn in range(1, patch_count):
        entry_rows.append(pick_patch(perturbed_frame_activation, tile_arrival_permutation[turn], 0)[None])
    other_patch = tile_arrival_permutation[jnp.mod(1 - segment, patch_count)]
    far_k = pick_patch(earlier_step_lookup_matrix[0], other_patch, 1)
    far_v = pick_patch(earlier_step_content_matrix[0], other_patch, 1)
    packed = jnp.concatenate(entry_rows + [far_k, far_v], axis=0)
    whole = lax.all_gather(packed, "ctx", axis=1, tiled=True)
    params = [
        adaptive_shifting[0],
        adaptive_scaling[0],
        tier_query_factor[0],
        tier_skip_coefficient[0],
    ]
    first_segment = (segment == 0).astype(jnp.int32)

    def flags(tier):
        return jnp.stack([(layers_here > tier).astype(jnp.int32), first_segment])

    def own_rows(state):
        return lax.dynamic_slice_in_dim(state, place * rows, rows, 0)

    outcomes = []
    source = (whole, 0)
    turn_zero_kv = []
    for tier in range(slot_count):
        state, fresh_key, fresh_value = fused_layer(
            flags(tier),
            source,
            params,
            tier,
            (whole, patch_count + tier),
            (whole, patch_count + slot_count + tier),
        )
        source = (state[None], 0)
        turn_zero_kv.append(((fresh_key[None], 0), (fresh_value[None], 0)))
    outcomes.append(own_rows(state))
    count = lax.axis_size("segment")
    for turn in range(1, patch_count):
        arrived = lax.ppermute(state, "segment", [(i, i + 1) for i in range(count - 1)])
        source = (arrived[None], 0)
        entry = (whole, turn)
        for tier in range(slot_count):
            state, _, _ = fused_layer(
                flags(tier), source, params, tier, *turn_zero_kv[tier], entry=entry, keep_kv=False
            )
            source = (state[None], 0)
            entry = None
        outcomes.append(own_rows(state))
    return jnp.stack(outcomes)[None]


def solution(mesh):
    return jax.shard_map(
        per_device,
        mesh=mesh,
        in_specs=(
            P(None, "ctx", None),
            P("segment", "ctx", None),
            P("segment"),
            P(),
            P("segment", None, None),
            P("segment", None, None),
            P("segment", None, None),
            P("segment", None, None),
            P("segment", None, None, "ctx", None),
            P("segment", None, None, "ctx", None),
        ),
        out_specs=P("segment", None, "ctx", None),
        check_vma=False,
    )
```

time: 162 us -> 155 us (0.957)
  other arithmetic: 10.7 us -> 2.73 us
  waiting for transfers between devices: 90.5 us -> 86.9 us
  Pallas kernels: 28.2 us -> 31.3 us
    select_n x4 -> x0, other arithmetic: 7.89 us -> none  [the longest x3 5.72 us: layer(): return (jnp.where(live, new_state, state), fresh_key, fresh_value)]
    squeeze x1 -> x0, local copies, waits for them, and re-layouts: 4.13 us -> none  [per_device(): state, fresh_key, fresh_value = layer(state, tier, far_k[tier], far_v[tier])]
    all_gather x1, waiting for transfers between devices: 70.1 us -> 67 us  [per_device(): whole = lax.all_gather(packed, 'ctx', axis=1, tiled=True)]
    pallas_call x4, Pallas kernels: 28.2 us -> 31.3 us  [fused_layer(): pl.pallas_call(functools.partial(layer_kernel, two_sources=entry is not N...]
    another operation x2 -> x4, local copies, waits for them, and re-layouts: 2.82 us -> 5.25 us  [fused_layer(): p.reshape(p.shape[0], 1, width)]
  transfers between devices with their start and end apart: 2 -> 2, of which waited for: 2 -> 2; matrix products, arithmetic and copies ran while one was open for 2% -> 4% of each run, Pallas kernels for 0% -> 0%
where the time goes in v5:
time: 155 us; the launch traced here: 153 us
  waiting for transfers between devices  86.9 us (56%)
  Pallas kernels  31.3 us (20%)
  between operations  19.8 us (13%)
  local copies, waits for them, and re-layouts  9.97 us (6%)
  other arithmetic  2.73 us (2%)
  starting transfers between devices  2.48 us (2%)
    all_gather x1, waiting for transfers between devices, per_device(): whole = lax.all_gather(packed, 'ctx', axis=1, tiled=True)  67 us
    pallas_call x4, Pallas kernels, fused_layer(): pl.pallas_call(functools.partial(layer_kernel, two_sources=entry is not N...  31.3 us
    ppermute x1, waiting for transfers between devices, per_device(): lax.ppermute(state, 'segment', [(i, i + 1) for i in range(count - 1)])  19.9 us
    another operation x4, local copies, waits for them, and re-layouts, fused_layer(): p.reshape(p.shape[0], 1, width)  5.25 us
  transfers between devices with their start and end apart: 2, of which 2 were waited for; matrix products, arithmetic and copies ran while one was open for 4% of the time, Pallas kernels for 0%

profile of v5, /device:TPU:33, one launch (start us, length us, event | category | flops | bytes accessed | tf_op | source)
XLA Modules:
  0.0 153.1 jit_solution(14402103681862935980)
XLA Ops:
  6.5 0.0 all-gather.2.cloned.1.call-start
  6.5 1.4 fusion
  13.7 0.8 dynamic-slice_bitcast_fusion
  14.5 0.8 dynamic-slice_select_fusion
  15.3 0.7 pad_maximum_fusion
  16.0 0.0 all-gather.2.cloned.1.call-update
  16.6 1.3 reshape_squeeze.8.refs_2_.refs_4_
  18.0 1.3 reshape_squeeze.9.refs_3_.refs_5_
  19.3 1.3 reshape_squeeze.10.refs_4_.refs_6_
  20.6 1.3 reshape_squeeze.11.refs_5_.refs_7_
  21.9 0.6 pad_add_fusion
  22.5 67.0 %all-gather.2.cloned.1.call-done.refs_0_.refs_1_.refs_6_.refs_7_.refs_2_.refs_3_ = bf16[6,256,1536]{2,1,0:T(8,128)(2,1)} async-done(((bf16[6,8,1536]{2,1,0:T(8,128)(2,1)}), bf16[6,256,1536]{2,1,0:T(8,128)(2,1)}) %all-gather.2.cloned.1.call-update) | async-done | bytes 4718608 | tf_op jit(solution)/shard_map/all_gather | solution.py:137
  89.6 7.7 %shard_map.100 = (bf16[256,1536]{1,0:T(8,128)(2,1)}, bf16[256,1536]{1,0:T(8,128)(2,1)}, bf16[256,1536]{1,0:T(8,128)(2,1)}) custom-call(s32[2]{0:T(128)} %get-tuple-element.23.flags_ref, bf16[6,256,1536]{2,1,0:T(8,128)(2,1)} %all-gather.2.cloned.1.call-done.refs_0_.refs_1_.refs_6_.refs_7_.refs_2_.refs_3_, ...), custom_call_target="tpu_custom_call" | custom-call | flops 1610612736 | bytes 3932160 | tf_op jit(solution)/shard_map/pallas_call | solution.py:84
  97.3 7.7 %shard_map.101 = (bf16[256,1536]{1,0:T(8,128)(2,1)}, bf16[256,1536]{1,0:T(8,128)(2,1)}, bf16[256,1536]{1,0:T(8,128)(2,1)}) custom-call(s32[2]{0:T(128)} %get-tuple-element.22.flags_ref, bf16[1,256,1536]{2,1,0:T(8,128)(2,1)} %bitcast.23, bf16[1,256,1536]{2,1,0:T(8,128)(2,1)} %bitcast.24, f32[2,1,1536]{2,1,0:T(1,128)} %reshape_squeeze.8.refs_2_.refs_4_, ...), custom_call_target="tpu_custom_call" | custom-call | flops 1610612736 | bytes 3932160 | tf_op jit(solution)/shard_map/pallas_call | solution.py:84
  105.0 2.5 %collective-permute-start = (bf16[256,1536]{1,0:T(8,128)(2,1)}, bf16[256,1536]{1,0:T(8,128)(2,1)S(1)}, u32[]{:S(2)}, u32[]{:S(2)}) collective-permute-start(bf16[256,1536]{1,0:T(8,128)(2,1)} %get-tuple-element.12), channel_id=1, source_target_pairs={{0,32},{32,64},{64,96},{96,128},{128,160},{160,192},{192,224},{224... | collective-permute-start | bytes 2359304 | tf_op jit(solution)/shard_map/ppermute | solution.py:169
  107.5 0.7 dynamic-slice_bitcast_fusion.3
  108.3 19.9 %collective-permute-done = bf16[256,1536]{1,0:T(8,128)(2,1)S(1)} collective-permute-done((bf16[256,1536]{1,0:T(8,128)(2,1)}, bf16[256,1536]{1,0:T(8,128)(2,1)S(1)}, u32[]{:S(2)}, u32[]{:S(2)}) %collective-permute-start) | collective-permute-done | bytes 786464 | tf_op jit(solution)/shard_map/ppermute | solution.py:169
  128.1 0.0 copy-start
  128.1 1.0 copy-done
  129.1 8.1 %shard_map.102 = bf16[256,1536]{1,0:T(8,128)(2,1)} custom-call(s32[2]{0:T(128)} %get-tuple-element.23.flags_ref, bf16[1,256,1536]{2,1,0:T(8,128)(2,1)} %bitcast.21, bf16[1,256,1536]{2,1,0:T(8,128)(2,1)} %bitcast.22, bf16[6,256,1536]{2,1,0:T(8,128)(2,1)} %all-gather.2.cloned.1.call-done.refs_0_.refs_1_.refs_6_.refs_7_.refs_2_.refs_3_, ...), custom_call_target="tpu_custom_call" | custom-call | flops 1610612736 | bytes 2359296 | tf_op jit(solution)/shard_map/pallas_call | solution.py:84
  137.2 7.7 %shard_map.103 = bf16[256,1536]{1,0:T(8,128)(2,1)} custom-call(s32[2]{0:T(128)} %get-tuple-element.22.flags_ref, bf16[1,256,1536]{2,1,0:T(8,128)(2,1)} %bitcast.27, bf16[1,256,1536]{2,1,0:T(8,128)(2,1)} %bitcast.28, f32[2,1,1536]{2,1,0:T(1,128)} %reshape_squeeze.8.refs_2_.refs_4_, f32[2,1,1536]{2,1,0:T(1,128)} %reshape_squeeze.9.refs_3_.refs_5_, ...), custom_call_target="tpu_custom_call" | custom-call | flops 1610612736 | bytes 2359296 | tf_op jit(solution)/shard_map/pallas_call | solution.py:84
  144.9 0.7 dynamic-slice_bitcast_fusion.2
  145.7 0.6 maximum_bitcast_fusion
Async XLA Ops:
  6.5 83.0 %all-gather.2.cloned.1.call-start = ((), (), s32[]{:S(2)}) async-start(), calls=%async_computation | async-start | bytes 4866048 | tf_op jit(solution)/shard_map/all_gather | solution.py:137
  105.0 23.1 %collective-permute-start = (bf16[256,1536]{1,0:T(8,128)(2,1)}, bf16[256,1536]{1,0:T(8,128)(2,1)S(1)}, u32[]{:S(2)}, u32[]{:S(2)}) collective-permute-start(bf16[256,1536]{1,0:T(8,128)(2,1)} %get-tuple-element.12), channel_id=1, source_target_pairs={{0,32},{32,64},{64,96},{96,128},{128,160},{160,192},{192,224},{224... | collective-permute-start | bytes 2359304 | tf_op jit(solution)/shard_map/ppermute | solution.py:169
  128.1 1.0 copy-start
Sparse Core Ops, SparseCore 0:
  16.1 73.4 all-gather.1

commit v6 on v5

--- a/solution.py
+++ b/solution.py
@@ -57,7 +57,7 @@
         o_ref[:, cols] = jnp.where(live, new_state, x_rounded)
 
 
-def fused_layer(flags, source, params, tier, far_k, far_v, entry=None, keep_kv=True, block=384):
+def fused_layer(flags, source, params, tier, far_k, far_v, entry=None, keep_kv=True, block=1536):
     array, slab = source
     _, tokens, width = array.shape
 

time: 155 us -> 151 us (0.974)
  Pallas kernels: 31.3 us -> 28.1 us
    pallas_call x4, Pallas kernels: 31.3 us -> 28.1 us  [fused_layer(): pl.pallas_call(functools.partial(layer_kernel, two_sources=entry is not N...]
where the time goes in v6:
time: 151 us; the launch traced here: 150 us
  waiting for transfers between devices  86.7 us (57%)
  Pallas kernels  28.1 us (19%)
  between operations  19.8 us (13%)
  local copies, waits for them, and re-layouts  9.96 us (7%)
  other arithmetic  2.73 us (2%)
  starting transfers between devices  2.66 us (2%)
    all_gather x1, waiting for transfers between devices, per_device(): whole = lax.all_gather(packed, 'ctx', axis=1, tiled=True)  67 us
    pallas_call x4, Pallas kernels, fused_layer(): pl.pallas_call(functools.partial(layer_kernel, two_sources=entry is not N...  28.1 us
    ppermute x1, waiting for transfers between devices, per_device(): lax.ppermute(state, 'segment', [(i, i + 1) for i in range(count - 1)])  19.7 us
    another operation x4, local copies, waits for them, and re-layouts, fused_layer(): p.reshape(p.shape[0], 1, width)  5.25 us
  transfers between devices with their start and end apart: 2, of which 2 were waited for; matrix products, arithmetic and copies ran while one was open for 4% of the time, Pallas kernels for 0%

profile of v6, /device:TPU:33, one launch (start us, length us, event | category | flops | bytes accessed | tf_op | source)
XLA Modules:
  0.0 150.0 jit_solution(7613774322548487696)
XLA Ops:
  6.5 0.0 all-gather.2.cloned.1.call-start
  6.5 1.4 fusion
  13.7 0.8 dynamic-slice_bitcast_fusion
  14.5 0.8 dynamic-slice_select_fusion
  15.3 0.7 pad_maximum_fusion
  16.0 0.0 all-gather.2.cloned.1.call-update
  16.6 1.3 reshape_squeeze.8.refs_2_.refs_4_
  18.0 1.3 reshape_squeeze.9.refs_3_.refs_5_
  19.3 1.3 reshape_squeeze.10.refs_4_.refs_6_
  20.6 1.3 reshape_squeeze.11.refs_5_.refs_7_
  21.9 0.6 pad_add_fusion
  22.5 67.0 %all-gather.2.cloned.1.call-done.refs_0_.refs_1_.refs_6_.refs_7_.refs_2_.refs_3_ = bf16[6,256,1536]{2,1,0:T(8,128)(2,1)} async-done(((bf16[6,8,1536]{2,1,0:T(8,128)(2,1)}), bf16[6,256,1536]{2,1,0:T(8,128)(2,1)}) %all-gather.2.cloned.1.call-update) | async-done | bytes 4718608 | tf_op jit(solution)/shard_map/all_gather | solution.py:137
  89.6 6.9 %shard_map.100 = (bf16[256,1536]{1,0:T(8,128)(2,1)}, bf16[256,1536]{1,0:T(8,128)(2,1)}, bf16[256,1536]{1,0:T(8,128)(2,1)}) custom-call(s32[2]{0:T(128)} %get-tuple-element.23.flags_ref, bf16[6,256,1536]{2,1,0:T(8,128)(2,1)} %all-gather.2.cloned.1.call-done.refs_0_.refs_1_.refs_6_.refs_7_.refs_2_.refs_3_, ...), custom_call_target="tpu_custom_call" | custom-call | flops 1610612736 | bytes 3932160 | tf_op jit(solution)/shard_map/pallas_call | solution.py:84
  96.5 7.0 %shard_map.101 = (bf16[256,1536]{1,0:T(8,128)(2,1)}, bf16[256,1536]{1,0:T(8,128)(2,1)}, bf16[256,1536]{1,0:T(8,128)(2,1)}) custom-call(s32[2]{0:T(128)} %get-tuple-element.22.flags_ref, bf16[1,256,1536]{2,1,0:T(8,128)(2,1)} %bitcast.23, bf16[1,256,1536]{2,1,0:T(8,128)(2,1)} %bitcast.24, f32[2,1,1536]{2,1,0:T(1,128)} %reshape_squeeze.8.refs_2_.refs_4_, ...), custom_call_target="tpu_custom_call" | custom-call | flops 1610612736 | bytes 3932160 | tf_op jit(solution)/shard_map/pallas_call | solution.py:84
  103.5 2.7 %collective-permute-start = (bf16[256,1536]{1,0:T(8,128)(2,1)}, bf16[256,1536]{1,0:T(8,128)(2,1)S(1)}, u32[]{:S(2)}, u32[]{:S(2)}) collective-permute-start(bf16[256,1536]{1,0:T(8,128)(2,1)} %get-tuple-element.12), channel_id=1, source_target_pairs={{0,32},{32,64},{64,96},{96,128},{128,160},{160,192},{192,224},{224... | collective-permute-start | bytes 2359304 | tf_op jit(solution)/shard_map/ppermute | solution.py:169
  106.2 0.7 dynamic-slice_bitcast_fusion.3
  106.9 19.7 %collective-permute-done = bf16[256,1536]{1,0:T(8,128)(2,1)S(1)} collective-permute-done((bf16[256,1536]{1,0:T(8,128)(2,1)}, bf16[256,1536]{1,0:T(8,128)(2,1)S(1)}, u32[]{:S(2)}, u32[]{:S(2)}) %collective-permute-start) | collective-permute-done | bytes 786464 | tf_op jit(solution)/shard_map/ppermute | solution.py:169
  126.6 0.0 copy-start
  126.6 1.0 copy-done
  127.6 7.4 %shard_map.102 = bf16[256,1536]{1,0:T(8,128)(2,1)} custom-call(s32[2]{0:T(128)} %get-tuple-element.23.flags_ref, bf16[1,256,1536]{2,1,0:T(8,128)(2,1)} %bitcast.21, bf16[1,256,1536]{2,1,0:T(8,128)(2,1)} %bitcast.22, bf16[6,256,1536]{2,1,0:T(8,128)(2,1)} %all-gather.2.cloned.1.call-done.refs_0_.refs_1_.refs_6_.refs_7_.refs_2_.refs_3_, ...), custom_call_target="tpu_custom_call" | custom-call | flops 1610612736 | bytes 2359296 | tf_op jit(solution)/shard_map/pallas_call | solution.py:84
  135.0 6.8 %shard_map.103 = bf16[256,1536]{1,0:T(8,128)(2,1)} custom-call(s32[2]{0:T(128)} %get-tuple-element.22.flags_ref, bf16[1,256,1536]{2,1,0:T(8,128)(2,1)} %bitcast.27, bf16[1,256,1536]{2,1,0:T(8,128)(2,1)} %bitcast.28, f32[2,1,1536]{2,1,0:T(1,128)} %reshape_squeeze.8.refs_2_.refs_4_, f32[2,1,1536]{2,1,0:T(1,128)} %reshape_squeeze.9.refs_3_.refs_5_, ...), custom_call_target="tpu_custom_call" | custom-call | flops 1610612736 | bytes 2359296 | tf_op jit(solution)/shard_map/pallas_call | solution.py:84
  141.8 0.7 dynamic-slice_bitcast_fusion.2
  142.5 0.6 maximum_bitcast_fusion
Async XLA Ops:
  6.5 83.0 %all-gather.2.cloned.1.call-start = ((), (), s32[]{:S(2)}) async-start(), calls=%async_computation | async-start | bytes 4866048 | tf_op jit(solution)/shard_map/all_gather | solution.py:137
  103.5 23.1 %collective-permute-start = (bf16[256,1536]{1,0:T(8,128)(2,1)}, bf16[256,1536]{1,0:T(8,128)(2,1)S(1)}, u32[]{:S(2)}, u32[]{:S(2)}) collective-permute-start(bf16[256,1536]{1,0:T(8,128)(2,1)} %get-tuple-element.12), channel_id=1, source_target_pairs={{0,32},{32,64},{64,96},{96,128},{128,160},{160,192},{192,224},{224... | collective-permute-start | bytes 2359304 | tf_op jit(solution)/shard_map/ppermute | solution.py:169
  126.6 1.0 copy-start
Sparse Core Ops, SparseCore 0:
  16.1 73.4 all-gather.1

commit v7 on v6

--- a/solution.py
+++ b/solution.py
@@ -166,7 +166,17 @@
     outcomes.append(own_rows(state))
     count = lax.axis_size("segment")
     for turn in range(1, patch_count):
-        arrived = lax.ppermute(state, "segment", [(i, i + 1) for i in range(count - 1)])
+        core = jnp.mod(place, 2)
+        half = state.shape[0] // 2
+        sent = lax.dynamic_slice_in_dim(state, core * half, half, 0)
+        got = lax.ppermute(sent, "segment", [(i, i + 1) for i in range(count - 1)])
+        ctx_count = lax.axis_size("ctx")
+        swapped = lax.ppermute(got, "ctx", [(c, c ^ 1) for c in range(ctx_count)])
+        arrived = jnp.where(
+            core == 0,
+            jnp.concatenate([got, swapped], axis=0),
+            jnp.concatenate([swapped, got], axis=0),
+        )
         source = (arrived[None], 0)
         entry = (whole, turn)
         for tier in range(slot_count):

time: 151 us -> 148 us (0.980)
  waiting for transfers between devices: 86.7 us -> 79.4 us
  starting transfers between devices: 2.66 us -> 5.63 us
    ppermute x1 -> x2, waiting for transfers between devices: 19.7 us -> 12.4 us  [the longest x1 12 us: per_device(): got = lax.ppermute(sent, 'segment', [(i, i + 1) for i in range(count - 1)])]
    ppermute x1 -> x2, starting transfers between devices: 2.66 us -> 5.62 us  [the longest x1 3.14 us: per_device(): swapped = lax.ppermute(got, 'ctx', [(c, c ^ 1) for c in range(ctx_count)])]
  transfers between devices with their start and end apart: 2 -> 3, of which waited for: 2 -> 3; matrix products, arithmetic and copies ran while one was open for 4% -> 5% of each run, Pallas kernels for 0% -> 0%
where the time goes in v7:
time: 148 us; the launch traced here: 147 us
  waiting for transfers between devices  79.4 us (54%)
  Pallas kernels  28.1 us (19%)
  between operations  19.8 us (13%)
  local copies, waits for them, and re-layouts  10 us (7%)
  starting transfers between devices  5.63 us (4%)
  other arithmetic  3.88 us (3%)
    all_gather x1, waiting for transfers between devices, per_device(): whole = lax.all_gather(packed, 'ctx', axis=1, tiled=True)  67 us
    pallas_call x4, Pallas kernels, fused_layer(): pl.pallas_call(functools.partial(layer_kernel, two_sources=entry is not N...  28.1 us
    ppermute x1, waiting for transfers between devices, per_device(): got = lax.ppermute(sent, 'segment', [(i, i + 1) for i in range(count - 1)])  12 us
    another operation x4, local copies, waits for them, and re-layouts, fused_layer(): p.reshape(p.shape[0], 1, width)  5.25 us
    ppermute x1, starting transfers between devices, per_device(): swapped = lax.ppermute(got, 'ctx', [(c, c ^ 1) for c in range(ctx_count)])  3.14 us
  transfers between devices with their start and end apart: 3, of which 3 were waited for; matrix products, arithmetic and copies ran while one was open for 5% of the time, Pallas kernels for 0%

profile of v7, /device:TPU:33, one launch (start us, length us, event | category | flops | bytes accessed | tf_op | source)
XLA Modules:
  0.0 146.9 jit_solution(191821523777385160)
XLA Ops:
  6.5 1.4 fusion
  13.7 0.8 dynamic-slice_bitcast_fusion
  14.5 0.8 dynamic-slice_select_fusion
  15.3 0.7 pad_maximum_fusion
  16.0 0.0 all-gather.2.cloned.1.call-update
  16.7 1.3 reshape_squeeze.8.refs_2_.refs_4_
  18.0 1.3 reshape_squeeze.9.refs_3_.refs_5_
  19.3 1.3 reshape_squeeze.10.refs_4_.refs_6_
  20.6 1.3 reshape_squeeze.11.refs_5_.refs_7_
  21.9 0.6 pad_add_fusion
  22.5 67.0 %all-gather.2.cloned.1.call-done.refs_0_.refs_1_.refs_6_.refs_7_.refs_2_.refs_3_ = bf16[6,256,1536]{2,1,0:T(8,128)(2,1)} async-done(((bf16[6,8,1536]{2,1,0:T(8,128)(2,1)}), bf16[6,256,1536]{2,1,0:T(8,128)(2,1)}) %all-gather.2.cloned.1.call-update) | async-done | bytes 4718608 | tf_op jit(solution)/shard_map/all_gather | solution.py:137
  89.6 6.9 %shard_map.100 = (bf16[256,1536]{1,0:T(8,128)(2,1)}, bf16[256,1536]{1,0:T(8,128)(2,1)}, bf16[256,1536]{1,0:T(8,128)(2,1)}) custom-call(s32[2]{0:T(128)} %get-tuple-element.23.flags_ref, bf16[6,256,1536]{2,1,0:T(8,128)(2,1)} %all-gather.2.cloned.1.call-done.refs_0_.refs_1_.refs_6_.refs_7_.refs_2_.refs_3_, ...), custom_call_target="tpu_custom_call" | custom-call | flops 1610612736 | bytes 3932160 | tf_op jit(solution)/shard_map/pallas_call | solution.py:84
  96.5 7.0 %shard_map.101 = (bf16[256,1536]{1,0:T(8,128)(2,1)}, bf16[256,1536]{1,0:T(8,128)(2,1)}, bf16[256,1536]{1,0:T(8,128)(2,1)}) custom-call(s32[2]{0:T(128)} %get-tuple-element.22.flags_ref, bf16[1,256,1536]{2,1,0:T(8,128)(2,1)} %bitcast.22, bf16[1,256,1536]{2,1,0:T(8,128)(2,1)} %bitcast.23, f32[2,1,1536]{2,1,0:T(1,128)} %reshape_squeeze.8.refs_2_.refs_4_, ...), custom_call_target="tpu_custom_call" | custom-call | flops 1610612736 | bytes 3932160 | tf_op jit(solution)/shard_map/pallas_call | solution.py:84
  103.5 1.0 constant_dynamic-slice_fusion
  104.5 2.5 %collective-permute-start = (bf16[128,1536]{1,0:T(8,128)(2,1)S(1)}, bf16[128,1536]{1,0:T(8,128)(2,1)S(1)}, u32[]{:S(2)}, u32[]{:S(2)}) collective-permute-start(bf16[128,1536]{1,0:T(8,128)(2,1)S(1)} %constant_dynamic-slice_fusion), channel_id=1, source_target_pairs={{0,32},{32,64},{64,96},{96,128},{128,160},{160,192},{192,224},{224... | collective-permute-start | bytes 1179656 | tf_op jit(solution)/shard_map/ppermute | solution.py:172
  107.0 12.0 %collective-permute-done = bf16[128,1536]{1,0:T(8,128)(2,1)S(1)} collective-permute-done((bf16[128,1536]{1,0:T(8,128)(2,1)S(1)}, bf16[128,1536]{1,0:T(8,128)(2,1)S(1)}, u32[]{:S(2)}, u32[]{:S(2)}) %collective-permute-start) | collective-permute-done | bytes 393248 | tf_op jit(solution)/shard_map/ppermute | solution.py:172
  119.0 3.1 %collective-permute-start.1 = (bf16[128,1536]{1,0:T(8,128)(2,1)S(1)}, bf16[128,1536]{1,0:T(8,128)(2,1)S(1)}, u32[]{:S(2)}, u32[]{:S(2)}) collective-permute-start(bf16[128,1536]{1,0:T(8,128)(2,1)S(1)} %collective-permute-done), channel_id=1, source_target_pairs={{0,1},{1,0},{2,3},{3,2},{4,5},{5,4},{6,7},{7,6},{8,9},{9,8},{10,11... | collective-permute-start | bytes 1179656 | tf_op jit(solution)/shard_map/ppermute | solution.py:174
  122.1 0.7 dynamic-slice_bitcast_fusion.3
  122.9 0.4 collective-permute-done.1
  123.3 1.1 maximum_select_fusion.refs_0_.refs_1_
  124.4 7.4 %shard_map.102 = bf16[256,1536]{1,0:T(8,128)(2,1)} custom-call(s32[2]{0:T(128)} %get-tuple-element.23.flags_ref, bf16[1,256,1536]{2,1,0:T(8,128)(2,1)} %maximum_select_fusion.refs_0_.refs_1_, bf16[1,256,1536]{2,1,0:T(8,128)(2,1)} %maximum_select_fusion.refs_0_.refs_1_, ...), custom_call_target="tpu_custom_call" | custom-call | flops 1610612736 | bytes 2359296 | tf_op jit(solution)/shard_map/pallas_call | solution.py:84
  131.8 6.8 %shard_map.103 = bf16[256,1536]{1,0:T(8,128)(2,1)} custom-call(s32[2]{0:T(128)} %get-tuple-element.22.flags_ref, bf16[1,256,1536]{2,1,0:T(8,128)(2,1)} %bitcast.26, bf16[1,256,1536]{2,1,0:T(8,128)(2,1)} %bitcast.27, f32[2,1,1536]{2,1,0:T(1,128)} %reshape_squeeze.8.refs_2_.refs_4_, f32[2,1,1536]{2,1,0:T(1,128)} %reshape_squeeze.9.refs_3_.refs_5_, ...), custom_call_target="tpu_custom_call" | custom-call | flops 1610612736 | bytes 2359296 | tf_op jit(solution)/shard_map/pallas_call | solution.py:84
  138.6 0.7 dynamic-slice_bitcast_fusion.2
  139.4 0.6 maximum_bitcast_fusion
  (1 shorter events, 0.0 us)
Async XLA Ops:
  6.5 83.0 %all-gather.2.cloned.1.call-start = ((), (), s32[]{:S(2)}) async-start(), calls=%async_computation | async-start | bytes 4866048 | tf_op jit(solution)/shard_map/all_gather | solution.py:137
  104.5 14.5 %collective-permute-start = (bf16[128,1536]{1,0:T(8,128)(2,1)S(1)}, bf16[128,1536]{1,0:T(8,128)(2,1)S(1)}, u32[]{:S(2)}, u32[]{:S(2)}) collective-permute-start(bf16[128,1536]{1,0:T(8,128)(2,1)S(1)} %constant_dynamic-slice_fusion), channel_id=1, source_target_pairs={{0,32},{32,64},{64,96},{96,128},{128,160},{160,192},{192,224},{224... | collective-permute-start | bytes 1179656 | tf_op jit(solution)/shard_map/ppermute | solution.py:172
  119.0 4.3 %collective-permute-start.1 = (bf16[128,1536]{1,0:T(8,128)(2,1)S(1)}, bf16[128,1536]{1,0:T(8,128)(2,1)S(1)}, u32[]{:S(2)}, u32[]{:S(2)}) collective-permute-start(bf16[128,1536]{1,0:T(8,128)(2,1)S(1)} %collective-permute-done), channel_id=1, source_target_pairs={{0,1},{1,0},{2,3},{3,2},{4,5},{5,4},{6,7},{7,6},{8,9},{9,8},{10,11... | collective-permute-start | bytes 1179656 | tf_op jit(solution)/shard_map/ppermute | solution.py:174
Sparse Core Ops, SparseCore 0:
  16.1 73.4 all-gather.1

commit v8 on v7

--- a/solution.py
+++ b/solution.py
@@ -120,7 +120,16 @@
     layers_here = section_block_indices[0]
 
     def pick_patch(stack, patch, axis):
-        return lax.dynamic_index_in_dim(stack, patch, axis, keepdims=False)
+        chosen = lax.index_in_dim(stack, 0, axis, keepdims=False)
+        for other in range(1, stack.shape[axis]):
+            chosen = jnp.where(patch == other, lax.index_in_dim(stack, other, axis, keepdims=False), chosen)
+        return chosen
+
+    def arrival(position):
+        chosen = tile_arrival_permutation[0]
+        for index in range(1, patch_count):
+            chosen = jnp.where(position == index, tile_arrival_permutation[index], chosen)
+        return chosen
 
     first_rows = jnp.where(
         segment == 0,
@@ -130,7 +139,7 @@
     entry_rows = [first_rows[None]]
     for turn in range(1, patch_count):
         entry_rows.append(pick_patch(perturbed_frame_activation, tile_arrival_permutation[turn], 0)[None])
-    other_patch = tile_arrival_permutation[jnp.mod(1 - segment, patch_count)]
+    other_patch = arrival(jnp.mod(1 - segment, patch_count))
     far_k = pick_patch(earlier_step_lookup_matrix[0], other_patch, 1)
     far_v = pick_patch(earlier_step_content_matrix[0], other_patch, 1)
     packed = jnp.concatenate(entry_rows + [far_k, far_v], axis=0)

time: 148 us -> 145 us (0.980)
  between operations: 19.8 us -> 16.7 us
    unnamed x0 -> x2, local copies, waits for them, and re-layouts: none -> 1.8 us
where the time goes in v8:
time: 145 us
  waiting for transfers between devices  79.4 us (55%)
  Pallas kernels  28.1 us (19%)
  between operations  16.7 us (12%)
  local copies, waits for them, and re-layouts  10.9 us (8%)
  starting transfers between devices  5.62 us (4%)
  other arithmetic  3.9 us (3%)
    all_gather x1, waiting for transfers between devices, per_device(): whole = lax.all_gather(packed, 'ctx', axis=1, tiled=True)  67 us
    pallas_call x4, Pallas kernels, fused_layer(): pl.pallas_call(functools.partial(layer_kernel, two_sources=entry is not N...  28.1 us
    ppermute x1, waiting for transfers between devices, per_device(): got = lax.ppermute(sent, 'segment', [(i, i + 1) for i in range(count - 1)])  12 us
    another operation x4, local copies, waits for them, and re-layouts, fused_layer(): p.reshape(p.shape[0], 1, width)  5.25 us
    ppermute x1, starting transfers between devices, per_device(): swapped = lax.ppermute(got, 'ctx', [(c, c ^ 1) for c in range(ctx_count)])  3.13 us
  transfers between devices with their start and end apart: 3, of which 3 were waited for; matrix products, arithmetic and copies ran while one was open for 5% of the time, Pallas kernels for 0%

profile of v8, /device:TPU:33, one launch (start us, length us, event | category | flops | bytes accessed | tf_op | source)
XLA Modules:
  0.0 144.6 jit_solution(434133345467421493)
XLA Ops:
  6.5 1.3 fusion.2
  10.4 0.9 copy.16
  11.3 0.9 copy.15
  12.3 0.8 select_select_fusion
  13.1 0.7 pad_maximum_fusion
  14.4 1.3 reshape_squeeze.8.refs_2_.refs_4_
  15.7 1.3 reshape_squeeze.9.refs_3_.refs_5_
  17.1 1.3 reshape_squeeze.10.refs_4_.refs_6_
  18.4 1.3 reshape_squeeze.11.refs_5_.refs_7_
  19.7 0.6 pad_add_fusion
  20.3 67.0 %all-gather.2.cloned.1.call-done.refs_0_.refs_1_.refs_6_.refs_7_.refs_2_.refs_3_ = bf16[6,256,1536]{2,1,0:T(8,128)(2,1)} async-done(((bf16[6,8,1536]{2,1,0:T(8,128)(2,1)}), bf16[6,256,1536]{2,1,0:T(8,128)(2,1)}) %all-gather.2.cloned.1.call-update) | async-done | bytes 4718608 | tf_op jit(solution)/shard_map/all_gather | solution.py:146
  87.3 6.9 %shard_map.100 = (bf16[256,1536]{1,0:T(8,128)(2,1)}, bf16[256,1536]{1,0:T(8,128)(2,1)}, bf16[256,1536]{1,0:T(8,128)(2,1)}) custom-call(s32[2]{0:T(128)} %get-tuple-element.22.flags_ref, bf16[6,256,1536]{2,1,0:T(8,128)(2,1)} %all-gather.2.cloned.1.call-done.refs_0_.refs_1_.refs_6_.refs_7_.refs_2_.refs_3_, ...), custom_call_target="tpu_custom_call" | custom-call | flops 1610612736 | bytes 3932160 | tf_op jit(solution)/shard_map/pallas_call | solution.py:84
  94.3 7.0 %shard_map.101 = (bf16[256,1536]{1,0:T(8,128)(2,1)}, bf16[256,1536]{1,0:T(8,128)(2,1)}, bf16[256,1536]{1,0:T(8,128)(2,1)}) custom-call(s32[2]{0:T(128)} %get-tuple-element.21.flags_ref, bf16[1,256,1536]{2,1,0:T(8,128)(2,1)} %bitcast.27, bf16[1,256,1536]{2,1,0:T(8,128)(2,1)} %bitcast.28, f32[2,1,1536]{2,1,0:T(1,128)} %reshape_squeeze.8.refs_2_.refs_4_, ...), custom_call_target="tpu_custom_call" | custom-call | flops 1610612736 | bytes 3932160 | tf_op jit(solution)/shard_map/pallas_call | solution.py:84
  101.3 1.0 constant_dynamic-slice_fusion
  102.3 2.5 %collective-permute-start = (bf16[128,1536]{1,0:T(8,128)(2,1)S(1)}, bf16[128,1536]{1,0:T(8,128)(2,1)S(1)}, u32[]{:S(2)}, u32[]{:S(2)}) collective-permute-start(bf16[128,1536]{1,0:T(8,128)(2,1)S(1)} %constant_dynamic-slice_fusion), channel_id=1, source_target_pairs={{0,32},{32,64},{64,96},{96,128},{128,160},{160,192},{192,224},{224... | collective-permute-start | bytes 1179656 | tf_op jit(solution)/shard_map/ppermute | solution.py:181
  104.8 12.0 %collective-permute-done = bf16[128,1536]{1,0:T(8,128)(2,1)S(1)} collective-permute-done((bf16[128,1536]{1,0:T(8,128)(2,1)S(1)}, bf16[128,1536]{1,0:T(8,128)(2,1)S(1)}, u32[]{:S(2)}, u32[]{:S(2)}) %collective-permute-start) | collective-permute-done | bytes 393248 | tf_op jit(solution)/shard_map/ppermute | solution.py:181
  116.8 3.1 %collective-permute-start.1 = (bf16[128,1536]{1,0:T(8,128)(2,1)S(1)}, bf16[128,1536]{1,0:T(8,128)(2,1)S(1)}, u32[]{:S(2)}, u32[]{:S(2)}) collective-permute-start(bf16[128,1536]{1,0:T(8,128)(2,1)S(1)} %collective-permute-done), channel_id=1, source_target_pairs={{0,1},{1,0},{2,3},{3,2},{4,5},{5,4},{6,7},{7,6},{8,9},{9,8},{10,11... | collective-permute-start | bytes 1179656 | tf_op jit(solution)/shard_map/ppermute | solution.py:183
  119.9 0.7 dynamic-slice_bitcast_fusion.1
  120.7 0.4 collective-permute-done.1
  121.1 1.1 maximum_select_fusion.refs_0_.refs_1_
  122.2 7.4 %shard_map.102 = bf16[256,1536]{1,0:T(8,128)(2,1)} custom-call(s32[2]{0:T(128)} %get-tuple-element.22.flags_ref, bf16[1,256,1536]{2,1,0:T(8,128)(2,1)} %maximum_select_fusion.refs_0_.refs_1_, bf16[1,256,1536]{2,1,0:T(8,128)(2,1)} %maximum_select_fusion.refs_0_.refs_1_, ...), custom_call_target="tpu_custom_call" | custom-call | flops 1610612736 | bytes 2359296 | tf_op jit(solution)/shard_map/pallas_call | solution.py:84
  129.6 6.8 %shard_map.103 = bf16[256,1536]{1,0:T(8,128)(2,1)} custom-call(s32[2]{0:T(128)} %get-tuple-element.21.flags_ref, bf16[1,256,1536]{2,1,0:T(8,128)(2,1)} %bitcast.31, bf16[1,256,1536]{2,1,0:T(8,128)(2,1)} %bitcast.32, f32[2,1,1536]{2,1,0:T(1,128)} %reshape_squeeze.8.refs_2_.refs_4_, f32[2,1,1536]{2,1,0:T(1,128)} %reshape_squeeze.9.refs_3_.refs_5_, ...), custom_call_target="tpu_custom_call" | custom-call | flops 1610612736 | bytes 2359296 | tf_op jit(solution)/shard_map/pallas_call | solution.py:84
  136.4 0.7 dynamic-slice_bitcast_fusion
  137.2 0.6 maximum_bitcast_fusion
  (3 shorter events, 0.0 us)
Async XLA Ops:
  6.5 80.8 %all-gather.2.cloned.1.call-start = ((), (), s32[]{:S(2)}) async-start(), calls=%async_computation | async-start | bytes 4866048 | tf_op jit(solution)/shard_map/all_gather | solution.py:146
  102.3 14.5 %collective-permute-start = (bf16[128,1536]{1,0:T(8,128)(2,1)S(1)}, bf16[128,1536]{1,0:T(8,128)(2,1)S(1)}, u32[]{:S(2)}, u32[]{:S(2)}) collective-permute-start(bf16[128,1536]{1,0:T(8,128)(2,1)S(1)} %constant_dynamic-slice_fusion), channel_id=1, source_target_pairs={{0,32},{32,64},{64,96},{96,128},{128,160},{160,192},{192,224},{224... | collective-permute-start | bytes 1179656 | tf_op jit(solution)/shard_map/ppermute | solution.py:181
  116.8 4.3 %collective-permute-start.1 = (bf16[128,1536]{1,0:T(8,128)(2,1)S(1)}, bf16[128,1536]{1,0:T(8,128)(2,1)S(1)}, u32[]{:S(2)}, u32[]{:S(2)}) collective-permute-start(bf16[128,1536]{1,0:T(8,128)(2,1)S(1)} %collective-permute-done), channel_id=1, source_target_pairs={{0,1},{1,0},{2,3},{3,2},{4,5},{5,4},{6,7},{7,6},{8,9},{9,8},{10,11... | collective-permute-start | bytes 1179656 | tf_op jit(solution)/shard_map/ppermute | solution.py:183
Sparse Core Ops, SparseCore 0:
  13.9 73.4 all-gather.1

commit v9 on v8

--- a/solution.py
+++ b/solution.py
@@ -16,7 +16,7 @@
     return values * lax.rsqrt(jnp.mean(values * values, axis=-1, keepdims=True) + EPSILON)
 
 
-def layer_kernel(flags_ref, *refs, two_sources, keep_kv):
+def layer_kernel(flags_ref, *refs, two_sources, keep_kv, query_rows):
     if two_sources:
         full_ref, x_ref, entry_full_ref, entry_x_ref, *refs = refs
     else:
@@ -31,16 +31,29 @@
         use_entry = flags_ref[1] > 0
         whole = jnp.where(use_entry, entry_full_ref[...], whole)
         state = jnp.where(use_entry, entry_x_ref[...], state)
-    whole = whole.astype(jnp.float32)
-    row_scale = lax.rsqrt(jnp.mean(whole * whole, axis=-1, keepdims=True) + EPSILON)
+    def row_scale_of(rows_value):
+        rows_value = rows_value.astype(jnp.float32)
+        return lax.rsqrt(jnp.mean(rows_value * rows_value, axis=-1, keepdims=True) + EPSILON)
+
+    row_scale = row_scale_of(whole)
+    if query_rows is None:
+        state_q, row_scale_q = state, row_scale
+    else:
+        start = pl.multiple_of(flags_ref[2], query_rows)
+        state_q = x_ref[pl.ds(start, query_rows), :]
+        row_scale_q = row_scale_of(full_ref[pl.ds(start, query_rows), :])
     for j in range(state.shape[1] // HD):
         cols = slice(j * HD, (j + 1) * HD)
-        x_rounded = state[:, cols]
-        x = x_rounded.astype(jnp.float32)
-        hidden = x * row_scale * (1.0 + stretch_ref[:, cols]) + shift_ref[:, cols]
-        query = head_norm(hidden).astype(jnp.bfloat16)
+        stretch = 1.0 + stretch_ref[:, cols]
+        x_all = state[:, cols].astype(jnp.float32)
+        hidden = x_all * row_scale * stretch + shift_ref[:, cols]
         fresh_key = head_norm(hidden * factor_ref[:, cols]).astype(jnp.bfloat16)
         fresh_value = hidden.astype(jnp.bfloat16)
+        x_rounded = state_q[:, cols]
+        x = x_rounded.astype(jnp.float32)
+        if query_rows is not None:
+            hidden = x * row_scale_q * stretch + shift_ref[:, cols]
+        query = head_norm(hidden).astype(jnp.bfloat16)
         if keep_kv:
             kv_refs[0][:, cols] = fresh_key
             kv_refs[1][:, cols] = fresh_value
@@ -57,7 +70,9 @@
         o_ref[:, cols] = jnp.where(live, new_state, x_rounded)
 
 
-def fused_layer(flags, source, params, tier, far_k, far_v, entry=None, keep_kv=True, block=1536):
+def fused_layer(
+    flags, source, params, tier, far_k, far_v, entry=None, keep_kv=True, query_rows=None, block=1536
+):
     array, slab = source
     _, tokens, width = array.shape
 
@@ -81,14 +96,22 @@
     out_tile = pl.BlockSpec((tokens, block), lambda i, f: (0, i))
     out = jax.ShapeDtypeStruct((tokens, width), jnp.bfloat16)
     count = 3 if keep_kv else 1
+    out_shapes = (out,) * count
+    out_specs = (out_tile,) * count
+    if query_rows is not None:
+        assert not keep_kv and block == width and entry is None
+        out_shapes = (jax.ShapeDtypeStruct((query_rows, width), jnp.bfloat16),)
+        out_specs = (pl.BlockSpec((query_rows, block), lambda i, f: (0, i)),)
     results = pl.pallas_call(
-        functools.partial(layer_kernel, two_sources=entry is not None, keep_kv=keep_kv),
-        out_shape=(out,) * count,
+        functools.partial(
+            layer_kernel, two_sources=entry is not None, keep_kv=keep_kv, query_rows=query_rows
+        ),
+        out_shape=out_shapes,
         grid_spec=pltpu.PrefetchScalarGridSpec(
             num_scalar_prefetch=1,
             grid=(width // block,),
             in_specs=in_specs,
-            out_specs=(out_tile,) * count,
+            out_specs=out_specs,
         ),
         cost_estimate=pl.CostEstimate(
             flops=8 * tokens * 2 * tokens * width,
@@ -153,7 +176,8 @@
     first_segment = (segment == 0).astype(jnp.int32)
 
     def flags(tier):
-        return jnp.stack([(layers_here > tier).astype(jnp.int32), first_segment])
+        live = (layers_here > tier).astype(jnp.int32)
+        return jnp.stack([live, first_segment, (place * rows).astype(jnp.int32)])
 
     def own_rows(state):
         return lax.dynamic_slice_in_dim(state, place * rows, rows, 0)
@@ -189,12 +213,20 @@
         source = (arrived[None], 0)
         entry = (whole, turn)
         for tier in range(slot_count):
+            last = turn == patch_count - 1 and tier == slot_count - 1
             state, _, _ = fused_layer(
-                flags(tier), source, params, tier, *turn_zero_kv[tier], entry=entry, keep_kv=False
+                flags(tier),
+                source,
+                params,
+                tier,
+                *turn_zero_kv[tier],
+                entry=entry,
+                keep_kv=False,
+                query_rows=rows if last else None,
             )
             source = (state[None], 0)
             entry = None
-        outcomes.append(own_rows(state))
+        outcomes.append(state if state.shape[0] == rows else own_rows(state))
     return jnp.stack(outcomes)[None]
 
 

time: 145 us -> 144 us (level)
  no operation moved by 1% of the time
where the time goes in v9:
time: 144 us; the launch traced here: 143 us
  waiting for transfers between devices  79.4 us (55%)
  Pallas kernels  26.8 us (19%)
  between operations  16.7 us (12%)
  local copies, waits for them, and re-layouts  10.2 us (7%)
  starting transfers between devices  5.63 us (4%)
  other arithmetic  4.63 us (3%)
    all_gather x1, waiting for transfers between devices, per_device(): whole = lax.all_gather(packed, 'ctx', axis=1, tiled=True)  67 us
    pallas_call x4, Pallas kernels, fused_layer(): pl.pallas_call(functools.partial(layer_kernel, two_sources=entry is not N...  26.8 us
    ppermute x1, waiting for transfers between devices, per_device(): got = lax.ppermute(sent, 'segment', [(i, i + 1) for i in range(count - 1)])  12 us
    another operation x4, local copies, waits for them, and re-layouts, fused_layer(): p.reshape(p.shape[0], 1, width)  5.25 us
    ppermute x1, starting transfers between devices, per_device(): swapped = lax.ppermute(got, 'ctx', [(c, c ^ 1) for c in range(ctx_count)])  3.14 us
  transfers between devices with their start and end apart: 3, of which 3 were waited for; matrix products, arithmetic and copies ran while one was open for 5% of the time, Pallas kernels for 0%

profile of v9, /device:TPU:33, one launch (start us, length us, event | category | flops | bytes accessed | tf_op | source)
XLA Modules:
  0.0 143.3 jit_solution(16822613256415226604)
XLA Ops:
  6.5 1.3 fusion.2
  10.4 0.9 copy.16
  11.3 0.9 copy.15
  12.3 0.8 select_select_fusion
  13.1 0.7 pad_maximum_fusion
  13.7 0.0 all-gather.2.cloned.1.call-update
  14.4 1.3 reshape_squeeze.8.refs_2_.refs_4_
  15.7 1.3 reshape_squeeze.9.refs_3_.refs_5_
  17.1 1.3 reshape_squeeze.10.refs_4_.refs_6_
  18.4 1.3 reshape_squeeze.11.refs_5_.refs_7_
  19.7 0.6 add_add_fusion
  20.3 67.0 %all-gather.2.cloned.1.call-done.refs_0_.refs_1_.refs_6_.refs_7_.refs_2_.refs_3_ = bf16[6,256,1536]{2,1,0:T(8,128)(2,1)} async-done(((bf16[6,8,1536]{2,1,0:T(8,128)(2,1)}), bf16[6,256,1536]{2,1,0:T(8,128)(2,1)}) %all-gather.2.cloned.1.call-update) | async-done | bytes 4718608 | tf_op jit(solution)/shard_map/all_gather | solution.py:169
  87.3 6.9 %shard_map.100 = (bf16[256,1536]{1,0:T(8,128)(2,1)}, bf16[256,1536]{1,0:T(8,128)(2,1)}, bf16[256,1536]{1,0:T(8,128)(2,1)}) custom-call(s32[3]{0:T(128)} %get-tuple-element.22.flags_ref, bf16[6,256,1536]{2,1,0:T(8,128)(2,1)} %all-gather.2.cloned.1.call-done.refs_0_.refs_1_.refs_6_.refs_7_.refs_2_.refs_3_, ...), custom_call_target="tpu_custom_call" | custom-call | flops 1610612736 | bytes 3932160 | tf_op jit(solution)/shard_map/pallas_call | solution.py:105
  94.3 7.0 %shard_map.101 = (bf16[256,1536]{1,0:T(8,128)(2,1)}, bf16[256,1536]{1,0:T(8,128)(2,1)}, bf16[256,1536]{1,0:T(8,128)(2,1)}) custom-call(s32[3]{0:T(128)} %get-tuple-element.21.flags_ref, bf16[1,256,1536]{2,1,0:T(8,128)(2,1)} %bitcast.27, bf16[1,256,1536]{2,1,0:T(8,128)(2,1)} %bitcast.28, f32[2,1,1536]{2,1,0:T(1,128)} %reshape_squeeze.8.refs_2_.refs_4_, ...), custom_call_target="tpu_custom_call" | custom-call | flops 1610612736 | bytes 3932160 | tf_op jit(solution)/shard_map/pallas_call | solution.py:105
  101.3 1.0 constant_dynamic-slice_fusion
  102.3 2.5 %collective-permute-start = (bf16[128,1536]{1,0:T(8,128)(2,1)S(1)}, bf16[128,1536]{1,0:T(8,128)(2,1)S(1)}, u32[]{:S(2)}, u32[]{:S(2)}) collective-permute-start(bf16[128,1536]{1,0:T(8,128)(2,1)S(1)} %constant_dynamic-slice_fusion), channel_id=1, source_target_pairs={{0,32},{32,64},{64,96},{96,128},{128,160},{160,192},{192,224},{224... | collective-permute-start | bytes 1179656 | tf_op jit(solution)/shard_map/ppermute | solution.py:205
  104.8 12.0 %collective-permute-done = bf16[128,1536]{1,0:T(8,128)(2,1)S(1)} collective-permute-done((bf16[128,1536]{1,0:T(8,128)(2,1)S(1)}, bf16[128,1536]{1,0:T(8,128)(2,1)S(1)}, u32[]{:S(2)}, u32[]{:S(2)}) %collective-permute-start) | collective-permute-done | bytes 393248 | tf_op jit(solution)/shard_map/ppermute | solution.py:205
  116.8 3.1 %collective-permute-start.1 = (bf16[128,1536]{1,0:T(8,128)(2,1)S(1)}, bf16[128,1536]{1,0:T(8,128)(2,1)S(1)}, u32[]{:S(2)}, u32[]{:S(2)}) collective-permute-start(bf16[128,1536]{1,0:T(8,128)(2,1)S(1)} %collective-permute-done), channel_id=1, source_target_pairs={{0,1},{1,0},{2,3},{3,2},{4,5},{5,4},{6,7},{7,6},{8,9},{9,8},{10,11... | collective-permute-start | bytes 1179656 | tf_op jit(solution)/shard_map/ppermute | solution.py:207
  119.9 0.7 dynamic-slice_bitcast_fusion
  120.7 0.4 collective-permute-done.1
  121.1 1.1 maximum_select_fusion.refs_0_.refs_1_
  122.2 7.4 %shard_map.102 = bf16[256,1536]{1,0:T(8,128)(2,1)} custom-call(s32[3]{0:T(128)} %get-tuple-element.22.flags_ref, bf16[1,256,1536]{2,1,0:T(8,128)(2,1)} %maximum_select_fusion.refs_0_.refs_1_, bf16[1,256,1536]{2,1,0:T(8,128)(2,1)} %maximum_select_fusion.refs_0_.refs_1_, ...), custom_call_target="tpu_custom_call" | custom-call | flops 1610612736 | bytes 2359296 | tf_op jit(solution)/shard_map/pallas_call | solution.py:105
  129.6 5.5 %shard_map.103 = bf16[8,1536]{1,0:T(8,128)(2,1)} custom-call(s32[3]{0:T(128)} %get-tuple-element.21.flags_ref, bf16[1,256,1536]{2,1,0:T(8,128)(2,1)} %bitcast.31, bf16[1,256,1536]{2,1,0:T(8,128)(2,1)} %bitcast.32, f32[2,1,1536]{2,1,0:T(1,128)} %reshape_squeeze.8.refs_2_.refs_4_, f32[2,1,1536]{2,1,0:T(1,128)} %reshape_squeeze.9.refs_3_.refs_5_, ...), custom_call_target="tpu_custom_call" | custom-call | flops 1610612736 | bytes 2359296 | tf_op jit(solution)/shard_map/pallas_call | solution.py:105
  135.1 1.4 maximum_bitcast_fusion
  (2 shorter events, 0.0 us)
Async XLA Ops:
  6.5 80.8 %all-gather.2.cloned.1.call-start = ((), (), s32[]{:S(2)}) async-start(), calls=%async_computation | async-start | bytes 4866048 | tf_op jit(solution)/shard_map/all_gather | solution.py:169
  102.3 14.5 %collective-permute-start = (bf16[128,1536]{1,0:T(8,128)(2,1)S(1)}, bf16[128,1536]{1,0:T(8,128)(2,1)S(1)}, u32[]{:S(2)}, u32[]{:S(2)}) collective-permute-start(bf16[128,1536]{1,0:T(8,128)(2,1)S(1)} %constant_dynamic-slice_fusion), channel_id=1, source_target_pairs={{0,32},{32,64},{64,96},{96,128},{128,160},{160,192},{192,224},{224... | collective-permute-start | bytes 1179656 | tf_op jit(solution)/shard_map/ppermute | solution.py:205
  116.8 4.3 %collective-permute-start.1 = (bf16[128,1536]{1,0:T(8,128)(2,1)S(1)}, bf16[128,1536]{1,0:T(8,128)(2,1)S(1)}, u32[]{:S(2)}, u32[]{:S(2)}) collective-permute-start(bf16[128,1536]{1,0:T(8,128)(2,1)S(1)} %collective-permute-done), channel_id=1, source_target_pairs={{0,1},{1,0},{2,3},{3,2},{4,5},{5,4},{6,7},{7,6},{8,9},{9,8},{10,11... | collective-permute-start | bytes 1179656 | tf_op jit(solution)/shard_map/ppermute | solution.py:207
Sparse Core Ops, SparseCore 0:
  13.9 73.4 all-gather.1

commit v10 on v9

--- a/solution.py
+++ b/solution.py
@@ -18,9 +18,11 @@
 
 def layer_kernel(flags_ref, *refs, two_sources, keep_kv, query_rows):
     if two_sources:
-        full_ref, x_ref, entry_full_ref, entry_x_ref, *refs = refs
+        full_ref, entry_full_ref, *refs = refs
+        entry_x_ref = entry_full_ref
     else:
-        full_ref, x_ref, *refs = refs
+        full_ref, *refs = refs
+    x_ref = full_ref
     shift_ref, stretch_ref, factor_ref, skip_ref, kf_ref, vf_ref, o_ref, *kv_refs = refs
     live = flags_ref[0] > 0
     scale = 1.0 / math.sqrt(HD)
@@ -70,27 +72,23 @@
         o_ref[:, cols] = jnp.where(live, new_state, x_rounded)
 
 
-def fused_layer(
-    flags, source, params, tier, far_k, far_v, entry=None, keep_kv=True, query_rows=None, block=1536
-):
+def fused_layer(flags, source, params, tier, far_k, far_v, entry=None, keep_kv=True, query_rows=None):
     array, slab = source
     _, tokens, width = array.shape
+    block = width
 
     def slab_specs(slab_index):
-        return [
-            pl.BlockSpec((None, tokens, width), lambda i, f: (slab_index, 0, 0)),
-            pl.BlockSpec((None, tokens, block), lambda i, f: (slab_index, 0, i)),
-        ]
+        return [pl.BlockSpec((None, tokens, width), lambda i, f: (slab_index, 0, 0))]
 
     def tile_of(slab_index):
         return pl.BlockSpec((None, tokens, block), lambda i, f: (slab_index, 0, i))
 
     line = pl.BlockSpec((None, 1, block), lambda i, f: (tier, 0, i))
     in_specs = slab_specs(slab)
-    operands = [array, array]
+    operands = [array]
     if entry is not None:
         in_specs += slab_specs(entry[1])
-        operands += [entry[0], entry[0]]
+        operands += [entry[0]]
     in_specs += [line] * 4 + [tile_of(far_k[1]), tile_of(far_v[1])]
     operands += [p.reshape(p.shape[0], 1, width) for p in params] + [far_k[0], far_v[0]]
     out_tile = pl.BlockSpec((tokens, block), lambda i, f: (0, i))
@@ -99,7 +97,7 @@
     out_shapes = (out,) * count
     out_specs = (out_tile,) * count
     if query_rows is not None:
-        assert not keep_kv and block == width and entry is None
+        assert not keep_kv and entry is None
         out_shapes = (jax.ShapeDtypeStruct((query_rows, width), jnp.bfloat16),)
         out_specs = (pl.BlockSpec((query_rows, block), lambda i, f: (0, i)),)
     results = pl.pallas_call(

time: 144 us -> 143 us (level)
  no operation moved by 1% of the time
where the time goes in v10:
time: 143 us; the launch traced here: 142 us
  waiting for transfers between devices  79.4 us (56%)
  Pallas kernels  25.4 us (18%)
  between operations  16.7 us (12%)
  local copies, waits for them, and re-layouts  10.2 us (7%)
  starting transfers between devices  5.63 us (4%)
  other arithmetic  4.63 us (3%)
    all_gather x1, waiting for transfers between devices, per_device(): whole = lax.all_gather(packed, 'ctx', axis=1, tiled=True)  67 us
    pallas_call x4, Pallas kernels, fused_layer(): pl.pallas_call(functools.partial(layer_kernel, two_sources=entry is not N...  25.4 us
    ppermute x1, waiting for transfers between devices, per_device(): got = lax.ppermute(sent, 'segment', [(i, i + 1) for i in range(count - 1)])  12 us
    another operation x4, local copies, waits for them, and re-layouts, fused_layer(): p.reshape(p.shape[0], 1, width)  5.25 us
    ppermute x1, starting transfers between devices, per_device(): swapped = lax.ppermute(got, 'ctx', [(c, c ^ 1) for c in range(ctx_count)])  3.14 us
  transfers between devices with their start and end apart: 3, of which 3 were waited for; matrix products, arithmetic and copies ran while one was open for 5% of the time, Pallas kernels for 0%

profile of v10, /device:TPU:33, one launch (start us, length us, event | category | flops | bytes accessed | tf_op | source)
XLA Modules:
  0.0 141.9 jit_solution(9850195746169772304)
XLA Ops:
  6.5 1.3 fusion.2
  10.4 0.9 copy.16
  11.3 0.9 copy.15
  12.3 0.8 select_select_fusion
  13.1 0.7 pad_maximum_fusion
  13.7 0.0 all-gather.2.cloned.1.call-update
  14.4 1.3 reshape_squeeze.8.refs_1_.refs_2_
  15.7 1.3 reshape_squeeze.9.refs_2_.refs_3_
  17.1 1.3 reshape_squeeze.10.refs_3_.refs_4_
  18.4 1.3 reshape_squeeze.11.refs_4_.refs_5_
  19.7 0.6 add_add_fusion
  20.3 67.0 %all-gather.2.cloned.1.call-done.refs_0_.refs_5_.refs_6_.refs_1_ = bf16[6,256,1536]{2,1,0:T(8,128)(2,1)} async-done(((bf16[6,8,1536]{2,1,0:T(8,128)(2,1)}), bf16[6,256,1536]{2,1,0:T(8,128)(2,1)}) %all-gather.2.cloned.1.call-update) | async-done | bytes 4718608 | tf_op jit(solution)/shard_map/all_gather | solution.py:167
  87.3 6.6 %shard_map.100 = (bf16[256,1536]{1,0:T(8,128)(2,1)}, bf16[256,1536]{1,0:T(8,128)(2,1)}, bf16[256,1536]{1,0:T(8,128)(2,1)}) custom-call(s32[3]{0:T(128)} %get-tuple-element.22.flags_ref, bf16[6,256,1536]{2,1,0:T(8,128)(2,1)} %all-gather.2.cloned.1.call-done.refs_0_.refs_5_.refs_6_.refs_1_, f32[2,1,1536]{2,1,0:T(1,128)} %reshape_squeeze.8.refs_1_.refs_2_, ...), custom_call_target="tpu_custom_call" | custom-call | flops 1610612736 | bytes 3932160 | tf_op jit(solution)/shard_map/pallas_call | solution.py:103
  94.0 6.7 %shard_map.101 = (bf16[256,1536]{1,0:T(8,128)(2,1)}, bf16[256,1536]{1,0:T(8,128)(2,1)}, bf16[256,1536]{1,0:T(8,128)(2,1)}) custom-call(s32[3]{0:T(128)} %get-tuple-element.21.flags_ref, bf16[1,256,1536]{2,1,0:T(8,128)(2,1)} %bitcast.27, f32[2,1,1536]{2,1,0:T(1,128)} %reshape_squeeze.8.refs_1_.refs_2_, f32[2,1,1536]{2,1,0:T(1,128)} %reshape_squeeze.9.refs_2_.refs_3_, ...), custom_call_target="tpu_custom_call" | custom-call | flops 1610612736 | bytes 3932160 | tf_op jit(solution)/shard_map/pallas_call | solution.py:103
  100.7 1.0 constant_dynamic-slice_fusion
  101.7 2.5 %collective-permute-start = (bf16[128,1536]{1,0:T(8,128)(2,1)S(1)}, bf16[128,1536]{1,0:T(8,128)(2,1)S(1)}, u32[]{:S(2)}, u32[]{:S(2)}) collective-permute-start(bf16[128,1536]{1,0:T(8,128)(2,1)S(1)} %constant_dynamic-slice_fusion), channel_id=1, source_target_pairs={{0,32},{32,64},{64,96},{96,128},{128,160},{160,192},{192,224},{224... | collective-permute-start | bytes 1179656 | tf_op jit(solution)/shard_map/ppermute | solution.py:203
  104.2 12.0 %collective-permute-done = bf16[128,1536]{1,0:T(8,128)(2,1)S(1)} collective-permute-done((bf16[128,1536]{1,0:T(8,128)(2,1)S(1)}, bf16[128,1536]{1,0:T(8,128)(2,1)S(1)}, u32[]{:S(2)}, u32[]{:S(2)}) %collective-permute-start) | collective-permute-done | bytes 393248 | tf_op jit(solution)/shard_map/ppermute | solution.py:203
  116.2 3.1 %collective-permute-start.1 = (bf16[128,1536]{1,0:T(8,128)(2,1)S(1)}, bf16[128,1536]{1,0:T(8,128)(2,1)S(1)}, u32[]{:S(2)}, u32[]{:S(2)}) collective-permute-start(bf16[128,1536]{1,0:T(8,128)(2,1)S(1)} %collective-permute-done), channel_id=1, source_target_pairs={{0,1},{1,0},{2,3},{3,2},{4,5},{5,4},{6,7},{7,6},{8,9},{9,8},{10,11... | collective-permute-start | bytes 1179656 | tf_op jit(solution)/shard_map/ppermute | solution.py:205
  119.3 0.7 dynamic-slice_bitcast_fusion
  120.1 0.4 collective-permute-done.1
  120.5 1.1 maximum_select_fusion.refs_0_
  121.6 6.8 %shard_map.102 = bf16[256,1536]{1,0:T(8,128)(2,1)} custom-call(s32[3]{0:T(128)} %get-tuple-element.22.flags_ref, bf16[1,256,1536]{2,1,0:T(8,128)(2,1)} %maximum_select_fusion.refs_0_, bf16[6,256,1536]{2,1,0:T(8,128)(2,1)} %all-gather.2.cloned.1.call-done.refs_0_.refs_5_.refs_6_.refs_1_, f32[2,1,1536]{2,1,0:T(1,128)} %reshape_squeeze.8.refs_1_.refs_2_, ...), custom_call_target="tpu_custom_call" | custom-call | flops 1610612736 | bytes 2359296 | tf_op jit(solution)/shard_map/pallas_call | solution.py:103
  128.4 5.3 %shard_map.103 = bf16[8,1536]{1,0:T(8,128)(2,1)} custom-call(s32[3]{0:T(128)} %get-tuple-element.21.flags_ref, bf16[1,256,1536]{2,1,0:T(8,128)(2,1)} %bitcast.30, f32[2,1,1536]{2,1,0:T(1,128)} %reshape_squeeze.8.refs_1_.refs_2_, f32[2,1,1536]{2,1,0:T(1,128)} %reshape_squeeze.9.refs_2_.refs_3_, f32[2,1,1536]{2,1,0:T(1,128)} %reshape_squeeze.10.refs_3_.refs_4_, ...), custom_call_target="tpu_custom_call" | custom-call | flops 1610612736 | bytes 2359296 | tf_op jit(solution)/shard_map/pallas_call | solution.py:103
  133.7 1.4 maximum_bitcast_fusion
  (2 shorter events, 0.0 us)
Async XLA Ops:
  6.5 80.8 %all-gather.2.cloned.1.call-start = ((), (), s32[]{:S(2)}) async-start(), calls=%async_computation | async-start | bytes 4866048 | tf_op jit(solution)/shard_map/all_gather | solution.py:167
  101.7 14.5 %collective-permute-start = (bf16[128,1536]{1,0:T(8,128)(2,1)S(1)}, bf16[128,1536]{1,0:T(8,128)(2,1)S(1)}, u32[]{:S(2)}, u32[]{:S(2)}) collective-permute-start(bf16[128,1536]{1,0:T(8,128)(2,1)S(1)} %constant_dynamic-slice_fusion), channel_id=1, source_target_pairs={{0,32},{32,64},{64,96},{96,128},{128,160},{160,192},{192,224},{224... | collective-permute-start | bytes 1179656 | tf_op jit(solution)/shard_map/ppermute | solution.py:203
  116.2 4.3 %collective-permute-start.1 = (bf16[128,1536]{1,0:T(8,128)(2,1)S(1)}, bf16[128,1536]{1,0:T(8,128)(2,1)S(1)}, u32[]{:S(2)}, u32[]{:S(2)}) collective-permute-start(bf16[128,1536]{1,0:T(8,128)(2,1)S(1)} %collective-permute-done), channel_id=1, source_target_pairs={{0,1},{1,0},{2,3},{3,2},{4,5},{5,4},{6,7},{7,6},{8,9},{9,8},{10,11... | collective-permute-start | bytes 1179656 | tf_op jit(solution)/shard_map/ppermute | solution.py:205
Sparse Core Ops, SparseCore 0:
  13.9 73.4 all-gather.1

commit v11 on v10

--- a/solution.py
+++ b/solution.py
@@ -16,14 +16,18 @@
     return values * lax.rsqrt(jnp.mean(values * values, axis=-1, keepdims=True) + EPSILON)
 
 
-def layer_kernel(flags_ref, *refs, two_sources, keep_kv, query_rows):
+def layer_kernel(flags_ref, *refs, two_sources, keep_kv, query_rows, emit_rows, aliased):
     if two_sources:
         full_ref, entry_full_ref, *refs = refs
         entry_x_ref = entry_full_ref
     else:
         full_ref, *refs = refs
     x_ref = full_ref
-    shift_ref, stretch_ref, factor_ref, skip_ref, kf_ref, vf_ref, o_ref, *kv_refs = refs
+    shift_ref, stretch_ref, factor_ref, skip_ref, kf_ref, vf_ref, *refs = refs
+    if aliased:
+        refs = refs[1:]
+    o_ref, *refs = refs
+    kv_refs = refs[:2] if keep_kv else ()
     live = flags_ref[0] > 0
     scale = 1.0 / math.sqrt(HD)
     dims = (((1,), (1,)), ((), ()))
@@ -70,9 +74,27 @@
         attended = numerator / total
         new_state = (x + skip_ref[:, cols] * attended).astype(o_ref.dtype)
         o_ref[:, cols] = jnp.where(live, new_state, x_rounded)
-
-
-def fused_layer(flags, source, params, tier, far_k, far_v, entry=None, keep_kv=True, query_rows=None):
+    if emit_rows:
+        half_ref, rows_ref = refs[len(kv_refs) :]
+        half = half_ref.shape[0]
+        rows = rows_ref.shape[0]
+        half_ref[...] = o_ref[pl.ds(pl.multiple_of(flags_ref[3], half), half), :]
+        rows_ref[...] = o_ref[pl.ds(pl.multiple_of(flags_ref[2], rows), rows), :]
+
+
+def fused_layer(
+    flags,
+    source,
+    params,
+    tier,
+    far_k,
+    far_v,
+    entry=None,
+    keep_kv=True,
+    query_rows=None,
+    emit_rows=None,
+    into=None,
+):
     array, slab = source
     _, tokens, width = array.shape
     block = width
@@ -91,6 +113,7 @@
         operands += [entry[0]]
     in_specs += [line] * 4 + [tile_of(far_k[1]), tile_of(far_v[1])]
     operands += [p.reshape(p.shape[0], 1, width) for p in params] + [far_k[0], far_v[0]]
+    aliases = {}
     out_tile = pl.BlockSpec((tokens, block), lambda i, f: (0, i))
     out = jax.ShapeDtypeStruct((tokens, width), jnp.bfloat16)
     count = 3 if keep_kv else 1
@@ -100,9 +123,32 @@
         assert not keep_kv and entry is None
         out_shapes = (jax.ShapeDtypeStruct((query_rows, width), jnp.bfloat16),)
         out_specs = (pl.BlockSpec((query_rows, block), lambda i, f: (0, i)),)
-    results = pl.pallas_call(
+    if into is not None:
+        assert query_rows is not None
+        buffer, slot = into
+        in_specs.append(pl.BlockSpec(memory_space=pl.ANY))
+        operands.append(buffer)
+        aliases = {len(operands): 0}
+        out_shapes = (jax.ShapeDtypeStruct(buffer.shape, buffer.dtype),)
+        out_specs = (pl.BlockSpec((None, query_rows, block), lambda i, f: (slot, 0, i)),)
+    if emit_rows is not None:
+        half, rows, slots = emit_rows
+        out_shapes += (
+            jax.ShapeDtypeStruct((half, width), jnp.bfloat16),
+            jax.ShapeDtypeStruct((slots, rows, width), jnp.bfloat16),
+        )
+        out_specs += (
+            pl.BlockSpec((half, block), lambda i, f: (0, i)),
+            pl.BlockSpec((None, rows, block), lambda i, f: (0, 0, i)),
+        )
+    return pl.pallas_call(
         functools.partial(
-            layer_kernel, two_sources=entry is not None, keep_kv=keep_kv, query_rows=query_rows
+            layer_kernel,
+            two_sources=entry is not None,
+            keep_kv=keep_kv,
+            query_rows=query_rows,
+            emit_rows=emit_rows is not None,
+            aliased=into is not None,
         ),
         out_shape=out_shapes,
         grid_spec=pltpu.PrefetchScalarGridSpec(
@@ -111,13 +157,13 @@
             in_specs=in_specs,
             out_specs=out_specs,
         ),
+        input_output_aliases=aliases,
         cost_estimate=pl.CostEstimate(
             flops=8 * tokens * 2 * tokens * width,
             transcendentals=tokens * 2 * tokens * (width // HD),
             bytes_accessed=(4 + 2 * count) * tokens * width,
         ),
     )(flags, *operands)
-    return results if keep_kv else (results[0], None, None)
 
 
 def per_device(
@@ -172,34 +218,32 @@
         tier_skip_coefficient[0],
     ]
     first_segment = (segment == 0).astype(jnp.int32)
+    core = jnp.mod(place, 2)
+    half = rows * lax.axis_size("ctx") // 2
 
     def flags(tier):
         live = (layers_here > tier).astype(jnp.int32)
-        return jnp.stack([live, first_segment, (place * rows).astype(jnp.int32)])
-
-    def own_rows(state):
-        return lax.dynamic_slice_in_dim(state, place * rows, rows, 0)
-
-    outcomes = []
+        return jnp.stack([live, first_segment, (place * rows).astype(jnp.int32), (core * half).astype(jnp.int32)])
+
     source = (whole, 0)
     turn_zero_kv = []
     for tier in range(slot_count):
-        state, fresh_key, fresh_value = fused_layer(
+        last = tier == slot_count - 1
+        results = fused_layer(
             flags(tier),
             source,
             params,
             tier,
             (whole, patch_count + tier),
             (whole, patch_count + slot_count + tier),
-        )
+            emit_rows=(half, rows, patch_count) if last else None,
+        )
+        state, fresh_key, fresh_value = results[:3]
         source = (state[None], 0)
         turn_zero_kv.append(((fresh_key[None], 0), (fresh_value[None], 0)))
-    outcomes.append(own_rows(state))
+    sent, outcomes = results[3:]
     count = lax.axis_size("segment")
     for turn in range(1, patch_count):
-        core = jnp.mod(place, 2)
-        half = state.shape[0] // 2
-        sent = lax.dynamic_slice_in_dim(state, core * half, half, 0)
         got = lax.ppermute(sent, "segment", [(i, i + 1) for i in range(count - 1)])
         ctx_count = lax.axis_size("ctx")
         swapped = lax.ppermute(got, "ctx", [(c, c ^ 1) for c in range(ctx_count)])
@@ -211,21 +255,26 @@
         source = (arrived[None], 0)
         entry = (whole, turn)
         for tier in range(slot_count):
-            last = turn == patch_count - 1 and tier == slot_count - 1
-            state, _, _ = fused_layer(
-                flags(tier),
-                source,
-                params,
-                tier,
-                *turn_zero_kv[tier],
-                entry=entry,
-                keep_kv=False,
-                query_rows=rows if last else None,
-            )
-            source = (state[None], 0)
-            entry = None
-        outcomes.append(state if state.shape[0] == rows else own_rows(state))
-    return jnp.stack(outcomes)[None]
+            last = tier == slot_count - 1
+            if last:
+                assert turn == patch_count - 1
+                (outcomes,) = fused_layer(
+                    flags(tier),
+                    source,
+                    params,
+                    tier,
+                    *turn_zero_kv[tier],
+                    keep_kv=False,
+                    query_rows=rows,
+                    into=(outcomes, turn),
+                )
+            else:
+                (state,) = fused_layer(
+                    flags(tier), source, params, tier, *turn_zero_kv[tier], entry=entry, keep_kv=False
+                )
+                source = (state[None], 0)
+                entry = None
+    return outcomes[None]
 
 
 def solution(mesh):

time: 143 us -> 141 us (0.986)
  local copies, waits for them, and re-layouts: 10.2 us -> 8.39 us
  transfers between devices with their start and end apart: 3 -> 3, of which waited for: 3 -> 3; matrix products, arithmetic and copies ran while one was open for 5% -> 4% of each run, Pallas kernels for 0% -> 0%
where the time goes in v11:
time: 141 us; the launch traced here: 140 us
  waiting for transfers between devices  80.4 us (57%)
  Pallas kernels  25.7 us (18%)
  between operations  16.7 us (12%)
  local copies, waits for them, and re-layouts  8.39 us (6%)
  starting transfers between devices  5.62 us (4%)
  other arithmetic  3.25 us (2%)
    all_gather x1, waiting for transfers between devices, per_device(): whole = lax.all_gather(packed, 'ctx', axis=1, tiled=True)  67 us
    pallas_call x4, Pallas kernels, fused_layer(): pl.pallas_call(functools.partial(layer_kernel, two_sources=entry is not N...  25.7 us
    ppermute x1, waiting for transfers between devices, per_device(): got = lax.ppermute(sent, 'segment', [(i, i + 1) for i in range(count - 1)])  12.2 us
    another operation x4, local copies, waits for them, and re-layouts, fused_layer(): p.reshape(p.shape[0], 1, width)  5.25 us
    ppermute x1, starting transfers between devices, per_device(): swapped = lax.ppermute(got, 'ctx', [(c, c ^ 1) for c in range(ctx_count)])  3.14 us
  transfers between devices with their start and end apart: 3, of which 3 were waited for; matrix products, arithmetic and copies ran while one was open for 4% of the time, Pallas kernels for 0%

profile of v11, /device:TPU:33, one launch (start us, length us, event | category | flops | bytes accessed | tf_op | source)
XLA Modules:
  0.0 140.0 jit_solution(7492748879691988733)
XLA Ops:
  6.5 0.0 all-gather.2.cloned.1.call-start
  6.5 1.3 fusion.2
  10.4 0.9 copy.17
  11.3 0.9 copy.16
  12.3 0.8 select_select_fusion
  13.1 0.7 pad_maximum_fusion
  13.7 0.0 all-gather.2.cloned.1.call-update
  14.4 1.3 reshape_squeeze.8.refs_1_.refs_2_
  15.7 1.3 reshape_squeeze.9.refs_2_.refs_3_
  17.1 1.3 reshape_squeeze.10.refs_3_.refs_4_
  18.4 1.3 reshape_squeeze.11.refs_4_.refs_5_
  19.7 0.6 add_add_fusion
  20.3 67.0 %all-gather.2.cloned.1.call-done.refs_0_.refs_5_.refs_6_.refs_1_ = bf16[6,256,1536]{2,1,0:T(8,128)(2,1)} async-done(((bf16[6,8,1536]{2,1,0:T(8,128)(2,1)}), bf16[6,256,1536]{2,1,0:T(8,128)(2,1)}) %all-gather.2.cloned.1.call-update) | async-done | bytes 4718608 | tf_op jit(solution)/shard_map/all_gather | solution.py:213
  87.3 6.7 %shard_map.100 = (bf16[256,1536]{1,0:T(8,128)(2,1)}, bf16[256,1536]{1,0:T(8,128)(2,1)}, bf16[256,1536]{1,0:T(8,128)(2,1)}) custom-call(s32[4]{0:T(128)} %get-tuple-element.24.flags_ref, bf16[6,256,1536]{2,1,0:T(8,128)(2,1)} %all-gather.2.cloned.1.call-done.refs_0_.refs_5_.refs_6_.refs_1_, f32[2,1,1536]{2,1,0:T(1,128)} %reshape_squeeze.8.refs_1_.refs_2_, ...), custom_call_target="tpu_custom_call" | custom-call | flops 1610612736 | bytes 3932160 | tf_op jit(solution)/shard_map/pallas_call | solution.py:144
  94.0 6.8 %shard_map.101 = (bf16[256,1536]{1,0:T(8,128)(2,1)}, bf16[256,1536]{1,0:T(8,128)(2,1)}, bf16[256,1536]{1,0:T(8,128)(2,1)}, bf16[128,1536]{1,0:T(8,128)(2,1)}, bf16[2,8,1536]{2,1,0:T(8,128)(2,1)}) custom-call(s32[4]{0:T(128)} %get-tuple-element.23.flags_ref, bf16[1,256,1536]{2,1,0:T(8,128)(2,1)} %bitcast.24, f32[2,1,1536]{2,1,0:T(1,128)} %reshape_squeeze.8.refs_1_.refs_2_, ...), custom_call_target="tpu_custom_call" | custom-call | flops 1610612736 | bytes 3932160 | tf_op jit(solution)/shard_map/pallas_call | solution.py:144
  100.8 2.5 %collective-permute-start = (bf16[128,1536]{1,0:T(8,128)(2,1)}, bf16[128,1536]{1,0:T(8,128)(2,1)S(1)}, u32[]{:S(2)}, u32[]{:S(2)}) collective-permute-start(bf16[128,1536]{1,0:T(8,128)(2,1)} %get-tuple-element.13), channel_id=1, source_target_pairs={{0,32},{32,64},{64,96},{96,128},{128,160},{160,192},{192,224},{224... | collective-permute-start | bytes 1179656 | tf_op jit(solution)/shard_map/ppermute | solution.py:247
  103.3 12.2 %collective-permute-done = bf16[128,1536]{1,0:T(8,128)(2,1)S(1)} collective-permute-done((bf16[128,1536]{1,0:T(8,128)(2,1)}, bf16[128,1536]{1,0:T(8,128)(2,1)S(1)}, u32[]{:S(2)}, u32[]{:S(2)}) %collective-permute-start) | collective-permute-done | bytes 393248 | tf_op jit(solution)/shard_map/ppermute | solution.py:247
  115.5 3.1 %collective-permute-start.1 = (bf16[128,1536]{1,0:T(8,128)(2,1)S(1)}, bf16[128,1536]{1,0:T(8,128)(2,1)S(1)}, u32[]{:S(2)}, u32[]{:S(2)}) collective-permute-start(bf16[128,1536]{1,0:T(8,128)(2,1)S(1)} %collective-permute-done), channel_id=1, source_target_pairs={{0,1},{1,0},{2,3},{3,2},{4,5},{5,4},{6,7},{7,6},{8,9},{9,8},{10,11... | collective-permute-start | bytes 1179656 | tf_op jit(solution)/shard_map/ppermute | solution.py:249
  118.6 1.1 collective-permute-done.1
  119.8 1.1 maximum_select_fusion.refs_0_
  120.9 6.9 %shard_map.102 = bf16[256,1536]{1,0:T(8,128)(2,1)} custom-call(s32[4]{0:T(128)} %get-tuple-element.24.flags_ref, bf16[1,256,1536]{2,1,0:T(8,128)(2,1)} %maximum_select_fusion.refs_0_, bf16[6,256,1536]{2,1,0:T(8,128)(2,1)} %all-gather.2.cloned.1.call-done.refs_0_.refs_5_.refs_6_.refs_1_, f32[2,1,1536]{2,1,0:T(1,128)} %reshape_squeeze.8.refs_1_.refs_2_, ...), custom_call_target="tpu_custom_call" | custom-call | flops 1610612736 | bytes 2359296 | tf_op jit(solution)/shard_map/pallas_call | solution.py:144
  127.8 5.3 %shard_map.103 = bf16[2,8,1536]{2,1,0:T(8,128)(2,1)} custom-call(s32[4]{0:T(128)} %get-tuple-element.23.flags_ref, bf16[1,256,1536]{2,1,0:T(8,128)(2,1)} %bitcast.27, f32[2,1,1536]{2,1,0:T(1,128)} %reshape_squeeze.8.refs_1_.refs_2_, f32[2,1,1536]{2,1,0:T(1,128)} %reshape_squeeze.9.refs_2_.refs_3_, ...), custom_call_target="tpu_custom_call", output_to_operand_aliasing={{}: (8, {})} | custom-call | flops 1610612736 | bytes 2359296 | tf_op jit(solution)/shard_map/pallas_call | solution.py:144
  (1 shorter events, 0.0 us)
Async XLA Ops:
  6.5 80.8 %all-gather.2.cloned.1.call-start = ((), (), s32[]{:S(2)}) async-start(), calls=%async_computation | async-start | bytes 4866048 | tf_op jit(solution)/shard_map/all_gather | solution.py:213
  100.8 14.7 %collective-permute-start = (bf16[128,1536]{1,0:T(8,128)(2,1)}, bf16[128,1536]{1,0:T(8,128)(2,1)S(1)}, u32[]{:S(2)}, u32[]{:S(2)}) collective-permute-start(bf16[128,1536]{1,0:T(8,128)(2,1)} %get-tuple-element.13), channel_id=1, source_target_pairs={{0,32},{32,64},{64,96},{96,128},{128,160},{160,192},{192,224},{224... | collective-permute-start | bytes 1179656 | tf_op jit(solution)/shard_map/ppermute | solution.py:247
  115.5 4.3 %collective-permute-start.1 = (bf16[128,1536]{1,0:T(8,128)(2,1)S(1)}, bf16[128,1536]{1,0:T(8,128)(2,1)S(1)}, u32[]{:S(2)}, u32[]{:S(2)}) collective-permute-start(bf16[128,1536]{1,0:T(8,128)(2,1)S(1)} %collective-permute-done), channel_id=1, source_target_pairs={{0,1},{1,0},{2,3},{3,2},{4,5},{5,4},{6,7},{7,6},{8,9},{9,8},{10,11... | collective-permute-start | bytes 1179656 | tf_op jit(solution)/shard_map/ppermute | solution.py:249
Sparse Core Ops, SparseCore 0:
  13.9 73.4 all-gather.1

commit v12 on v11

--- a/solution.py
+++ b/solution.py
@@ -16,18 +16,26 @@
     return values * lax.rsqrt(jnp.mean(values * values, axis=-1, keepdims=True) + EPSILON)
 
 
-def layer_kernel(flags_ref, *refs, two_sources, keep_kv, query_rows, emit_rows, aliased):
+def layer_kernel(flags_ref, *refs, two_sources, keep_kv, query_rows, emit_rows, aliased, far_slabs):
     if two_sources:
         full_ref, entry_full_ref, *refs = refs
         entry_x_ref = entry_full_ref
     else:
         full_ref, *refs = refs
     x_ref = full_ref
-    shift_ref, stretch_ref, factor_ref, skip_ref, kf_ref, vf_ref, *refs = refs
+    shift_ref, stretch_ref, factor_ref, skip_ref, kf_hbm, vf_hbm, *refs = refs
     if aliased:
         refs = refs[1:]
     o_ref, *refs = refs
+    kf_ref, vf_ref, num_ref, total_ref, query_ref, copy_sems = refs[-6:]
+    refs = refs[:-6]
     kv_refs = refs[:2] if keep_kv else ()
+    far_copies = [
+        pltpu.make_async_copy(kf_hbm.at[far_slabs[0]], kf_ref, copy_sems.at[0]),
+        pltpu.make_async_copy(vf_hbm.at[far_slabs[1]], vf_ref, copy_sems.at[1]),
+    ]
+    for copy in far_copies:
+        copy.start()
     live = flags_ref[0] > 0
     scale = 1.0 / math.sqrt(HD)
     dims = (((1,), (1,)), ((), ()))
@@ -37,6 +45,7 @@
         use_entry = flags_ref[1] > 0
         whole = jnp.where(use_entry, entry_full_ref[...], whole)
         state = jnp.where(use_entry, entry_x_ref[...], state)
+
     def row_scale_of(rows_value):
         rows_value = rows_value.astype(jnp.float32)
         return lax.rsqrt(jnp.mean(rows_value * rows_value, axis=-1, keepdims=True) + EPSILON)
@@ -48,30 +57,40 @@
         start = pl.multiple_of(flags_ref[2], query_rows)
         state_q = x_ref[pl.ds(start, query_rows), :]
         row_scale_q = row_scale_of(full_ref[pl.ds(start, query_rows), :])
-    for j in range(state.shape[1] // HD):
+    heads = state.shape[1] // HD
+    for j in range(heads):
         cols = slice(j * HD, (j + 1) * HD)
         stretch = 1.0 + stretch_ref[:, cols]
         x_all = state[:, cols].astype(jnp.float32)
         hidden = x_all * row_scale * stretch + shift_ref[:, cols]
         fresh_key = head_norm(hidden * factor_ref[:, cols]).astype(jnp.bfloat16)
         fresh_value = hidden.astype(jnp.bfloat16)
-        x_rounded = state_q[:, cols]
-        x = x_rounded.astype(jnp.float32)
         if query_rows is not None:
+            x = state_q[:, cols].astype(jnp.float32)
             hidden = x * row_scale_q * stretch + shift_ref[:, cols]
         query = head_norm(hidden).astype(jnp.bfloat16)
+        query_ref[:, cols] = query
         if keep_kv:
             kv_refs[0][:, cols] = fresh_key
             kv_refs[1][:, cols] = fresh_value
         near = lax.dot_general(query, fresh_key, dims, preferred_element_type=jnp.float32) * scale
+        near = jnp.exp(near)
+        total_ref[:, cols] = jnp.broadcast_to(jnp.sum(near, axis=-1, keepdims=True), query.shape)
+        num_ref[:, cols] = jnp.dot(near.astype(jnp.bfloat16), fresh_value, preferred_element_type=jnp.float32)
+    for copy in far_copies:
+        copy.wait()
+    for j in range(heads):
+        cols = slice(j * HD, (j + 1) * HD)
+        query = query_ref[:, cols]
         far = lax.dot_general(query, kf_ref[:, cols], dims, preferred_element_type=jnp.float32) * scale
-        near = jnp.exp(near)
         far = jnp.exp(far)
-        total = jnp.sum(near, axis=-1, keepdims=True) + jnp.sum(far, axis=-1, keepdims=True)
-        numerator = jnp.dot(
-            near.astype(jnp.bfloat16), fresh_value, preferred_element_type=jnp.float32
-        ) + jnp.dot(far.astype(jnp.bfloat16), vf_ref[:, cols], preferred_element_type=jnp.float32)
+        total = total_ref[:, cols][:, :1] + jnp.sum(far, axis=-1, keepdims=True)
+        numerator = num_ref[:, cols] + jnp.dot(
+            far.astype(jnp.bfloat16), vf_ref[:, cols], preferred_element_type=jnp.float32
+        )
         attended = numerator / total
+        x_rounded = state_q[:, cols]
+        x = x_rounded.astype(jnp.float32)
         new_state = (x + skip_ref[:, cols] * attended).astype(o_ref.dtype)
         o_ref[:, cols] = jnp.where(live, new_state, x_rounded)
     if emit_rows:
@@ -111,7 +130,7 @@
     if entry is not None:
         in_specs += slab_specs(entry[1])
         operands += [entry[0]]
-    in_specs += [line] * 4 + [tile_of(far_k[1]), tile_of(far_v[1])]
+    in_specs += [line] * 4 + [pl.BlockSpec(memory_space=pl.ANY)] * 2
     operands += [p.reshape(p.shape[0], 1, width) for p in params] + [far_k[0], far_v[0]]
     aliases = {}
     out_tile = pl.BlockSpec((tokens, block), lambda i, f: (0, i))
@@ -149,6 +168,7 @@
             query_rows=query_rows,
             emit_rows=emit_rows is not None,
             aliased=into is not None,
+            far_slabs=(far_k[1], far_v[1]),
         ),
         out_shape=out_shapes,
         grid_spec=pltpu.PrefetchScalarGridSpec(
@@ -156,6 +176,14 @@
             grid=(width // block,),
             in_specs=in_specs,
             out_specs=out_specs,
+            scratch_shapes=[
+                pltpu.VMEM((tokens, width), jnp.bfloat16),
+                pltpu.VMEM((tokens, width), jnp.bfloat16),
+                pltpu.VMEM((query_rows or tokens, width), jnp.float32),
+                pltpu.VMEM((query_rows or tokens, width), jnp.float32),
+                pltpu.VMEM((query_rows or tokens, width), jnp.bfloat16),
+                pltpu.SemaphoreType.DMA((2,)),
+            ],
         ),
         input_output_aliases=aliases,
         cost_estimate=pl.CostEstimate(

time: 141 us -> 148 us (1.050)
  Pallas kernels: 25.7 us -> 32.9 us
    pallas_call x4, Pallas kernels: 25.7 us -> 32.9 us  [fused_layer(): pl.pallas_call(functools.partial(layer_kernel, two_sources=entry is not N...]
where the time goes in v12:
time: 148 us; the launch traced here: 147 us
  waiting for transfers between devices  80.4 us (54%)
  Pallas kernels  32.9 us (22%)
  between operations  16.7 us (11%)
  local copies, waits for them, and re-layouts  8.39 us (6%)
  starting transfers between devices  5.62 us (4%)
  other arithmetic  3.25 us (2%)
    all_gather x1, waiting for transfers between devices, per_device(): whole = lax.all_gather(packed, 'ctx', axis=1, tiled=True)  67 us
    pallas_call x4, Pallas kernels, fused_layer(): pl.pallas_call(functools.partial(layer_kernel, two_sources=entry is not N...  32.9 us
    ppermute x1, waiting for transfers between devices, per_device(): got = lax.ppermute(sent, 'segment', [(i, i + 1) for i in range(count - 1)])  12.2 us
    another operation x4, local copies, waits for them, and re-layouts, fused_layer(): p.reshape(p.shape[0], 1, width)  5.25 us
    ppermute x1, starting transfers between devices, per_device(): swapped = lax.ppermute(got, 'ctx', [(c, c ^ 1) for c in range(ctx_count)])  3.13 us
  transfers between devices with their start and end apart: 3, of which 3 were waited for; matrix products, arithmetic and copies ran while one was open for 4% of the time, Pallas kernels for 0%

profile of v12, /device:TPU:33, one launch (start us, length us, event | category | flops | bytes accessed | tf_op | source)
XLA Modules:
  0.0 147.2 jit_solution(18385667150253491740)
XLA Ops:
  6.5 0.0 all-gather.2.cloned.1.call-start
  6.5 1.3 fusion.2
  10.4 0.9 copy.17
  11.3 0.9 copy.16
  12.3 0.8 select_select_fusion
  13.1 0.7 pad_maximum_fusion
  13.7 0.0 all-gather.2.cloned.1.call-update
  14.4 1.3 reshape_squeeze.8.refs_1_.refs_2_
  15.7 1.3 reshape_squeeze.9.refs_2_.refs_3_
  17.1 1.3 reshape_squeeze.10.refs_3_.refs_4_
  18.4 1.3 reshape_squeeze.11.refs_4_.refs_5_
  19.7 0.6 add_add_fusion
  20.3 67.0 %all-gather.2.cloned.1.call-done.refs_0_.refs_5_.refs_6_.refs_1_ = bf16[6,256,1536]{2,1,0:T(8,128)(2,1)} async-done(((bf16[6,8,1536]{2,1,0:T(8,128)(2,1)}), bf16[6,256,1536]{2,1,0:T(8,128)(2,1)}) %all-gather.2.cloned.1.call-update) | async-done | bytes 4718608 | tf_op jit(solution)/shard_map/all_gather | solution.py:241
  87.3 8.6 %shard_map.100 = (bf16[256,1536]{1,0:T(8,128)(2,1)}, bf16[256,1536]{1,0:T(8,128)(2,1)}, bf16[256,1536]{1,0:T(8,128)(2,1)}) custom-call(s32[4]{0:T(128)} %get-tuple-element.24.flags_ref, bf16[6,256,1536]{2,1,0:T(8,128)(2,1)} %all-gather.2.cloned.1.call-done.refs_0_.refs_5_.refs_6_.refs_1_, f32[2,1,1536]{2,1,0:T(1,128)} %reshape_squeeze.8.refs_1_.refs_2_, ...), custom_call_target="tpu_custom_call" | custom-call | flops 1610612736 | bytes 3932160 | tf_op jit(solution)/shard_map/pallas_call | solution.py:163
  96.0 8.7 %shard_map.101 = (bf16[256,1536]{1,0:T(8,128)(2,1)}, bf16[256,1536]{1,0:T(8,128)(2,1)}, bf16[256,1536]{1,0:T(8,128)(2,1)}, bf16[128,1536]{1,0:T(8,128)(2,1)}, bf16[2,8,1536]{2,1,0:T(8,128)(2,1)}) custom-call(s32[4]{0:T(128)} %get-tuple-element.23.flags_ref, bf16[1,256,1536]{2,1,0:T(8,128)(2,1)} %bitcast.24, f32[2,1,1536]{2,1,0:T(1,128)} %reshape_squeeze.8.refs_1_.refs_2_, ...), custom_call_target="tpu_custom_call" | custom-call | flops 1610612736 | bytes 3932160 | tf_op jit(solution)/shard_map/pallas_call | solution.py:163
  104.7 2.5 %collective-permute-start = (bf16[128,1536]{1,0:T(8,128)(2,1)}, bf16[128,1536]{1,0:T(8,128)(2,1)S(1)}, u32[]{:S(2)}, u32[]{:S(2)}) collective-permute-start(bf16[128,1536]{1,0:T(8,128)(2,1)} %get-tuple-element.13), channel_id=1, source_target_pairs={{0,32},{32,64},{64,96},{96,128},{128,160},{160,192},{192,224},{224... | collective-permute-start | bytes 1179656 | tf_op jit(solution)/shard_map/ppermute | solution.py:275
  107.2 12.2 %collective-permute-done = bf16[128,1536]{1,0:T(8,128)(2,1)S(1)} collective-permute-done((bf16[128,1536]{1,0:T(8,128)(2,1)}, bf16[128,1536]{1,0:T(8,128)(2,1)S(1)}, u32[]{:S(2)}, u32[]{:S(2)}) %collective-permute-start) | collective-permute-done | bytes 393248 | tf_op jit(solution)/shard_map/ppermute | solution.py:275
  119.4 3.1 %collective-permute-start.1 = (bf16[128,1536]{1,0:T(8,128)(2,1)S(1)}, bf16[128,1536]{1,0:T(8,128)(2,1)S(1)}, u32[]{:S(2)}, u32[]{:S(2)}) collective-permute-start(bf16[128,1536]{1,0:T(8,128)(2,1)S(1)} %collective-permute-done), channel_id=1, source_target_pairs={{0,1},{1,0},{2,3},{3,2},{4,5},{5,4},{6,7},{7,6},{8,9},{9,8},{10,11... | collective-permute-start | bytes 1179656 | tf_op jit(solution)/shard_map/ppermute | solution.py:277
  122.5 1.1 collective-permute-done.1
  123.7 1.1 maximum_select_fusion.refs_0_
  124.8 8.7 %shard_map.102 = bf16[256,1536]{1,0:T(8,128)(2,1)} custom-call(s32[4]{0:T(128)} %get-tuple-element.24.flags_ref, bf16[1,256,1536]{2,1,0:T(8,128)(2,1)} %maximum_select_fusion.refs_0_, bf16[6,256,1536]{2,1,0:T(8,128)(2,1)} %all-gather.2.cloned.1.call-done.refs_0_.refs_5_.refs_6_.refs_1_, f32[2,1,1536]{2,1,0:T(1,128)} %reshape_squeeze.8.refs_1_.refs_2_, ...), custom_call_target="tpu_custom_call" | custom-call | flops 1610612736 | bytes 2359296 | tf_op jit(solution)/shard_map/pallas_call | solution.py:163
  133.5 6.8 %shard_map.103 = bf16[2,8,1536]{2,1,0:T(8,128)(2,1)} custom-call(s32[4]{0:T(128)} %get-tuple-element.23.flags_ref, bf16[1,256,1536]{2,1,0:T(8,128)(2,1)} %bitcast.27, f32[2,1,1536]{2,1,0:T(1,128)} %reshape_squeeze.8.refs_1_.refs_2_, f32[2,1,1536]{2,1,0:T(1,128)} %reshape_squeeze.9.refs_2_.refs_3_, ...), custom_call_target="tpu_custom_call", output_to_operand_aliasing={{}: (8, {})} | custom-call | flops 1610612736 | bytes 2359296 | tf_op jit(solution)/shard_map/pallas_call | solution.py:163
  (1 shorter events, 0.0 us)
Async XLA Ops:
  6.5 80.8 %all-gather.2.cloned.1.call-start = ((), (), s32[]{:S(2)}) async-start(), calls=%async_computation | async-start | bytes 4866048 | tf_op jit(solution)/shard_map/all_gather | solution.py:241
  104.7 14.7 %collective-permute-start = (bf16[128,1536]{1,0:T(8,128)(2,1)}, bf16[128,1536]{1,0:T(8,128)(2,1)S(1)}, u32[]{:S(2)}, u32[]{:S(2)}) collective-permute-start(bf16[128,1536]{1,0:T(8,128)(2,1)} %get-tuple-element.13), channel_id=1, source_target_pairs={{0,32},{32,64},{64,96},{96,128},{128,160},{160,192},{192,224},{224... | collective-permute-start | bytes 1179656 | tf_op jit(solution)/shard_map/ppermute | solution.py:275
  119.4 4.3 %collective-permute-start.1 = (bf16[128,1536]{1,0:T(8,128)(2,1)S(1)}, bf16[128,1536]{1,0:T(8,128)(2,1)S(1)}, u32[]{:S(2)}, u32[]{:S(2)}) collective-permute-start(bf16[128,1536]{1,0:T(8,128)(2,1)S(1)} %collective-permute-done), channel_id=1, source_target_pairs={{0,1},{1,0},{2,3},{3,2},{4,5},{5,4},{6,7},{7,6},{8,9},{9,8},{10,11... | collective-permute-start | bytes 1179656 | tf_op jit(solution)/shard_map/ppermute | solution.py:277
Sparse Core Ops, SparseCore 0:
  13.9 73.4 all-gather.1

commit v13 on v11

--- a/solution.py
+++ b/solution.py
@@ -207,9 +207,17 @@
     for turn in range(1, patch_count):
         entry_rows.append(pick_patch(perturbed_frame_activation, tile_arrival_permutation[turn], 0)[None])
     other_patch = arrival(jnp.mod(1 - segment, patch_count))
-    far_k = pick_patch(earlier_step_lookup_matrix[0], other_patch, 1)
-    far_v = pick_patch(earlier_step_content_matrix[0], other_patch, 1)
-    packed = jnp.concatenate(entry_rows + [far_k, far_v], axis=0)
+    candidates = [
+        jnp.concatenate(
+            entry_rows
+            + [earlier_step_lookup_matrix[0, :, patch], earlier_step_content_matrix[0, :, patch]],
+            axis=0,
+        )
+        for patch in range(patch_count)
+    ]
+    packed = candidates[0]
+    for patch in range(1, patch_count):
+        packed = jnp.where(other_patch == patch, candidates[patch], packed)
     whole = lax.all_gather(packed, "ctx", axis=1, tiled=True)
     params = [
         adaptive_shifting[0],

time: 141 us -> 140 us (level)
    unnamed x2 -> x0, local copies, waits for them, and re-layouts: 1.8 us -> none
where the time goes in v13:
time: 140 us; the launch traced here: 139 us
  waiting for transfers between devices  80.4 us (57%)
  Pallas kernels  25.7 us (18%)
  between operations  16.6 us (12%)
  local copies, waits for them, and re-layouts  7.48 us (5%)
  starting transfers between devices  5.61 us (4%)
  other arithmetic  3.24 us (2%)
    all_gather x1, waiting for transfers between devices, per_device(): whole = lax.all_gather(packed, 'ctx', axis=1, tiled=True)  67 us
    pallas_call x4, Pallas kernels, fused_layer(): pl.pallas_call(functools.partial(layer_kernel, two_sources=entry is not N...  25.7 us
    ppermute x1, waiting for transfers between devices, per_device(): got = lax.ppermute(sent, 'segment', [(i, i + 1) for i in range(count - 1)])  12.2 us
    another operation x4, local copies, waits for them, and re-layouts, fused_layer(): p.reshape(p.shape[0], 1, width)  5.25 us
    ppermute x1, starting transfers between devices, per_device(): swapped = lax.ppermute(got, 'ctx', [(c, c ^ 1) for c in range(ctx_count)])  3.14 us
  transfers between devices with their start and end apart: 3, of which 3 were waited for; matrix products, arithmetic and copies ran while one was open for 4% of the time, Pallas kernels for 0%

profile of v13, /device:TPU:33, one launch (start us, length us, event | category | flops | bytes accessed | tf_op | source)
XLA Modules:
  0.0 139.0 jit_solution(10734947529210985838)
XLA Ops:
  6.5 0.0 all-gather.2.cloned.1.call-start
  6.5 1.3 fusion
  10.4 0.9 slice_bitcast_fusion
  11.3 0.8 select_select_fusion
  12.1 0.7 maximum_select_fusion.1
  12.8 0.0 all-gather.2.cloned.1.call-update
  13.5 1.3 reshape_squeeze.8.refs_1_.refs_2_
  14.8 1.3 reshape_squeeze.9.refs_2_.refs_3_
  16.1 1.3 reshape_squeeze.10.refs_3_.refs_4_
  17.4 1.3 reshape_squeeze.11.refs_4_.refs_5_
  18.8 0.6 add_add_fusion
  19.4 67.0 %all-gather.2.cloned.1.call-done.refs_0_.refs_5_.refs_6_.refs_1_ = bf16[6,256,1536]{2,1,0:T(8,128)(2,1)} async-done(((bf16[6,8,1536]{2,1,0:T(8,128)(2,1)}), bf16[6,256,1536]{2,1,0:T(8,128)(2,1)}) %all-gather.2.cloned.1.call-update) | async-done | bytes 4718608 | tf_op jit(solution)/shard_map/all_gather | solution.py:221
  86.4 6.7 %shard_map.100 = (bf16[256,1536]{1,0:T(8,128)(2,1)}, bf16[256,1536]{1,0:T(8,128)(2,1)}, bf16[256,1536]{1,0:T(8,128)(2,1)}) custom-call(s32[4]{0:T(128)} %get-tuple-element.28.flags_ref, bf16[6,256,1536]{2,1,0:T(8,128)(2,1)} %all-gather.2.cloned.1.call-done.refs_0_.refs_5_.refs_6_.refs_1_, f32[2,1,1536]{2,1,0:T(1,128)} %reshape_squeeze.8.refs_1_.refs_2_, ...), custom_call_target="tpu_custom_call" | custom-call | flops 1610612736 | bytes 3932160 | tf_op jit(solution)/shard_map/pallas_call | solution.py:144
  93.1 6.8 %shard_map.101 = (bf16[256,1536]{1,0:T(8,128)(2,1)}, bf16[256,1536]{1,0:T(8,128)(2,1)}, bf16[256,1536]{1,0:T(8,128)(2,1)}, bf16[128,1536]{1,0:T(8,128)(2,1)}, bf16[2,8,1536]{2,1,0:T(8,128)(2,1)}) custom-call(s32[4]{0:T(128)} %get-tuple-element.27.flags_ref, bf16[1,256,1536]{2,1,0:T(8,128)(2,1)} %bitcast.30, f32[2,1,1536]{2,1,0:T(1,128)} %reshape_squeeze.8.refs_1_.refs_2_, ...), custom_call_target="tpu_custom_call" | custom-call | flops 1610612736 | bytes 3932160 | tf_op jit(solution)/shard_map/pallas_call | solution.py:144
  99.9 2.5 %collective-permute-start = (bf16[128,1536]{1,0:T(8,128)(2,1)}, bf16[128,1536]{1,0:T(8,128)(2,1)S(1)}, u32[]{:S(2)}, u32[]{:S(2)}) collective-permute-start(bf16[128,1536]{1,0:T(8,128)(2,1)} %get-tuple-element.13), channel_id=1, source_target_pairs={{0,32},{32,64},{64,96},{96,128},{128,160},{160,192},{192,224},{224... | collective-permute-start | bytes 1179656 | tf_op jit(solution)/shard_map/ppermute | solution.py:255
  102.4 12.2 %collective-permute-done = bf16[128,1536]{1,0:T(8,128)(2,1)S(1)} collective-permute-done((bf16[128,1536]{1,0:T(8,128)(2,1)}, bf16[128,1536]{1,0:T(8,128)(2,1)S(1)}, u32[]{:S(2)}, u32[]{:S(2)}) %collective-permute-start) | collective-permute-done | bytes 393248 | tf_op jit(solution)/shard_map/ppermute | solution.py:255
  114.6 3.1 %collective-permute-start.1 = (bf16[128,1536]{1,0:T(8,128)(2,1)S(1)}, bf16[128,1536]{1,0:T(8,128)(2,1)S(1)}, u32[]{:S(2)}, u32[]{:S(2)}) collective-permute-start(bf16[128,1536]{1,0:T(8,128)(2,1)S(1)} %collective-permute-done), channel_id=1, source_target_pairs={{0,1},{1,0},{2,3},{3,2},{4,5},{5,4},{6,7},{7,6},{8,9},{9,8},{10,11... | collective-permute-start | bytes 1179656 | tf_op jit(solution)/shard_map/ppermute | solution.py:257
  117.7 1.1 collective-permute-done.1
  118.9 1.1 maximum_select_fusion.refs_0_
  120.0 6.9 %shard_map.102 = bf16[256,1536]{1,0:T(8,128)(2,1)} custom-call(s32[4]{0:T(128)} %get-tuple-element.28.flags_ref, bf16[1,256,1536]{2,1,0:T(8,128)(2,1)} %maximum_select_fusion.refs_0_, bf16[6,256,1536]{2,1,0:T(8,128)(2,1)} %all-gather.2.cloned.1.call-done.refs_0_.refs_5_.refs_6_.refs_1_, f32[2,1,1536]{2,1,0:T(1,128)} %reshape_squeeze.8.refs_1_.refs_2_, ...), custom_call_target="tpu_custom_call" | custom-call | flops 1610612736 | bytes 2359296 | tf_op jit(solution)/shard_map/pallas_call | solution.py:144
  126.9 5.3 %shard_map.103 = bf16[2,8,1536]{2,1,0:T(8,128)(2,1)} custom-call(s32[4]{0:T(128)} %get-tuple-element.27.flags_ref, bf16[1,256,1536]{2,1,0:T(8,128)(2,1)} %bitcast.33, f32[2,1,1536]{2,1,0:T(1,128)} %reshape_squeeze.8.refs_1_.refs_2_, f32[2,1,1536]{2,1,0:T(1,128)} %reshape_squeeze.9.refs_2_.refs_3_, ...), custom_call_target="tpu_custom_call", output_to_operand_aliasing={{}: (8, {})} | custom-call | flops 1610612736 | bytes 2359296 | tf_op jit(solution)/shard_map/pallas_call | solution.py:144
Async XLA Ops:
  6.5 79.9 %all-gather.2.cloned.1.call-start = ((), (), s32[]{:S(2)}) async-start(), calls=%async_computation | async-start | bytes 4866048 | tf_op jit(solution)/shard_map/all_gather | solution.py:221
  99.9 14.7 %collective-permute-start = (bf16[128,1536]{1,0:T(8,128)(2,1)}, bf16[128,1536]{1,0:T(8,128)(2,1)S(1)}, u32[]{:S(2)}, u32[]{:S(2)}) collective-permute-start(bf16[128,1536]{1,0:T(8,128)(2,1)} %get-tuple-element.13), channel_id=1, source_target_pairs={{0,32},{32,64},{64,96},{96,128},{128,160},{160,192},{192,224},{224... | collective-permute-start | bytes 1179656 | tf_op jit(solution)/shard_map/ppermute | solution.py:255
  114.6 4.3 %collective-permute-start.1 = (bf16[128,1536]{1,0:T(8,128)(2,1)S(1)}, bf16[128,1536]{1,0:T(8,128)(2,1)S(1)}, u32[]{:S(2)}, u32[]{:S(2)}) collective-permute-start(bf16[128,1536]{1,0:T(8,128)(2,1)S(1)} %collective-permute-done), channel_id=1, source_target_pairs={{0,1},{1,0},{2,3},{3,2},{4,5},{5,4},{6,7},{7,6},{8,9},{9,8},{10,11... | collective-permute-start | bytes 1179656 | tf_op jit(solution)/shard_map/ppermute | solution.py:257
Sparse Core Ops, SparseCore 0:
  13.0 73.4 all-gather.1

commit v14 on v13

--- a/solution.py
+++ b/solution.py
@@ -16,13 +16,21 @@
     return values * lax.rsqrt(jnp.mean(values * values, axis=-1, keepdims=True) + EPSILON)
 
 
-def layer_kernel(flags_ref, *refs, two_sources, keep_kv, query_rows, emit_rows, aliased):
+def layer_kernel(flags_ref, *refs, two_sources, keep_kv, query_rows, emit_rows, aliased, halves):
+    if halves:
+        received_ref, partner_ref, *refs = refs
+        received_first = flags_ref[3] == 0
+        received, partner = received_ref[...], partner_ref[...]
+        arrived = jnp.concatenate(
+            [jnp.where(received_first, received, partner), jnp.where(received_first, partner, received)],
+            axis=0,
+        )
+    else:
+        full_ref, *refs = refs
+        x_ref = full_ref
     if two_sources:
-        full_ref, entry_full_ref, *refs = refs
+        entry_full_ref, *refs = refs
         entry_x_ref = entry_full_ref
-    else:
-        full_ref, *refs = refs
-    x_ref = full_ref
     shift_ref, stretch_ref, factor_ref, skip_ref, kf_ref, vf_ref, *refs = refs
     if aliased:
         refs = refs[1:]
@@ -31,8 +39,12 @@
     live = flags_ref[0] > 0
     scale = 1.0 / math.sqrt(HD)
     dims = (((1,), (1,)), ((), ()))
-    whole = full_ref[...]
-    state = x_ref[...]
+    if halves:
+        assert query_rows is None
+        whole = state = arrived
+    else:
+        whole = full_ref[...]
+        state = x_ref[...]
     if two_sources:
         use_entry = flags_ref[1] > 0
         whole = jnp.where(use_entry, entry_full_ref[...], whole)
@@ -95,8 +107,13 @@
     emit_rows=None,
     into=None,
 ):
-    array, slab = source
-    _, tokens, width = array.shape
+    halves = isinstance(source, list)
+    if halves:
+        tokens = source[0].shape[0] * 2
+        width = source[0].shape[1]
+    else:
+        array, slab = source
+        _, tokens, width = array.shape
     block = width
 
     def slab_specs(slab_index):
@@ -106,8 +123,12 @@
         return pl.BlockSpec((None, tokens, block), lambda i, f: (slab_index, 0, i))
 
     line = pl.BlockSpec((None, 1, block), lambda i, f: (tier, 0, i))
-    in_specs = slab_specs(slab)
-    operands = [array]
+    if halves:
+        in_specs = [pl.BlockSpec((tokens // 2, width), lambda i, f: (0, 0))] * 2
+        operands = list(source)
+    else:
+        in_specs = slab_specs(slab)
+        operands = [array]
     if entry is not None:
         in_specs += slab_specs(entry[1])
         operands += [entry[0]]
@@ -149,6 +170,7 @@
             query_rows=query_rows,
             emit_rows=emit_rows is not None,
             aliased=into is not None,
+            halves=halves,
         ),
         out_shape=out_shapes,
         grid_spec=pltpu.PrefetchScalarGridSpec(
@@ -255,12 +277,7 @@
         got = lax.ppermute(sent, "segment", [(i, i + 1) for i in range(count - 1)])
         ctx_count = lax.axis_size("ctx")
         swapped = lax.ppermute(got, "ctx", [(c, c ^ 1) for c in range(ctx_count)])
-        arrived = jnp.where(
-            core == 0,
-            jnp.concatenate([got, swapped], axis=0),
-            jnp.concatenate([swapped, got], axis=0),
-        )
-        source = (arrived[None], 0)
+        source = [got, swapped]
         entry = (whole, turn)
         for tier in range(slot_count):
             last = tier == slot_count - 1

time: 140 us -> 139 us (level)
  no operation moved by 1% of the time
where the time goes in v14:
time: 139 us
  waiting for transfers between devices  80.4 us (58%)
  Pallas kernels  25.7 us (18%)
  between operations  16.7 us (12%)
  local copies, waits for them, and re-layouts  8.26 us (6%)
  starting transfers between devices  5.6 us (4%)
  other arithmetic  2.1 us (2%)
    all_gather x1, waiting for transfers between devices, per_device(): whole = lax.all_gather(packed, 'ctx', axis=1, tiled=True)  67 us
    pallas_call x4, Pallas kernels, fused_layer(): pl.pallas_call(functools.partial(layer_kernel, two_sources=entry is not N...  25.7 us
    ppermute x1, waiting for transfers between devices, per_device(): got = lax.ppermute(sent, 'segment', [(i, i + 1) for i in range(count - 1)])  12.2 us
    another operation x4, local copies, waits for them, and re-layouts, fused_layer(): p.reshape(p.shape[0], 1, width)  5.25 us
    ppermute x1, starting transfers between devices, per_device(): swapped = lax.ppermute(got, 'ctx', [(c, c ^ 1) for c in range(ctx_count)])  3.12 us
  transfers between devices with their start and end apart: 3, of which 3 were waited for; matrix products, arithmetic and copies ran while one was open for 4% of the time, Pallas kernels for 0%

profile of v14, /device:TPU:33, one launch (start us, length us, event | category | flops | bytes accessed | tf_op | source)
XLA Modules:
  0.0 138.7 jit_solution(2825965629263004913)
XLA Ops:
  6.5 0.0 all-gather.2.cloned.1.call-start
  6.5 1.3 fusion
  10.4 0.9 slice_bitcast_fusion
  11.3 0.8 select_select_fusion
  12.1 0.7 maximum_select_fusion
  12.8 0.0 all-gather.2.cloned.1.call-update
  13.5 1.3 reshape_squeeze.8.refs_1_.refs_3_
  14.8 1.3 reshape_squeeze.9.refs_2_.refs_4_
  16.1 1.3 reshape_squeeze.10.refs_3_.refs_5_
  17.4 1.3 reshape_squeeze.11.refs_4_.refs_6_
  18.8 0.6 add_add_fusion
  19.4 67.0 %all-gather.2.cloned.1.call-done.refs_0_.refs_5_.refs_6_.refs_2_ = bf16[6,256,1536]{2,1,0:T(8,128)(2,1)} async-done(((bf16[6,8,1536]{2,1,0:T(8,128)(2,1)}), bf16[6,256,1536]{2,1,0:T(8,128)(2,1)}) %all-gather.2.cloned.1.call-update) | async-done | bytes 4718608 | tf_op jit(solution)/shard_map/all_gather | solution.py:243
  86.4 6.7 %shard_map.100 = (bf16[256,1536]{1,0:T(8,128)(2,1)}, bf16[256,1536]{1,0:T(8,128)(2,1)}, bf16[256,1536]{1,0:T(8,128)(2,1)}) custom-call(s32[4]{0:T(128)} %get-tuple-element.28.flags_ref, bf16[6,256,1536]{2,1,0:T(8,128)(2,1)} %all-gather.2.cloned.1.call-done.refs_0_.refs_5_.refs_6_.refs_2_, f32[2,1,1536]{2,1,0:T(1,128)} %reshape_squeeze.8.refs_1_.refs_3_, ...), custom_call_target="tpu_custom_call" | custom-call | flops 1610612736 | bytes 3932160 | tf_op jit(solution)/shard_map/pallas_call | solution.py:165
  93.1 6.8 %shard_map.101 = (bf16[256,1536]{1,0:T(8,128)(2,1)}, bf16[256,1536]{1,0:T(8,128)(2,1)}, bf16[256,1536]{1,0:T(8,128)(2,1)}, bf16[128,1536]{1,0:T(8,128)(2,1)}, bf16[2,8,1536]{2,1,0:T(8,128)(2,1)}) custom-call(s32[4]{0:T(128)} %get-tuple-element.27.flags_ref, bf16[1,256,1536]{2,1,0:T(8,128)(2,1)} %bitcast.28, f32[2,1,1536]{2,1,0:T(1,128)} %reshape_squeeze.8.refs_1_.refs_3_, ...), custom_call_target="tpu_custom_call" | custom-call | flops 1610612736 | bytes 3932160 | tf_op jit(solution)/shard_map/pallas_call | solution.py:165
  99.9 2.5 %collective-permute-start = (bf16[128,1536]{1,0:T(8,128)(2,1)}, bf16[128,1536]{1,0:T(8,128)(2,1)S(1)}, u32[]{:S(2)}, u32[]{:S(2)}) collective-permute-start(bf16[128,1536]{1,0:T(8,128)(2,1)} %get-tuple-element.13), channel_id=1, source_target_pairs={{0,32},{32,64},{64,96},{96,128},{128,160},{160,192},{192,224},{224... | collective-permute-start | bytes 1179656 | tf_op jit(solution)/shard_map/ppermute | solution.py:277
  102.4 12.2 %collective-permute-done.refs_0_ = bf16[128,1536]{1,0:T(8,128)(2,1)S(1)} collective-permute-done((bf16[128,1536]{1,0:T(8,128)(2,1)}, bf16[128,1536]{1,0:T(8,128)(2,1)S(1)}, u32[]{:S(2)}, u32[]{:S(2)}) %collective-permute-start) | collective-permute-done | bytes 393248 | tf_op jit(solution)/shard_map/ppermute | solution.py:277
  114.6 0.0 copy-start
  114.6 3.1 %collective-permute-start.1 = (bf16[128,1536]{1,0:T(8,128)(2,1)S(1)}, bf16[128,1536]{1,0:T(8,128)(2,1)S(1)}, u32[]{:S(2)}, u32[]{:S(2)}) collective-permute-start(bf16[128,1536]{1,0:T(8,128)(2,1)S(1)} %collective-permute-done.refs_0_), channel_id=1, source_target_pairs={{0,1},{1,0},{2,3},{3,2},{4,5},{5,4},{6,7},{7,6},{8,9},{9,8},{10,11... | collective-permute-start | bytes 1179656 | tf_op jit(solution)/shard_map/ppermute | solution.py:279
  117.7 1.1 collective-permute-done.1.refs_1_
  118.9 0.0 copy-start.1
  118.9 0.0 copy-done
  118.9 0.8 copy-done.1
  119.7 6.9 %shard_map.102 = bf16[256,1536]{1,0:T(8,128)(2,1)} custom-call(s32[4]{0:T(128)} %get-tuple-element.28.flags_ref, bf16[128,1536]{1,0:T(8,128)(2,1)} %copy-done, bf16[128,1536]{1,0:T(8,128)(2,1)} %copy-done.1, bf16[6,256,1536]{2,1,0:T(8,128)(2,1)} %all-gather.2.cloned.1.call-done.refs_0_.refs_5_.refs_6_.refs_2_, f32[2,1,1536]{2,1,0:T(1,128)} %reshape_squeeze.8.refs_1_.refs_3_, ...), custom_call_target="tpu_custom_call" | custom-call | flops 1610612736 | bytes 2359296 | tf_op jit(solution)/shard_map/pallas_call | solution.py:165
  126.6 5.3 %shard_map.103 = bf16[2,8,1536]{2,1,0:T(8,128)(2,1)} custom-call(s32[4]{0:T(128)} %get-tuple-element.27.flags_ref, bf16[1,256,1536]{2,1,0:T(8,128)(2,1)} %bitcast.31, f32[2,1,1536]{2,1,0:T(1,128)} %reshape_squeeze.8.refs_1_.refs_3_, f32[2,1,1536]{2,1,0:T(1,128)} %reshape_squeeze.9.refs_2_.refs_4_, ...), custom_call_target="tpu_custom_call", output_to_operand_aliasing={{}: (8, {})} | custom-call | flops 1610612736 | bytes 2359296 | tf_op jit(solution)/shard_map/pallas_call | solution.py:165
Async XLA Ops:
  6.5 79.9 %all-gather.2.cloned.1.call-start = ((), (), s32[]{:S(2)}) async-start(), calls=%async_computation | async-start | bytes 4866048 | tf_op jit(solution)/shard_map/all_gather | solution.py:243
  99.9 14.7 %collective-permute-start = (bf16[128,1536]{1,0:T(8,128)(2,1)}, bf16[128,1536]{1,0:T(8,128)(2,1)S(1)}, u32[]{:S(2)}, u32[]{:S(2)}) collective-permute-start(bf16[128,1536]{1,0:T(8,128)(2,1)} %get-tuple-element.13), channel_id=1, source_target_pairs={{0,32},{32,64},{64,96},{96,128},{128,160},{160,192},{192,224},{224... | collective-permute-start | bytes 1179656 | tf_op jit(solution)/shard_map/ppermute | solution.py:277
  114.6 4.3 %copy-start = (bf16[128,1536]{1,0:T(8,128)(2,1)}, bf16[128,1536]{1,0:T(8,128)(2,1)S(1)}, u32[]{:S(2)}) copy-start(bf16[128,1536]{1,0:T(8,128)(2,1)S(1)} %collective-permute-done.refs_0_) | copy-start | bytes 1179652
  114.6 4.3 %collective-permute-start.1 = (bf16[128,1536]{1,0:T(8,128)(2,1)S(1)}, bf16[128,1536]{1,0:T(8,128)(2,1)S(1)}, u32[]{:S(2)}, u32[]{:S(2)}) collective-permute-start(bf16[128,1536]{1,0:T(8,128)(2,1)S(1)} %collective-permute-done.refs_0_), channel_id=1, source_target_pairs={{0,1},{1,0},{2,3},{3,2},{4,5},{5,4},{6,7},{7,6},{8,9},{9,8},{10,11... | collective-permute-start | bytes 1179656 | tf_op jit(solution)/shard_map/ppermute | solution.py:279
  118.9 0.8 copy-start.1
Sparse Core Ops, SparseCore 0:
  13.0 73.4 all-gather.1

commit v15 on v14

--- a/solution.py
+++ b/solution.py
@@ -34,8 +34,14 @@
     shift_ref, stretch_ref, factor_ref, skip_ref, kf_ref, vf_ref, *refs = refs
     if aliased:
         refs = refs[1:]
-    o_ref, *refs = refs
-    kv_refs = refs[:2] if keep_kv else ()
+    if emit_rows:
+        k_ref, v_ref, half_ref, rows_ref = refs
+        kv_refs = (k_ref, v_ref)
+        query_sets = [(flags_ref[3], half_ref), (flags_ref[2], rows_ref)]
+    else:
+        o_ref, *refs = refs
+        kv_refs = refs[:2] if keep_kv else ()
+        query_sets = [(None if query_rows is None else flags_ref[2], o_ref)]
     live = flags_ref[0] > 0
     scale = 1.0 / math.sqrt(HD)
     dims = (((1,), (1,)), ((), ()))
@@ -49,49 +55,53 @@
         use_entry = flags_ref[1] > 0
         whole = jnp.where(use_entry, entry_full_ref[...], whole)
         state = jnp.where(use_entry, entry_x_ref[...], state)
+
     def row_scale_of(rows_value):
         rows_value = rows_value.astype(jnp.float32)
         return lax.rsqrt(jnp.mean(rows_value * rows_value, axis=-1, keepdims=True) + EPSILON)
 
     row_scale = row_scale_of(whole)
-    if query_rows is None:
-        state_q, row_scale_q = state, row_scale
-    else:
-        start = pl.multiple_of(flags_ref[2], query_rows)
-        state_q = x_ref[pl.ds(start, query_rows), :]
-        row_scale_q = row_scale_of(full_ref[pl.ds(start, query_rows), :])
+    picked = []
+    for start, out_ref in query_sets:
+        if start is None:
+            picked.append((state, row_scale, out_ref, False))
+        else:
+            count = out_ref.shape[0]
+            start = pl.multiple_of(start, count)
+            picked.append(
+                (
+                    x_ref[pl.ds(start, count), :],
+                    row_scale_of(full_ref[pl.ds(start, count), :]),
+                    out_ref,
+                    True,
+                )
+            )
     for j in range(state.shape[1] // HD):
         cols = slice(j * HD, (j + 1) * HD)
         stretch = 1.0 + stretch_ref[:, cols]
         x_all = state[:, cols].astype(jnp.float32)
-        hidden = x_all * row_scale * stretch + shift_ref[:, cols]
-        fresh_key = head_norm(hidden * factor_ref[:, cols]).astype(jnp.bfloat16)
-        fresh_value = hidden.astype(jnp.bfloat16)
-        x_rounded = state_q[:, cols]
-        x = x_rounded.astype(jnp.float32)
-        if query_rows is not None:
-            hidden = x * row_scale_q * stretch + shift_ref[:, cols]
-        query = head_norm(hidden).astype(jnp.bfloat16)
-        if keep_kv:
+        hidden_all = x_all * row_scale * stretch + shift_ref[:, cols]
+        fresh_key = head_norm(hidden_all * factor_ref[:, cols]).astype(jnp.bfloat16)
+        fresh_value = hidden_all.astype(jnp.bfloat16)
+        if kv_refs:
             kv_refs[0][:, cols] = fresh_key
             kv_refs[1][:, cols] = fresh_value
-        near = lax.dot_general(query, fresh_key, dims, preferred_element_type=jnp.float32) * scale
-        far = lax.dot_general(query, kf_ref[:, cols], dims, preferred_element_type=jnp.float32) * scale
-        near = jnp.exp(near)
-        far = jnp.exp(far)
-        total = jnp.sum(near, axis=-1, keepdims=True) + jnp.sum(far, axis=-1, keepdims=True)
-        numerator = jnp.dot(
-            near.astype(jnp.bfloat16), fresh_value, preferred_element_type=jnp.float32
-        ) + jnp.dot(far.astype(jnp.bfloat16), vf_ref[:, cols], preferred_element_type=jnp.float32)
-        attended = numerator / total
-        new_state = (x + skip_ref[:, cols] * attended).astype(o_ref.dtype)
-        o_ref[:, cols] = jnp.where(live, new_state, x_rounded)
-    if emit_rows:
-        half_ref, rows_ref = refs[len(kv_refs) :]
-        half = half_ref.shape[0]
-        rows = rows_ref.shape[0]
-        half_ref[...] = o_ref[pl.ds(pl.multiple_of(flags_ref[3], half), half), :]
-        rows_ref[...] = o_ref[pl.ds(pl.multiple_of(flags_ref[2], rows), rows), :]
+        for state_q, row_scale_q, out_ref, separate in picked:
+            x_rounded = state_q[:, cols]
+            x = x_rounded.astype(jnp.float32)
+            hidden = x * row_scale_q * stretch + shift_ref[:, cols] if separate else hidden_all
+            query = head_norm(hidden).astype(jnp.bfloat16)
+            near = lax.dot_general(query, fresh_key, dims, preferred_element_type=jnp.float32) * scale
+            far = lax.dot_general(query, kf_ref[:, cols], dims, preferred_element_type=jnp.float32) * scale
+            near = jnp.exp(near)
+            far = jnp.exp(far)
+            total = jnp.sum(near, axis=-1, keepdims=True) + jnp.sum(far, axis=-1, keepdims=True)
+            numerator = jnp.dot(
+                near.astype(jnp.bfloat16), fresh_value, preferred_element_type=jnp.float32
+            ) + jnp.dot(far.astype(jnp.bfloat16), vf_ref[:, cols], preferred_element_type=jnp.float32)
+            attended = numerator / total
+            new_state = (x + skip_ref[:, cols] * attended).astype(out_ref.dtype)
+            out_ref[:, cols] = jnp.where(live, new_state, x_rounded)
 
 
 def fused_layer(
@@ -153,7 +163,9 @@
         out_shapes = (jax.ShapeDtypeStruct(buffer.shape, buffer.dtype),)
         out_specs = (pl.BlockSpec((None, query_rows, block), lambda i, f: (slot, 0, i)),)
     if emit_rows is not None:
+        assert keep_kv and entry is None and query_rows is None and not halves
         half, rows, slots = emit_rows
+        out_shapes, out_specs = out_shapes[1:], out_specs[1:]
         out_shapes += (
             jax.ShapeDtypeStruct((half, width), jnp.bfloat16),
             jax.ShapeDtypeStruct((slots, rows, width), jnp.bfloat16),
@@ -268,10 +280,12 @@
             (whole, patch_count + slot_count + tier),
             emit_rows=(half, rows, patch_count) if last else None,
         )
-        state, fresh_key, fresh_value = results[:3]
-        source = (state[None], 0)
+        if last:
+            fresh_key, fresh_value, sent, outcomes = results
+        else:
+            state, fresh_key, fresh_value = results
+            source = (state[None], 0)
         turn_zero_kv.append(((fresh_key[None], 0), (fresh_value[None], 0)))
-    sent, outcomes = results[3:]
     count = lax.axis_size("segment")
     for turn in range(1, patch_count):
         got = lax.ppermute(sent, "segment", [(i, i + 1) for i in range(count - 1)])

time: 139 us -> 140 us (level)
  no operation moved by 1% of the time
where the time goes in v15:
time: 140 us; the launch traced here: 139 us
  waiting for transfers between devices  80.4 us (57%)
  Pallas kernels  26.4 us (19%)
  between operations  16.6 us (12%)
  local copies, waits for them, and re-layouts  8.25 us (6%)
  starting transfers between devices  5.6 us (4%)
  other arithmetic  2.12 us (2%)
    all_gather x1, waiting for transfers between devices, per_device(): whole = lax.all_gather(packed, 'ctx', axis=1, tiled=True)  67 us
    pallas_call x4, Pallas kernels, fused_layer(): pl.pallas_call(functools.partial(layer_kernel, two_sources=entry is not N...  26.4 us
    ppermute x1, waiting for transfers between devices, per_device(): got = lax.ppermute(sent, 'segment', [(i, i + 1) for i in range(count - 1)])  12.2 us
    another operation x4, local copies, waits for them, and re-layouts, fused_layer(): p.reshape(p.shape[0], 1, width)  5.24 us
    ppermute x1, starting transfers between devices, per_device(): swapped = lax.ppermute(got, 'ctx', [(c, c ^ 1) for c in range(ctx_count)])  3.12 us
  transfers between devices with their start and end apart: 3, of which 3 were waited for; matrix products, arithmetic and copies ran while one was open for 4% of the time, Pallas kernels for 0%

profile of v15, /device:TPU:33, one launch (start us, length us, event | category | flops | bytes accessed | tf_op | source)
XLA Modules:
  0.0 139.4 jit_solution(16968245798581249008)
XLA Ops:
  6.5 0.0 all-gather.2.cloned.1.call-start
  6.5 1.3 fusion
  10.4 0.9 slice_bitcast_fusion
  11.3 0.8 select_select_fusion
  12.1 0.7 maximum_select_fusion
  12.8 0.0 all-gather.2.cloned.1.call-update
  13.5 1.3 reshape_squeeze.8.refs_1_.refs_3_
  14.8 1.3 reshape_squeeze.9.refs_2_.refs_4_
  16.1 1.3 reshape_squeeze.10.refs_3_.refs_5_
  17.4 1.3 reshape_squeeze.11.refs_4_.refs_6_
  18.7 0.6 add_add_fusion
  19.4 67.0 %all-gather.2.cloned.1.call-done.refs_0_.refs_5_.refs_6_.refs_2_ = bf16[6,256,1536]{2,1,0:T(8,128)(2,1)} async-done(((bf16[6,8,1536]{2,1,0:T(8,128)(2,1)}), bf16[6,256,1536]{2,1,0:T(8,128)(2,1)}) %all-gather.2.cloned.1.call-update) | async-done | bytes 4718608 | tf_op jit(solution)/shard_map/all_gather | solution.py:255
  86.4 6.6 %shard_map.100 = (bf16[256,1536]{1,0:T(8,128)(2,1)}, bf16[256,1536]{1,0:T(8,128)(2,1)}, bf16[256,1536]{1,0:T(8,128)(2,1)}) custom-call(s32[4]{0:T(128)} %get-tuple-element.28.flags_ref, bf16[6,256,1536]{2,1,0:T(8,128)(2,1)} %all-gather.2.cloned.1.call-done.refs_0_.refs_5_.refs_6_.refs_2_, f32[2,1,1536]{2,1,0:T(1,128)} %reshape_squeeze.8.refs_1_.refs_3_, ...), custom_call_target="tpu_custom_call" | custom-call | flops 1610612736 | bytes 3932160 | tf_op jit(solution)/shard_map/pallas_call | solution.py:177
  93.0 7.6 %shard_map.101 = (bf16[256,1536]{1,0:T(8,128)(2,1)}, bf16[256,1536]{1,0:T(8,128)(2,1)}, bf16[128,1536]{1,0:T(8,128)(2,1)}, bf16[2,8,1536]{2,1,0:T(8,128)(2,1)}) custom-call(s32[4]{0:T(128)} %get-tuple-element.27.flags_ref, bf16[1,256,1536]{2,1,0:T(8,128)(2,1)} %bitcast.28, f32[2,1,1536]{2,1,0:T(1,128)} %reshape_squeeze.8.refs_1_.refs_3_, ...), custom_call_target="tpu_custom_call" | custom-call | flops 1610612736 | bytes 3932160 | tf_op jit(solution)/shard_map/pallas_call | solution.py:177
  100.7 2.5 %collective-permute-start = (bf16[128,1536]{1,0:T(8,128)(2,1)}, bf16[128,1536]{1,0:T(8,128)(2,1)S(1)}, u32[]{:S(2)}, u32[]{:S(2)}) collective-permute-start(bf16[128,1536]{1,0:T(8,128)(2,1)} %get-tuple-element.13), channel_id=1, source_target_pairs={{0,32},{32,64},{64,96},{96,128},{128,160},{160,192},{192,224},{224... | collective-permute-start | bytes 1179656 | tf_op jit(solution)/shard_map/ppermute | solution.py:291
  103.2 12.2 %collective-permute-done.refs_0_ = bf16[128,1536]{1,0:T(8,128)(2,1)S(1)} collective-permute-done((bf16[128,1536]{1,0:T(8,128)(2,1)}, bf16[128,1536]{1,0:T(8,128)(2,1)S(1)}, u32[]{:S(2)}, u32[]{:S(2)}) %collective-permute-start) | collective-permute-done | bytes 393248 | tf_op jit(solution)/shard_map/ppermute | solution.py:291
  115.4 0.0 copy-start
  115.4 3.1 %collective-permute-start.1 = (bf16[128,1536]{1,0:T(8,128)(2,1)S(1)}, bf16[128,1536]{1,0:T(8,128)(2,1)S(1)}, u32[]{:S(2)}, u32[]{:S(2)}) collective-permute-start(bf16[128,1536]{1,0:T(8,128)(2,1)S(1)} %collective-permute-done.refs_0_), channel_id=1, source_target_pairs={{0,1},{1,0},{2,3},{3,2},{4,5},{5,4},{6,7},{7,6},{8,9},{9,8},{10,11... | collective-permute-start | bytes 1179656 | tf_op jit(solution)/shard_map/ppermute | solution.py:293
  118.5 1.1 collective-permute-done.1.refs_1_
  119.6 0.0 copy-start.1
  119.6 0.0 copy-done
  119.6 0.8 copy-done.1
  120.4 6.9 %shard_map.102 = bf16[256,1536]{1,0:T(8,128)(2,1)} custom-call(s32[4]{0:T(128)} %get-tuple-element.28.flags_ref, bf16[128,1536]{1,0:T(8,128)(2,1)} %copy-done, bf16[128,1536]{1,0:T(8,128)(2,1)} %copy-done.1, bf16[6,256,1536]{2,1,0:T(8,128)(2,1)} %all-gather.2.cloned.1.call-done.refs_0_.refs_5_.refs_6_.refs_2_, f32[2,1,1536]{2,1,0:T(1,128)} %reshape_squeeze.8.refs_1_.refs_3_, ...), custom_call_target="tpu_custom_call" | custom-call | flops 1610612736 | bytes 2359296 | tf_op jit(solution)/shard_map/pallas_call | solution.py:177
  127.3 5.3 %shard_map.103 = bf16[2,8,1536]{2,1,0:T(8,128)(2,1)} custom-call(s32[4]{0:T(128)} %get-tuple-element.27.flags_ref, bf16[1,256,1536]{2,1,0:T(8,128)(2,1)} %bitcast.31, f32[2,1,1536]{2,1,0:T(1,128)} %reshape_squeeze.8.refs_1_.refs_3_, f32[2,1,1536]{2,1,0:T(1,128)} %reshape_squeeze.9.refs_2_.refs_4_, ...), custom_call_target="tpu_custom_call", output_to_operand_aliasing={{}: (8, {})} | custom-call | flops 1610612736 | bytes 2359296 | tf_op jit(solution)/shard_map/pallas_call | solution.py:177
Async XLA Ops:
  6.5 79.9 %all-gather.2.cloned.1.call-start = ((), (), s32[]{:S(2)}) async-start(), calls=%async_computation | async-start | bytes 4866048 | tf_op jit(solution)/shard_map/all_gather | solution.py:255
  100.7 14.7 %collective-permute-start = (bf16[128,1536]{1,0:T(8,128)(2,1)}, bf16[128,1536]{1,0:T(8,128)(2,1)S(1)}, u32[]{:S(2)}, u32[]{:S(2)}) collective-permute-start(bf16[128,1536]{1,0:T(8,128)(2,1)} %get-tuple-element.13), channel_id=1, source_target_pairs={{0,32},{32,64},{64,96},{96,128},{128,160},{160,192},{192,224},{224... | collective-permute-start | bytes 1179656 | tf_op jit(solution)/shard_map/ppermute | solution.py:291
  115.4 4.3 %copy-start = (bf16[128,1536]{1,0:T(8,128)(2,1)}, bf16[128,1536]{1,0:T(8,128)(2,1)S(1)}, u32[]{:S(2)}) copy-start(bf16[128,1536]{1,0:T(8,128)(2,1)S(1)} %collective-permute-done.refs_0_) | copy-start | bytes 1179652
  115.4 4.3 %collective-permute-start.1 = (bf16[128,1536]{1,0:T(8,128)(2,1)S(1)}, bf16[128,1536]{1,0:T(8,128)(2,1)S(1)}, u32[]{:S(2)}, u32[]{:S(2)}) collective-permute-start(bf16[128,1536]{1,0:T(8,128)(2,1)S(1)} %collective-permute-done.refs_0_), channel_id=1, source_target_pairs={{0,1},{1,0},{2,3},{3,2},{4,5},{5,4},{6,7},{7,6},{8,9},{9,8},{10,11... | collective-permute-start | bytes 1179656 | tf_op jit(solution)/shard_map/ppermute | solution.py:293
  119.6 0.8 copy-start.1
Sparse Core Ops, SparseCore 0:
  13.0 73.4 all-gather.1

commit v16 on v14

--- a/solution.py
+++ b/solution.py
@@ -274,7 +274,12 @@
     sent, outcomes = results[3:]
     count = lax.axis_size("segment")
     for turn in range(1, patch_count):
-        got = lax.ppermute(sent, "segment", [(i, i + 1) for i in range(count - 1)])
+        pairs = [(i, i + 1) for i in range(count - 1)]
+        quarter = sent.shape[0] // 2
+        got = jnp.concatenate(
+            [lax.ppermute(sent[:quarter], "segment", pairs), lax.ppermute(sent[quarter:], "segment", pairs)],
+            axis=0,
+        )
         ctx_count = lax.axis_size("ctx")
         swapped = lax.ppermute(got, "ctx", [(c, c ^ 1) for c in range(ctx_count)])
         source = [got, swapped]

time: 139 us -> 140 us (level)
  waiting for transfers between devices: 80.4 us -> 77.3 us
  starting transfers between devices: 5.6 us -> 8.45 us
    ppermute x1 -> x2, waiting for transfers between devices: 12.2 us -> 9.14 us  [the longest x1 4.94 us: per_device(): lax.ppermute(sent[:quarter], 'segment', pairs)]
    ppermute x1 -> x2, starting transfers between devices: 2.47 us -> 5.3 us  [the longest x1 2.81 us: per_device(): lax.ppermute(sent[quarter:], 'segment', pairs)]
  transfers between devices with their start and end apart: 3 -> 4, of which waited for: 3 -> 4; matrix products, arithmetic and copies ran while one was open for 4% -> 4% of each run, Pallas kernels for 0% -> 0%
where the time goes in v16:
time: 140 us
  waiting for transfers between devices  77.3 us (55%)
  Pallas kernels  25.7 us (18%)
  between operations  16.7 us (12%)
  local copies, waits for them, and re-layouts  9.32 us (7%)
  starting transfers between devices  8.45 us (6%)
  other arithmetic  2.1 us (2%)
    all_gather x1, waiting for transfers between devices, per_device(): whole = lax.all_gather(packed, 'ctx', axis=1, tiled=True)  67 us
    pallas_call x4, Pallas kernels, fused_layer(): pl.pallas_call(functools.partial(layer_kernel, two_sources=entry is not N...  25.7 us
    another operation x4, local copies, waits for them, and re-layouts, fused_layer(): p.reshape(p.shape[0], 1, width)  5.24 us
    ppermute x1, waiting for transfers between devices, per_device(): lax.ppermute(sent[:quarter], 'segment', pairs)  4.94 us
    ppermute x1, waiting for transfers between devices, per_device(): lax.ppermute(sent[quarter:], 'segment', pairs)  4.2 us
    ppermute x1, starting transfers between devices, per_device(): swapped = lax.ppermute(got, 'ctx', [(c, c ^ 1) for c in range(ctx_count)])  3.15 us
    ppermute x1, starting transfers between devices, per_device(): lax.ppermute(sent[quarter:], 'segment', pairs)  2.81 us
  transfers between devices with their start and end apart: 4, of which 4 were waited for; matrix products, arithmetic and copies ran while one was open for 4% of the time, Pallas kernels for 0%

profile of v16, /device:TPU:33, one launch (start us, length us, event | category | flops | bytes accessed | tf_op | source)
XLA Modules:
  0.0 139.5 jit_solution(11373048037986268948)
XLA Ops:
  6.5 0.0 all-gather.2.cloned.1.call-start
  6.5 1.3 fusion.1
  10.4 0.9 slice_bitcast_fusion
  11.3 0.8 select_select_fusion
  12.1 0.7 maximum_select_fusion
  12.8 0.0 all-gather.2.cloned.1.call-update
  13.5 1.3 reshape_squeeze.8.refs_1_.refs_3_
  14.8 1.3 reshape_squeeze.9.refs_2_.refs_4_
  16.1 1.3 reshape_squeeze.10.refs_3_.refs_5_
  17.4 1.3 reshape_squeeze.11.refs_4_.refs_6_
  18.7 0.6 add_add_fusion
  19.4 67.0 %all-gather.2.cloned.1.call-done.refs_0_.refs_5_.refs_6_.refs_2_ = bf16[6,256,1536]{2,1,0:T(8,128)(2,1)} async-done(((bf16[6,8,1536]{2,1,0:T(8,128)(2,1)}), bf16[6,256,1536]{2,1,0:T(8,128)(2,1)}) %all-gather.2.cloned.1.call-update) | async-done | bytes 4718608 | tf_op jit(solution)/shard_map/all_gather | solution.py:243
  86.4 6.7 %shard_map.100 = (bf16[256,1536]{1,0:T(8,128)(2,1)}, bf16[256,1536]{1,0:T(8,128)(2,1)}, bf16[256,1536]{1,0:T(8,128)(2,1)}) custom-call(s32[4]{0:T(128)} %get-tuple-element.30.flags_ref, bf16[6,256,1536]{2,1,0:T(8,128)(2,1)} %all-gather.2.cloned.1.call-done.refs_0_.refs_5_.refs_6_.refs_2_, f32[2,1,1536]{2,1,0:T(1,128)} %reshape_squeeze.8.refs_1_.refs_3_, ...), custom_call_target="tpu_custom_call" | custom-call | flops 1610612736 | bytes 3932160 | tf_op jit(solution)/shard_map/pallas_call | solution.py:165
  93.1 6.8 %shard_map.101 = (bf16[256,1536]{1,0:T(8,128)(2,1)}, bf16[256,1536]{1,0:T(8,128)(2,1)}, bf16[256,1536]{1,0:T(8,128)(2,1)}, bf16[128,1536]{1,0:T(8,128)(2,1)}, bf16[2,8,1536]{2,1,0:T(8,128)(2,1)}) custom-call(s32[4]{0:T(128)} %get-tuple-element.29.flags_ref, bf16[1,256,1536]{2,1,0:T(8,128)(2,1)} %bitcast.28, f32[2,1,1536]{2,1,0:T(1,128)} %reshape_squeeze.8.refs_1_.refs_3_, ...), custom_call_target="tpu_custom_call" | custom-call | flops 1610612736 | bytes 3932160 | tf_op jit(solution)/shard_map/pallas_call | solution.py:165
  99.9 1.0 fusion
  100.9 2.5 %collective-permute-start = (bf16[64,1536]{1,0:T(8,128)(2,1)S(1)}, bf16[64,1536]{1,0:T(8,128)(2,1)S(1)}, u32[]{:S(2)}, u32[]{:S(2)}) collective-permute-start(bf16[64,1536]{1,0:T(8,128)(2,1)S(1)} %get-tuple-element.20), channel_id=1, source_target_pairs={{0,32},{32,64},{64,96},{96,128},{128,160},{160,192},{192,224},{224... | collective-permute-start | bytes 589832 | tf_op jit(solution)/shard_map/ppermute | solution.py:280
  103.4 2.8 %collective-permute-start.1 = (bf16[64,1536]{1,0:T(8,128)(2,1)S(1)}, bf16[64,1536]{1,0:T(8,128)(2,1)S(1)}, u32[]{:S(2)}, u32[]{:S(2)}) collective-permute-start(bf16[64,1536]{1,0:T(8,128)(2,1)S(1)} %get-tuple-element.19), channel_id=1, source_target_pairs={{0,32},{32,64},{64,96},{96,128},{128,160},{160,192},{192,224},{224... | collective-permute-start | bytes 589832 | tf_op jit(solution)/shard_map/ppermute | solution.py:280
  106.2 4.9 %collective-permute-done = bf16[64,1536]{1,0:T(8,128)(2,1)S(1)} collective-permute-done((bf16[64,1536]{1,0:T(8,128)(2,1)S(1)}, bf16[64,1536]{1,0:T(8,128)(2,1)S(1)}, u32[]{:S(2)}, u32[]{:S(2)}) %collective-permute-start) | collective-permute-done | bytes 196640 | tf_op jit(solution)/shard_map/ppermute | solution.py:280
  111.2 4.2 %collective-permute-done.1 = bf16[64,1536]{1,0:T(8,128)(2,1)S(1)} collective-permute-done((bf16[64,1536]{1,0:T(8,128)(2,1)S(1)}, bf16[64,1536]{1,0:T(8,128)(2,1)S(1)}, u32[]{:S(2)}, u32[]{:S(2)}) %collective-permute-start.1) | collective-permute-done | bytes 196640 | tf_op jit(solution)/shard_map/ppermute | solution.py:280
  115.4 3.1 %collective-permute-start.2 = (bf16[128,1536]{1,0:T(8,128)(2,1)S(1)}, bf16[128,1536]{1,0:T(8,128)(2,1)S(1)}, u32[]{:S(2)}, u32[]{:S(2)}) collective-permute-start(bf16[128,1536]{1,0:T(8,128)(2,1)S(1)} %constant_dynamic-update-slice_fusion.refs_0_), channel_id=1, source_target_pairs={{0,1},{1,0},{2,3},{3,2},{4,5},{5,4},{6,7},{7,6},{8,9},{9,8},{10,11... | collective-permute-start | bytes 1179656 | tf_op jit(solution)/shard_map/ppermute | solution.py:284
  118.6 1.1 collective-permute-done.2.refs_1_
  119.7 0.8 copy-done.1
  120.5 6.9 %shard_map.102 = bf16[256,1536]{1,0:T(8,128)(2,1)} custom-call(s32[4]{0:T(128)} %get-tuple-element.30.flags_ref, bf16[128,1536]{1,0:T(8,128)(2,1)} %copy-done, bf16[128,1536]{1,0:T(8,128)(2,1)} %copy-done.1, bf16[6,256,1536]{2,1,0:T(8,128)(2,1)} %all-gather.2.cloned.1.call-done.refs_0_.refs_5_.refs_6_.refs_2_, f32[2,1,1536]{2,1,0:T(1,128)} %reshape_squeeze.8.refs_1_.refs_3_, ...), custom_call_target="tpu_custom_call" | custom-call | flops 1610612736 | bytes 2359296 | tf_op jit(solution)/shard_map/pallas_call | solution.py:165
  127.4 5.3 %shard_map.103 = bf16[2,8,1536]{2,1,0:T(8,128)(2,1)} custom-call(s32[4]{0:T(128)} %get-tuple-element.29.flags_ref, bf16[1,256,1536]{2,1,0:T(8,128)(2,1)} %bitcast.31, f32[2,1,1536]{2,1,0:T(1,128)} %reshape_squeeze.8.refs_1_.refs_3_, f32[2,1,1536]{2,1,0:T(1,128)} %reshape_squeeze.9.refs_2_.refs_4_, ...), custom_call_target="tpu_custom_call", output_to_operand_aliasing={{}: (8, {})} | custom-call | flops 1610612736 | bytes 2359296 | tf_op jit(solution)/shard_map/pallas_call | solution.py:165
  (5 shorter events, 0.0 us)
Async XLA Ops:
  6.5 79.9 %all-gather.2.cloned.1.call-start = ((), (), s32[]{:S(2)}) async-start(), calls=%async_computation | async-start | bytes 4866048 | tf_op jit(solution)/shard_map/all_gather | solution.py:243
  100.9 10.3 %collective-permute-start = (bf16[64,1536]{1,0:T(8,128)(2,1)S(1)}, bf16[64,1536]{1,0:T(8,128)(2,1)S(1)}, u32[]{:S(2)}, u32[]{:S(2)}) collective-permute-start(bf16[64,1536]{1,0:T(8,128)(2,1)S(1)} %get-tuple-element.20), channel_id=1, source_target_pairs={{0,32},{32,64},{64,96},{96,128},{128,160},{160,192},{192,224},{224... | collective-permute-start | bytes 589832 | tf_op jit(solution)/shard_map/ppermute | solution.py:280
  103.4 12.0 %collective-permute-start.1 = (bf16[64,1536]{1,0:T(8,128)(2,1)S(1)}, bf16[64,1536]{1,0:T(8,128)(2,1)S(1)}, u32[]{:S(2)}, u32[]{:S(2)}) collective-permute-start(bf16[64,1536]{1,0:T(8,128)(2,1)S(1)} %get-tuple-element.19), channel_id=1, source_target_pairs={{0,32},{32,64},{64,96},{96,128},{128,160},{160,192},{192,224},{224... | collective-permute-start | bytes 589832 | tf_op jit(solution)/shard_map/ppermute | solution.py:280
  115.4 4.3 %copy-start = (bf16[128,1536]{1,0:T(8,128)(2,1)}, bf16[128,1536]{1,0:T(8,128)(2,1)S(1)}, u32[]{:S(2)}) copy-start(bf16[128,1536]{1,0:T(8,128)(2,1)S(1)} %constant_dynamic-update-slice_fusion.refs_0_) | copy-start | bytes 1179652
  115.4 4.3 %collective-permute-start.2 = (bf16[128,1536]{1,0:T(8,128)(2,1)S(1)}, bf16[128,1536]{1,0:T(8,128)(2,1)S(1)}, u32[]{:S(2)}, u32[]{:S(2)}) collective-permute-start(bf16[128,1536]{1,0:T(8,128)(2,1)S(1)} %constant_dynamic-update-slice_fusion.refs_0_), channel_id=1, source_target_pairs={{0,1},{1,0},{2,3},{3,2},{4,5},{5,4},{6,7},{7,6},{8,9},{9,8},{10,11... | collective-permute-start | bytes 1179656 | tf_op jit(solution)/shard_map/ppermute | solution.py:284
  119.7 0.8 copy-start.1
Sparse Core Ops, SparseCore 0:
  13.0 73.4 all-gather.1

commit v17 on v14

--- a/solution.py
+++ b/solution.py
@@ -75,14 +75,11 @@
         if keep_kv:
             kv_refs[0][:, cols] = fresh_key
             kv_refs[1][:, cols] = fresh_value
-        near = lax.dot_general(query, fresh_key, dims, preferred_element_type=jnp.float32) * scale
-        far = lax.dot_general(query, kf_ref[:, cols], dims, preferred_element_type=jnp.float32) * scale
-        near = jnp.exp(near)
-        far = jnp.exp(far)
-        total = jnp.sum(near, axis=-1, keepdims=True) + jnp.sum(far, axis=-1, keepdims=True)
-        numerator = jnp.dot(
-            near.astype(jnp.bfloat16), fresh_value, preferred_element_type=jnp.float32
-        ) + jnp.dot(far.astype(jnp.bfloat16), vf_ref[:, cols], preferred_element_type=jnp.float32)
+        keys = jnp.concatenate([fresh_key, kf_ref[:, cols]], axis=0)
+        values = jnp.concatenate([fresh_value, vf_ref[:, cols]], axis=0)
+        weights = jnp.exp(lax.dot_general(query, keys, dims, preferred_element_type=jnp.float32) * scale)
+        total = jnp.sum(weights, axis=-1, keepdims=True)
+        numerator = jnp.dot(weights.astype(jnp.bfloat16), values, preferred_element_type=jnp.float32)
         attended = numerator / total
         new_state = (x + skip_ref[:, cols] * attended).astype(o_ref.dtype)
         o_ref[:, cols] = jnp.where(live, new_state, x_rounded)

time: 139 us -> 139 us (level)
  no operation moved by 1% of the time
where the time goes in v17:
time: 139 us
  waiting for transfers between devices  80.5 us (58%)
  Pallas kernels  25.7 us (18%)
  between operations  16.6 us (12%)
  local copies, waits for them, and re-layouts  8.26 us (6%)
  starting transfers between devices  5.47 us (4%)
  other arithmetic  2.1 us (2%)
    all_gather x1, waiting for transfers between devices, per_device(): whole = lax.all_gather(packed, 'ctx', axis=1, tiled=True)  67 us
    pallas_call x4, Pallas kernels, fused_layer(): pl.pallas_call(functools.partial(layer_kernel, two_sources=entry is not N...  25.7 us
    ppermute x1, waiting for transfers between devices, per_device(): got = lax.ppermute(sent, 'segment', [(i, i + 1) for i in range(count - 1)])  12.2 us
    another operation x4, local copies, waits for them, and re-layouts, fused_layer(): p.reshape(p.shape[0], 1, width)  5.25 us
    ppermute x1, starting transfers between devices, per_device(): swapped = lax.ppermute(got, 'ctx', [(c, c ^ 1) for c in range(ctx_count)])  2.97 us
  transfers between devices with their start and end apart: 3, of which 3 were waited for; matrix products, arithmetic and copies ran while one was open for 4% of the time, Pallas kernels for 0%

profile of v17, /device:TPU:33, one launch (start us, length us, event | category | flops | bytes accessed | tf_op | source)
XLA Modules:
  0.0 138.7 jit_solution(2462896713083440009)
XLA Ops:
  6.5 0.0 all-gather.2.cloned.1.call-start
  6.5 1.3 fusion
  10.4 0.9 slice_bitcast_fusion
  11.3 0.8 select_select_fusion
  12.1 0.7 maximum_select_fusion
  12.8 0.0 all-gather.2.cloned.1.call-update
  13.5 1.3 reshape_squeeze.8.refs_1_.refs_3_
  14.8 1.3 reshape_squeeze.9.refs_2_.refs_4_
  16.1 1.3 reshape_squeeze.10.refs_3_.refs_5_
  17.4 1.3 reshape_squeeze.11.refs_4_.refs_6_
  18.8 0.6 add_add_fusion
  19.4 67.0 %all-gather.2.cloned.1.call-done.refs_0_.refs_5_.refs_6_.refs_2_ = bf16[6,256,1536]{2,1,0:T(8,128)(2,1)} async-done(((bf16[6,8,1536]{2,1,0:T(8,128)(2,1)}), bf16[6,256,1536]{2,1,0:T(8,128)(2,1)}) %all-gather.2.cloned.1.call-update) | async-done | bytes 4718608 | tf_op jit(solution)/shard_map/all_gather | solution.py:240
  86.4 6.7 %shard_map.100 = (bf16[256,1536]{1,0:T(8,128)(2,1)}, bf16[256,1536]{1,0:T(8,128)(2,1)}, bf16[256,1536]{1,0:T(8,128)(2,1)}) custom-call(s32[4]{0:T(128)} %get-tuple-element.28.flags_ref, bf16[6,256,1536]{2,1,0:T(8,128)(2,1)} %all-gather.2.cloned.1.call-done.refs_0_.refs_5_.refs_6_.refs_2_, f32[2,1,1536]{2,1,0:T(1,128)} %reshape_squeeze.8.refs_1_.refs_3_, ...), custom_call_target="tpu_custom_call" | custom-call | flops 1610612736 | bytes 3932160 | tf_op jit(solution)/shard_map/pallas_call | solution.py:162
  93.1 6.8 %shard_map.101 = (bf16[256,1536]{1,0:T(8,128)(2,1)}, bf16[256,1536]{1,0:T(8,128)(2,1)}, bf16[256,1536]{1,0:T(8,128)(2,1)}, bf16[128,1536]{1,0:T(8,128)(2,1)}, bf16[2,8,1536]{2,1,0:T(8,128)(2,1)}) custom-call(s32[4]{0:T(128)} %get-tuple-element.27.flags_ref, bf16[1,256,1536]{2,1,0:T(8,128)(2,1)} %bitcast.28, f32[2,1,1536]{2,1,0:T(1,128)} %reshape_squeeze.8.refs_1_.refs_3_, ...), custom_call_target="tpu_custom_call" | custom-call | flops 1610612736 | bytes 3932160 | tf_op jit(solution)/shard_map/pallas_call | solution.py:162
  99.9 2.5 %collective-permute-start = (bf16[128,1536]{1,0:T(8,128)(2,1)}, bf16[128,1536]{1,0:T(8,128)(2,1)S(1)}, u32[]{:S(2)}, u32[]{:S(2)}) collective-permute-start(bf16[128,1536]{1,0:T(8,128)(2,1)} %get-tuple-element.13), channel_id=1, source_target_pairs={{0,32},{32,64},{64,96},{96,128},{128,160},{160,192},{192,224},{224... | collective-permute-start | bytes 1179656 | tf_op jit(solution)/shard_map/ppermute | solution.py:274
  102.4 12.2 %collective-permute-done.refs_0_ = bf16[128,1536]{1,0:T(8,128)(2,1)S(1)} collective-permute-done((bf16[128,1536]{1,0:T(8,128)(2,1)}, bf16[128,1536]{1,0:T(8,128)(2,1)S(1)}, u32[]{:S(2)}, u32[]{:S(2)}) %collective-permute-start) | collective-permute-done | bytes 393248 | tf_op jit(solution)/shard_map/ppermute | solution.py:274
  114.5 0.0 copy-start
  114.5 3.0 %collective-permute-start.1 = (bf16[128,1536]{1,0:T(8,128)(2,1)S(1)}, bf16[128,1536]{1,0:T(8,128)(2,1)S(1)}, u32[]{:S(2)}, u32[]{:S(2)}) collective-permute-start(bf16[128,1536]{1,0:T(8,128)(2,1)S(1)} %collective-permute-done.refs_0_), channel_id=1, source_target_pairs={{0,1},{1,0},{2,3},{3,2},{4,5},{5,4},{6,7},{7,6},{8,9},{9,8},{10,11... | collective-permute-start | bytes 1179656 | tf_op jit(solution)/shard_map/ppermute | solution.py:276
  117.5 1.3 collective-permute-done.1.refs_1_
  118.8 0.0 copy-start.1
  118.8 0.0 copy-done
  118.8 0.8 copy-done.1
  119.6 7.0 %shard_map.102 = bf16[256,1536]{1,0:T(8,128)(2,1)} custom-call(s32[4]{0:T(128)} %get-tuple-element.28.flags_ref, bf16[128,1536]{1,0:T(8,128)(2,1)} %copy-done, bf16[128,1536]{1,0:T(8,128)(2,1)} %copy-done.1, bf16[6,256,1536]{2,1,0:T(8,128)(2,1)} %all-gather.2.cloned.1.call-done.refs_0_.refs_5_.refs_6_.refs_2_, f32[2,1,1536]{2,1,0:T(1,128)} %reshape_squeeze.8.refs_1_.refs_3_, ...), custom_call_target="tpu_custom_call" | custom-call | flops 1610612736 | bytes 2359296 | tf_op jit(solution)/shard_map/pallas_call | solution.py:162
  126.6 5.3 %shard_map.103 = bf16[2,8,1536]{2,1,0:T(8,128)(2,1)} custom-call(s32[4]{0:T(128)} %get-tuple-element.27.flags_ref, bf16[1,256,1536]{2,1,0:T(8,128)(2,1)} %bitcast.31, f32[2,1,1536]{2,1,0:T(1,128)} %reshape_squeeze.8.refs_1_.refs_3_, f32[2,1,1536]{2,1,0:T(1,128)} %reshape_squeeze.9.refs_2_.refs_4_, ...), custom_call_target="tpu_custom_call", output_to_operand_aliasing={{}: (8, {})} | custom-call | flops 1610612736 | bytes 2359296 | tf_op jit(solution)/shard_map/pallas_call | solution.py:162
Async XLA Ops:
  6.5 79.9 %all-gather.2.cloned.1.call-start = ((), (), s32[]{:S(2)}) async-start(), calls=%async_computation | async-start | bytes 4866048 | tf_op jit(solution)/shard_map/all_gather | solution.py:240
  99.9 14.7 %collective-permute-start = (bf16[128,1536]{1,0:T(8,128)(2,1)}, bf16[128,1536]{1,0:T(8,128)(2,1)S(1)}, u32[]{:S(2)}, u32[]{:S(2)}) collective-permute-start(bf16[128,1536]{1,0:T(8,128)(2,1)} %get-tuple-element.13), channel_id=1, source_target_pairs={{0,32},{32,64},{64,96},{96,128},{128,160},{160,192},{192,224},{224... | collective-permute-start | bytes 1179656 | tf_op jit(solution)/shard_map/ppermute | solution.py:274
  114.5 4.3 %copy-start = (bf16[128,1536]{1,0:T(8,128)(2,1)}, bf16[128,1536]{1,0:T(8,128)(2,1)S(1)}, u32[]{:S(2)}) copy-start(bf16[128,1536]{1,0:T(8,128)(2,1)S(1)} %collective-permute-done.refs_0_) | copy-start | bytes 1179652
  114.5 4.3 %collective-permute-start.1 = (bf16[128,1536]{1,0:T(8,128)(2,1)S(1)}, bf16[128,1536]{1,0:T(8,128)(2,1)S(1)}, u32[]{:S(2)}, u32[]{:S(2)}) collective-permute-start(bf16[128,1536]{1,0:T(8,128)(2,1)S(1)} %collective-permute-done.refs_0_), channel_id=1, source_target_pairs={{0,1},{1,0},{2,3},{3,2},{4,5},{5,4},{6,7},{7,6},{8,9},{9,8},{10,11... | collective-permute-start | bytes 1179656 | tf_op jit(solution)/shard_map/ppermute | solution.py:276
  118.8 0.8 copy-start.1
Sparse Core Ops, SparseCore 0:
  13.0 73.4 all-gather.1
